TPU v7x, 512 devices: a whole 4x8x8 slice. The times are simulated.
512 devices in a mesh: space: 128 (over z, y, core), mode: 4 (over x).
Axes of the slice: x: 4, y: 8, z: 8, core: 2. Of those that a mesh axis runs over, the one named last changes fastest.
Arguments:
- iterate: float32 [84, 16, 98304], P('mode', None, 'space'), may hold values from -6 to 6
- forcing: float32 [84, 16, 98304], P('mode', None, 'space'), may hold values from -6 to 6
- tiles: bfloat16 [3, 512, 3, 36864], P(None, 'space'), may hold values from -0.25 to 0.25
- inverse_blocks: bfloat16 [512, 36864], P('space'), may hold values from -0.4375 to 0.4375
- columns: int32 [512, 3], P('space'), may hold values from 0 to 7, as said below
- coupling: float32 [3, 84, 84], replicated, may hold values from -0.7 to 1.5, as said below
Outputs:
- updated: float32 [84, 16, 98304], P('mode', None, 'space')
- residual: float32 [84, 16, 98304], P('mode', None, 'space')
Inputs may be any that keep to these rules, and one draw needn't show every extreme that they name: For row block j at position q = j mod 4 of its device: columns[j, 0] = 2 + q; columns[j, 1] = 2 + q - 1 or 2 + q - 2; columns[j, 2] = 2 + q + 1 or 2 + q + 2. At q = 0 slot 1 is 2 + q - 2, at q = 3 slot 2 is 2 + q + 2. `coupling`: each matrix is symmetric; the first has ones added on its diagonal.
All inputs are finite; a program needn't handle non-finite values.
Results may differ from a plain program's by a relative error of at most 0.0033.
Values may be sent and summed in bfloat16 or wider, within the bound.
No kernel may reach another device: no remote copies, remote signals or barrier semaphores. Data moves between devices by JAX's collectives and lax.ppermute only.
A program may use at most 64 MiB of HBM per device.

v0:
```python
import jax
import jax.numpy as jnp
from jax import lax
from jax.sharding import PartitionSpec as P

H = 2


RELAXATION = 0.7


def padded(x, sides, width):
    for axis, dim in sides:
        devices, length = (lax.axis_size(axis), x.shape[dim])
        up = [(i, (i + 1) % devices) for i in range(devices)]
        down = [(j, i) for i, j in up]
        last = lax.slice_in_dim(x, length - width, length, axis=dim)
        initial = lax.slice_in_dim(x, 0, width, axis=dim)
        before = lax.ppermute(last, axis, up)
        after = lax.ppermute(initial, axis, down)
        x = jnp.concatenate([before, x, after], axis=dim)
    return x


def stiffness(extended, tile_rows, column_rows):
    block_size = extended.shape[-1]
    picked = jnp.take(extended, column_rows, axis=2)
    shaped = tile_rows.reshape(
        tile_rows.shape[0], tile_rows.shape[1], tile_rows.shape[2], block_size, block_size
    )
    return jnp.einsum("krsim,plrsm->kplri", shaped, picked, preferred_element_type=jnp.float32)


def body(iterate, forcing, tiles, inverse_blocks, columns, coupling):
    modes_here, loads, dofs_here = iterate.shape
    terms, block_count = (tiles.shape[0], tiles.shape[1])
    block_size = dofs_here // block_count
    rounded = iterate.astype(jnp.bfloat16).reshape(modes_here, loads, block_count, block_size)
    extended = padded(rounded, (("space", 2),), H)
    products = stiffness(extended, tiles, columns).astype(jnp.bfloat16)
    mixture = jnp.einsum(
        "kab,kblqn->alqn",
        coupling,
        lax.all_to_all(products, "mode", split_axis=3, concat_axis=1, tiled=True).astype(
            jnp.float32
        ),
        precision=lax.Precision.HIGHEST,
    )
    applied = lax.all_to_all(mixture, "mode", split_axis=0, concat_axis=2, tiled=True)
    applied = applied.reshape(modes_here, loads, dofs_here)
    residual = forcing - applied
    rounded_res = residual.astype(jnp.bfloat16).reshape(modes_here, loads, block_count, block_size)
    inverse = inverse_blocks.reshape(block_count, block_size, block_size)
    update = jnp.einsum("jim,pljm->plji", inverse, rounded_res, preferred_element_type=jnp.float32)
    updated = iterate + RELAXATION * update.reshape(modes_here, loads, dofs_here)
    return (updated, residual)


def solution(mesh):
    return jax.shard_map(
        body,
        mesh=mesh,
        in_specs=(
            P("mode", None, "space"),
            P("mode", None, "space"),
            P(None, "space", None, None),
            P("space", None),
            P("space", None),
            P(),
        ),
        out_specs=(P("mode", None, "space"), P("mode", None, "space")),
        check_vma=False,
    )
```

profile of v0, /device:TPU:56, one launch (start us, length us, event | category | flops | bytes accessed | tf_op | source)
XLA Modules:
  0.0 89.1 jit_solution(2074304558895671441)
XLA Ops:
  0.6 1.3 %convert_element_type.13 = bf16[21,16,768]{2,1,0:T(8,128)(2,1)S(1)} convert(f32[21,16,768]{2,1,0:T(8,128)} %param.6) | non-fusion elementwise | flops 258048 | bytes 1548288 | tf_op jit(solution)/shard_map/convert_element_type | solution.py:38
  2.0 0.6 reshape.33
  2.6 0.1 copy.28
  2.7 1.9 %collective-permute-start = (bf16[21,16,2,192]{3,1,2,0:T(8,128)(2,1)S(1)}, bf16[21,16,2,192]{3,1,2,0:T(8,128)(2,1)S(1)}, u32[]{:S(2)}, u32[]{:S(2)}) collective-permute-start(bf16[21,16,2,192]{3,1,2,0:T(8,128)(2,1)S(1)} %get-tuple-element.4), channel_id=1, source_target_pairs={{0,4},{4,8},{8,12},{12,16},{16,20},{20,24},{24,28},{28,32},{32,36}... | collective-permute-start | bytes 774152 | tf_op jit(solution)/shard_map/ppermute | solution.py:19
  4.7 3.6 %collective-permute-start.1 = (bf16[21,16,2,192]{3,1,2,0:T(8,128)(2,1)S(1)}, bf16[21,16,2,192]{3,1,2,0:T(8,128)(2,1)S(1)}, u32[]{:S(2)}, u32[]{:S(2)}) collective-permute-start(bf16[21,16,2,192]{3,1,2,0:T(8,128)(2,1)S(1)} %get-tuple-element.5), channel_id=1, source_target_pairs={{4,0},{8,4},{12,8},{16,12},{20,16},{24,20},{28,24},{32,28},{36,32}... | collective-permute-start | bytes 774152 | tf_op jit(solution)/shard_map/ppermute | solution.py:20
  8.3 0.1 reshape.41
  8.4 6.5 %reshape.34 = bf16[3,4,3,192,192]{4,3,1,2,0:T(8,128)(2,1)} reshape(bf16[3,4,3,36864]{3,1,2,0:T(4,128)(2,1)} %param.8) | data formatting | bytes 5308416 | tf_op jit(solution)/shard_map/reshape | solution.py:28
  14.9 0.3 pad_maximum_fusion
  15.2 2.1 %gather_fusion = bf16[12,21,16,192]{3,2,1,0:T(8,128)(2,1)} fusion(bf16[21,16,8,192]{3,1,2,0:T(8,128)(2,1)S(1)} %pad_maximum_fusion, s32[1024]{0:T(1024)S(1)} %pad_clamp_fusion), kind=kCustom, calls=%fused_computation | custom fusion | bytes 3096624 | tf_op jit(solution)/shard_map/jit(_take)/gather | solution.py:27
  17.3 4.4 %fusion.4 = bf16[3,21,16,4,192]{4,2,0,1,3:T(8,128)(2,1)S(1)} fusion(bf16[3,4,3,192,192]{4,3,1,2,0:T(8,128)(2,1)} %reshape.34, bf16[4,3,21,16,192]{4,3,2,1,0:T(8,128)(2,1)} %bitcast.47, pred[4,3]{1,0:T(4,128)(4,1)S(1)} %compare_and_fusion), kind=kOutput, calls=%fused_computation.6 | convolution fusion | flops 893362176 | bytes 5750796 | tf_op jit(solution)/shard_map/krsim,plrsm->kplri/dot_general | solution.py:31
  21.7 30.7 %all_to_all.30 = bf16[3,21,16,4,192]{4,2,0,1,3:T(8,128)(2,1)S(1)} all-to-all(bf16[3,21,16,4,192]{4,2,0,1,3:T(8,128)(2,1)S(1)} %fusion.4), channel_id=1, replica_groups=mesh['space'=128,'mode'=4] {'mode'}, dimensions={3} | all-to-all | bytes 3096576 | tf_op jit(solution)/shard_map/all_to_all | solution.py:44
  52.4 2.1 %fusion.10 = f32[84,16,1,192]{3,0,1,2:T(8,128)S(1)} fusion(bf16[3,84,16,192]{3,2,0,1:T(8,128)(2,1)S(1)} %bitcast.45, f32[3,84,84]{2,1,0:T(8,128)S(1)} %copy-done), kind=kOutput, calls=%fused_computation.9 | convolution fusion | flops 780337152 | bytes 2665152 | tf_op jit(solution)/shard_map/kab,kblqn->alqn/dot_general | solution.py:41
  54.5 1.5 %copy.34 = f32[84,16,1,192]{3,1,2,0:T(8,128)} copy(f32[84,16,1,192]{3,0,1,2:T(8,128)S(1)} %fusion.10) | data formatting | bytes 2064384 | tf_op jit(solution)/shard_map/kab,kblqn->alqn/dot_general | solution.py:41
  56.0 3.9 %all-to-all-start.1 = ((f32[84,16,1,192]{3,1,2,0:T(8,128)}), f32[84,16,1,192]{3,1,2,0:T(8,128)S(1)}, u32[]{:S(2)}, u32[]{:S(2)}) async-start(f32[84,16,1,192]{3,1,2,0:T(8,128)} %copy.34), calls=%async_computation.1 | async-start | bytes 2752512 | tf_op jit(solution)/shard_map/all_to_all | solution.py:49
  59.9 0.4 reshape.54
  60.3 19.0 %all-to-all-done.1 = f32[84,16,1,192]{3,1,2,0:T(8,128)S(1)} async-done(((f32[84,16,1,192]{3,1,2,0:T(8,128)}), f32[84,16,1,192]{3,1,2,0:T(8,128)S(1)}, u32[]{:S(2)}, u32[]{:S(2)}) %all-to-all-start.1) | async-done | bytes 1032224 | tf_op jit(solution)/shard_map/all_to_all | solution.py:49
  79.4 1.0 %copy.35 = f32[21,16,4,1,192]{4,2,1,0,3:T(4,128)S(1)} copy(f32[21,16,4,1,192]{4,1,0,2,3:T(8,128)S(1)} %bitcast.46) | data formatting | bytes 2064384 | tf_op jit(solution)/shard_map/all_to_all | solution.py:49
  80.4 0.9 %reshape.36 = f32[21,16,768]{2,1,0:T(8,128)S(1)} reshape(f32[21,16,4,1,192]{4,2,1,0,3:T(4,128)S(1)} %copy.35) | data formatting | bytes 2064384 | tf_op jit(solution)/shard_map/reshape | solution.py:50
  81.3 2.4 %fusion.17 = (bf16[21,16,768]{2,1,0:T(8,128)(2,1)S(1)}, f32[21,16,768]{2,1,0:T(8,128)}) fusion(f32[21,16,768]{2,1,0:T(8,128)} %param.7, f32[21,16,768]{2,1,0:T(8,128)S(1)} %reshape.36), kind=kLoop, calls=%fused_computation.19 | loop fusion | flops 516096 | bytes 3612672 | tf_op jit(solution)/shard_map/convert_element_type | solution.py:52
  83.8 0.6 reshape.37
  84.3 0.4 fusion.13
  84.7 1.0 %copy.37 = f32[21,16,4,192]{3,2,1,0:T(4,128)S(1)} copy(f32[21,16,4,192]{3,1,0,2:T(8,128)S(1)} %fusion.13) | data formatting | bytes 2064384 | tf_op jit(solution)/shard_map/mul | solution.py:55
  85.8 0.9 %mul.15 = f32[21,16,768]{2,1,0:T(8,128)S(1)} reshape(f32[21,16,4,192]{3,2,1,0:T(4,128)S(1)} %copy.37) | data formatting | bytes 2064384 | tf_op jit(solution)/shard_map/mul | solution.py:55
  86.7 2.4 %add.8 = f32[21,16,768]{2,1,0:T(8,128)} add(f32[21,16,768]{2,1,0:T(8,128)} %param.6, f32[21,16,768]{2,1,0:T(8,128)S(1)} %mul.15) | non-fusion elementwise | flops 258048 | bytes 3096576 | tf_op jit(solution)/shard_map/add | solution.py:55
  (12 shorter events, 0.1 us)
Async XLA Ops:
  0.6 51.8 %copy-start = (f32[3,84,84]{2,1,0:T(8,128)S(1)}, f32[3,84,84]{2,1,0:T(8,128)}, u32[]{:S(2)}) copy-start(f32[3,84,84]{2,1,0:T(8,128)} %param.11) | copy-start | bytes 254020
  2.0 6.4 %copy-start.2 = (s32[4,3]{1,0:T(4,128)S(1)}, s32[4,3]{1,0:T(4,128)}, u32[]{:S(2)}) copy-start(s32[4,3]{1,0:T(4,128)} %param.10) | copy-start | bytes 148
  2.7 12.2 %collective-permute-start = (bf16[21,16,2,192]{3,1,2,0:T(8,128)(2,1)S(1)}, bf16[21,16,2,192]{3,1,2,0:T(8,128)(2,1)S(1)}, u32[]{:S(2)}, u32[]{:S(2)}) collective-permute-start(bf16[21,16,2,192]{3,1,2,0:T(8,128)(2,1)S(1)} %get-tuple-element.4), channel_id=1, source_target_pairs={{0,4},{4,8},{8,12},{12,16},{16,20},{20,24},{24,28},{28,32},{32,36}... | collective-permute-start | bytes 774152 | tf_op jit(solution)/shard_map/ppermute | solution.py:19
  4.7 10.2 %collective-permute-start.1 = (bf16[21,16,2,192]{3,1,2,0:T(8,128)(2,1)S(1)}, bf16[21,16,2,192]{3,1,2,0:T(8,128)(2,1)S(1)}, u32[]{:S(2)}, u32[]{:S(2)}) collective-permute-start(bf16[21,16,2,192]{3,1,2,0:T(8,128)(2,1)S(1)} %get-tuple-element.5), channel_id=1, source_target_pairs={{4,0},{8,4},{12,8},{16,12},{20,16},{24,20},{28,24},{32,28},{36,32}... | collective-permute-start | bytes 774152 | tf_op jit(solution)/shard_map/ppermute | solution.py:20
  56.0 3.9 %copy-start.1 = (bf16[4,36864]{1,0:T(4,128)(2,1)S(1)}, bf16[4,36864]{1,0:T(4,128)(2,1)}, u32[]{:S(2)}) copy-start(bf16[4,36864]{1,0:T(4,128)(2,1)} %param.9) | copy-start | bytes 884740
  56.0 23.4 %all-to-all-start.1 = ((f32[84,16,1,192]{3,1,2,0:T(8,128)}), f32[84,16,1,192]{3,1,2,0:T(8,128)S(1)}, u32[]{:S(2)}, u32[]{:S(2)}) async-start(f32[84,16,1,192]{3,1,2,0:T(8,128)} %copy.34), calls=%async_computation.1 | async-start | bytes 2752512 | tf_op jit(solution)/shard_map/all_to_all | solution.py:49
where the time goes:
time: 89.8 us; the launch traced here: 89.1 us
  blocking collectives  30.7 us (34%)
  waiting for transfers between devices  19.1 us (21%)
  local copies, waits for them, and re-layouts  15.9 us (18%)
  starting transfers between devices  9.42 us (10%)
  matrix products  6.89 us (8%)
  other arithmetic  6.38 us (7%)
    all_to_all x1, blocking collectives, body(): lax.all_to_all(products, 'mode', split_axis=3, concat_axis=1, tiled=True)  30.7 us
    all_to_all x1, waiting for transfers between devices, body(): lax.all_to_all(mixture, 'mode', split_axis=0, concat_axis=2, tiled=True)  19 us
    reshape x1, local copies, waits for them, and re-layouts, stiffness(): tile_rows.reshape(tile_rows.shape[0], tile_rows.shape[1], tile_rows.shape...  6.46 us
    dot_general x1, matrix products, stiffness(): jnp.einsum('krsim,plrsm->kplri', shaped, picked, preferred_element_type=j...  4.43 us
    all_to_all x1, starting transfers between devices, body(): lax.all_to_all(mixture, 'mode', split_axis=0, concat_axis=2, tiled=True)  3.86 us
    ppermute x1, starting transfers between devices, padded(): after = lax.ppermute(initial, axis, down)  3.64 us
    convert_element_type x1, other arithmetic, body(): residual.astype(jnp.bfloat16)  2.42 us
    add x1, other arithmetic, body(): iterate + RELAXATION * update.reshape(modes_here, loads, dofs_here)  2.37 us
  transfers between devices with their start and end apart: 3, of which 1 were waited for; matrix products, arithmetic and copies ran while one was open for 8% of the time, Pallas kernels for 0%

commit v1 on v0

v1 whole, which is shorter than its diff:
```python
import functools

import jax
import jax.numpy as jnp
from jax import lax
from jax.experimental import pallas as pl
from jax.experimental.pallas import tpu as pltpu
from jax.sharding import PartitionSpec as P

H = 2


RELAXATION = 0.7


def halos(x, axis, width):
    devices = lax.axis_size(axis)
    blocks = x.shape[1]
    up = [(i, (i + 1) % devices) for i in range(devices)]
    down = [(j, i) for i, j in up]
    left = lax.ppermute(x[:, blocks - width:], axis, up)
    right = lax.ppermute(x[:, :width], axis, down)
    return left, right


def stiffness_kernel(cols_ref, xl_ref, xc_ref, xr_ref, t_ref, o_ref, acc_ref):
    r = pl.program_id(0)
    slots = t_ref.shape[2]
    width = xl_ref.shape[1]
    blocks = xc_ref.shape[1]
    block_size = t_ref.shape[-1]
    acc_ref[...] = jnp.zeros_like(acc_ref)

    def add_block(src_ref, idx, tile):
        xs = src_ref[:, idx]
        xs = xs.reshape(-1, block_size)
        acc_ref[...] += lax.dot_general(
            xs, tile, (((1,), (1,)), ((), ())), preferred_element_type=jnp.float32
        )

    for s in range(slots):
        e = cols_ref[r * slots + s]
        tile = t_ref[0, 0, s]

        @pl.when(e < width)
        def _():
            add_block(xl_ref, jnp.clip(e, 0, width - 1), tile)

        @pl.when((e >= width) & (e < width + blocks))
        def _():
            add_block(xc_ref, jnp.clip(e - width, 0, blocks - 1), tile)

        @pl.when(e >= width + blocks)
        def _():
            add_block(xr_ref, jnp.clip(e - width - blocks, 0, width - 1), tile)

    o_ref[0, 0] = acc_ref[...].reshape(o_ref.shape[2:]).astype(o_ref.dtype)


def stiffness(cols, xl, xc, xr, tiles5):
    terms, blocks, slots, bs, _ = tiles5.shape
    nm, _, rows, _ = xc.shape
    width = xl.shape[1]
    full = lambda r, k, c: (0, 0, 0, 0)
    return pl.pallas_call(
        stiffness_kernel,
        out_shape=jax.ShapeDtypeStruct((terms, blocks, nm, rows, bs), jnp.bfloat16),
        grid_spec=pltpu.PrefetchScalarGridSpec(
            num_scalar_prefetch=1,
            grid=(blocks, terms),
            in_specs=[
                pl.BlockSpec((nm, width, rows, bs), full),
                pl.BlockSpec((nm, blocks, rows, bs), full),
                pl.BlockSpec((nm, width, rows, bs), full),
                pl.BlockSpec((1, 1, slots, bs, bs), lambda r, k, c: (k, r, 0, 0, 0)),
            ],
            out_specs=pl.BlockSpec((1, 1, nm, rows, bs), lambda r, k, c: (k, r, 0, 0, 0)),
            scratch_shapes=[pltpu.VMEM((nm * rows, bs), jnp.float32)],
        ),
        compiler_params=pltpu.CompilerParams(vmem_limit_bytes=60 * 1024 * 1024),
        cost_estimate=pl.CostEstimate(
            flops=2 * terms * blocks * slots * nm * rows * bs * bs,
            transcendentals=0,
            bytes_accessed=2 * (tiles5.size + xc.size + xl.size + xr.size + terms * blocks * nm * rows * bs),
        ),
    )(cols, xl, xc, xr, tiles5)


def body(iterate, forcing, tiles, inverse_blocks, columns, coupling):
    modes_here, loads, dofs_here = iterate.shape
    terms, block_count, slots = tiles.shape[:3]
    block_size = dofs_here // block_count
    nm = lax.axis_size("mode")
    rounded = iterate.astype(jnp.bfloat16).reshape(modes_here, loads, block_count, block_size)
    rounded = jnp.transpose(rounded, (2, 0, 1, 3)).reshape(block_count, modes_here * loads, block_size)
    gathered = lax.all_gather(rounded, "mode", axis=0, tiled=False)
    left, right = halos(gathered, "space", H)
    tiles5 = tiles.reshape(terms, block_count, slots, block_size, block_size)
    cols = columns.reshape(-1).astype(jnp.int32)
    products = stiffness(cols, left, gathered, right, tiles5)
    products = products.reshape(terms, block_count, nm, modes_here, loads, block_size)
    first = lax.axis_index("mode") * modes_here
    mine = lax.dynamic_slice_in_dim(coupling, first, modes_here, axis=1)
    mine = mine.reshape(terms, modes_here, nm, modes_here)
    mixture = jnp.einsum(
        "kamp,krmpli->alri",
        mine,
        products.astype(jnp.float32),
        precision=lax.Precision.HIGHEST,
    )
    applied = mixture.reshape(modes_here, loads, dofs_here)
    residual = forcing - applied
    rounded_res = residual.astype(jnp.bfloat16).reshape(modes_here, loads, block_count, block_size)
    inverse = inverse_blocks.reshape(block_count, block_size, block_size)
    update = jnp.einsum("jim,pljm->plji", inverse, rounded_res, preferred_element_type=jnp.float32)
    updated = iterate + RELAXATION * update.reshape(modes_here, loads, dofs_here)
    return (updated, residual)


def solution(mesh):
    return jax.shard_map(
        body,
        mesh=mesh,
        in_specs=(
            P("mode", None, "space"),
            P("mode", None, "space"),
            P(None, "space", None, None),
            P("space", None),
            P("space", None),
            P(),
        ),
        out_specs=(P("mode", None, "space"), P("mode", None, "space")),
        check_vma=False,
    )
```

time: 89.8 us -> 130 us (1.45)
  the two profiles are of different devices: /device:TPU:56 before, /device:TPU:2 now
where the time goes in v1:
time: 130 us; the launch traced here: 129 us
  waiting for transfers between devices  42.5 us (33%)
  local copies, waits for them, and re-layouts  27.9 us (21%)
  Pallas kernels  19.8 us (15%)
  between operations  14.2 us (11%)
  starting transfers between devices  9.52 us (7%)
  matrix products  9.33 us (7%)
  other arithmetic  6.09 us (5%)
    all_gather x1, waiting for transfers between devices, body(): gathered = lax.all_gather(rounded, 'mode', axis=0, tiled=False)  42.4 us
    pallas_call x1, Pallas kernels, stiffness(): pl.pallas_call(stiffness_kernel, out_shape=jax.ShapeDtypeStruct((terms, b...  19.8 us
    reshape x2, local copies, waits for them, and re-layouts, body(): tiles5 = tiles.reshape(terms, block_count, slots, block_size, block_size)  9.59 us
    dot_general x1, matrix products, body(): jnp.einsum('kamp,krmpli->alri', mine, products.astype(jnp.float32), preci...  8.96 us
    ppermute x1, starting transfers between devices, halos(): right = lax.ppermute(x[:, :width], axis, down)  7.57 us
    slice x1, local copies, waits for them, and re-layouts, halos(): right = lax.ppermute(x[:, :width], axis, down)  3.31 us
    all_gather x1, local copies, waits for them, and re-layouts, body(): gathered = lax.all_gather(rounded, 'mode', axis=0, tiled=False)  2.77 us
  transfers between devices with their start and end apart: 3, of which 1 were waited for; matrix products, arithmetic and copies ran while one was open for 12% of the time, Pallas kernels for 0%

profile of v1, /device:TPU:2, one launch (start us, length us, event | category | flops | bytes accessed | tf_op | source)
XLA Modules:
  0.0 129.3 jit_solution(5422949689632700286)
XLA Ops:
  7.2 1.3 %convert_element_type.7 = bf16[21,16,768]{2,1,0:T(8,128)(2,1)S(1)} convert(f32[21,16,768]{2,1,0:T(8,128)} %param.6) | non-fusion elementwise | flops 258048 | bytes 1548288 | tf_op jit(solution)/shard_map/convert_element_type | solution.py:94
  8.5 0.6 reshape.32
  9.2 1.1 copy.30
  10.4 42.4 %all-gather.2.cloned.1.call-done = bf16[4,4,336,192]{2,3,1,0:T(8,128)(2,1)} async-done(((bf16[1,4,336,192]{2,3,1,0:T(8,128)(2,1)}), bf16[4,4,336,192]{2,3,1,0:T(8,128)(2,1)}) %all-gather.2.cloned.1.call-update) | async-done | bytes 2064400 | tf_op jit(solution)/shard_map/all_gather | solution.py:96
  52.8 3.3 %fusion.10 = (bf16[4,2,336,192]{2,3,1,0:T(8,128)(2,1)}, bf16[4,2,336,192]{2,3,1,0:T(8,128)(2,1)}) fusion(bf16[4,4,336,192]{2,3,1,0:T(8,128)(2,1)} %all-gather.2.cloned.1.call-done), kind=kLoop, calls=%fused_computation.10 | loop fusion | bytes 4128768 | tf_op jit(solution)/shard_map/slice | solution.py:22
  56.1 1.9 %collective-permute-start = (bf16[4,2,336,192]{2,3,1,0:T(8,128)(2,1)}, bf16[4,2,336,192]{2,3,1,0:T(8,128)(2,1)}, u32[]{:S(2)}, u32[]{:S(2)}) collective-permute-start(bf16[4,2,336,192]{2,3,1,0:T(8,128)(2,1)} %get-tuple-element.5), channel_id=1, source_target_pairs={{0,4},{4,8},{8,12},{12,16},{16,20},{20,24},{24,28},{28,32},{32,36}... | collective-permute-start | bytes 3096584 | tf_op jit(solution)/shard_map/ppermute | solution.py:21
  58.0 7.6 %collective-permute-start.1 = (bf16[4,2,336,192]{2,3,1,0:T(8,128)(2,1)}, bf16[4,2,336,192]{2,3,1,0:T(8,128)(2,1)}, u32[]{:S(2)}, u32[]{:S(2)}) collective-permute-start(bf16[4,2,336,192]{2,3,1,0:T(8,128)(2,1)} %get-tuple-element.4), channel_id=1, source_target_pairs={{4,0},{8,4},{12,8},{16,12},{20,16},{24,20},{28,24},{32,28},{36,32}... | collective-permute-start | bytes 3096584 | tf_op jit(solution)/shard_map/ppermute | solution.py:22
  65.6 0.6 reshape.31.cols_ref
  66.2 5.3 %reshape.33 = bf16[3,4,3,192,192]{4,3,1,2,0:T(8,128)(2,1)} reshape(bf16[3,4,3,36864]{3,1,2,0:T(4,128)(2,1)S(1)} %copy-done.2) | data formatting | bytes 5308416 | tf_op jit(solution)/shard_map/reshape | solution.py:98
  71.5 4.3 %copy.34.t_ref = bf16[3,4,3,192,192]{4,3,2,1,0:T(8,128)(2,1)} copy(bf16[3,4,3,192,192]{4,3,1,2,0:T(8,128)(2,1)} %reshape.33) | data formatting | bytes 5308416 | tf_op jit(solution)/shard_map/reshape | solution.py:98
  76.0 0.4 reshape.41
  76.4 2.8 %copy.32.xc_ref = bf16[4,4,336,192]{3,2,1,0:T(8,128)(2,1)} copy(bf16[4,4,336,192]{2,3,1,0:T(8,128)(2,1)S(1)} %copy-done.1) | data formatting | bytes 4128768 | tf_op jit(solution)/shard_map/all_gather | solution.py:96
  79.2 2.5 %copy.31.xl_ref = bf16[4,2,336,192]{3,2,1,0:T(8,128)(2,1)} copy(bf16[4,2,336,192]{2,3,1,0:T(8,128)(2,1)} %collective-permute-done) | data formatting | bytes 2064384 | tf_op jit(solution)/shard_map/ppermute | solution.py:21
  81.7 2.5 %copy.33.xr_ref = bf16[4,2,336,192]{3,2,1,0:T(8,128)(2,1)} copy(bf16[4,2,336,192]{2,3,1,0:T(8,128)(2,1)} %collective-permute-done.1) | data formatting | bytes 2064384 | tf_op jit(solution)/shard_map/ppermute | solution.py:22
  84.2 19.8 %shard_map.77 = bf16[3,4,4,336,192]{4,3,2,1,0:T(8,128)(2,1)} custom-call(s32[12]{0:T(128)} %reshape.31.cols_ref, bf16[4,2,336,192]{3,2,1,0:T(8,128)(2,1)} %copy.31.xl_ref, bf16[4,4,336,192]{3,2,1,0:T(8,128)(2,1)} %copy.32.xc_ref, bf16[4,2,336,192]{3,2,1,0:T(8,128)(2,1)} %copy.33.xr_ref, bf16[3,4,3,192,192]{4,3,2,1,0:T(8,128)(2,1)} %copy.34.t_ref), custom_call_target="tpu_custom_call" | custom-call | flops 3567255552 | bytes 12976128 | tf_op jit(solution)/shard_map/pallas_call | solution.py:65
  103.9 9.0 %fusion.2 = f32[21,16,4,192]{3,0,1,2:T(8,128)S(1)} fusion(bf16[3,4,4,21,16,192]{5,4,3,2,1,0:T(8,128)(2,1)} %bitcast.18, f32[3,21,4,21,1,1]{3,2,1,0,5,4:T(4,128)S(1)} %bitcast.20), kind=kOutput, calls=%fused_computation.2 | convolution fusion | flops 780337152 | bytes 7246512 | tf_op jit(solution)/shard_map/kamp,krmpli->alri/dot_general | solution.py:105
  112.9 0.9 copy.37
  113.8 0.9 reshape.36
  114.7 2.4 %fusion.9 = (bf16[21,16,768]{2,1,0:T(8,128)(2,1)S(1)}, f32[21,16,768]{2,1,0:T(8,128)}) fusion(f32[21,16,768]{2,1,0:T(8,128)} %param.7, f32[21,16,768]{2,1,0:T(8,128)S(1)} %reshape.36), kind=kLoop, calls=%fused_computation.9 | loop fusion | flops 516096 | bytes 3612672 | tf_op jit(solution)/shard_map/convert_element_type | solution.py:113
  117.1 0.6 reshape.37
  117.7 0.4 fusion.5
  118.1 1.0 copy.39
  119.2 0.9 mul.19
  120.1 2.4 %add.7 = f32[21,16,768]{2,1,0:T(8,128)} add(f32[21,16,768]{2,1,0:T(8,128)} %param.6, f32[21,16,768]{2,1,0:T(8,128)S(1)} %mul.19) | non-fusion elementwise | flops 258048 | bytes 3096576 | tf_op jit(solution)/shard_map/add | solution.py:116
  (17 shorter events, 0.3 us)
Async XLA Ops:
  7.2 68.7 %copy-start = (f32[3,84,84]{2,1,0:T(8,128)S(1)}, f32[3,84,84]{2,1,0:T(8,128)}, u32[]{:S(2)}) copy-start(f32[3,84,84]{2,1,0:T(8,128)} %param.11) | copy-start | bytes 254020
  7.2 45.6 %all-gather.2.cloned.1.call-start = ((), (), s32[]{:S(2)}) async-start(), calls=%async_computation | async-start | bytes 2949120 | tf_op jit(solution)/shard_map/all_gather | solution.py:96
  10.3 55.3 %copy-start.4 = (s32[4,3]{1,0:T(4,128)S(1)}, s32[4,3]{1,0:T(4,128)}, u32[]{:S(2)}) copy-start(s32[4,3]{1,0:T(4,128)} %param.10) | copy-start | bytes 148
  10.4 55.9 %copy-start.2 = (bf16[3,4,3,36864]{3,1,2,0:T(4,128)(2,1)S(1)}, bf16[3,4,3,36864]{3,1,2,0:T(4,128)(2,1)}, u32[]{:S(2)}) copy-start(bf16[3,4,3,36864]{3,1,2,0:T(4,128)(2,1)} %param.8) | copy-start | bytes 7962628
  56.1 23.1 %collective-permute-start = (bf16[4,2,336,192]{2,3,1,0:T(8,128)(2,1)}, bf16[4,2,336,192]{2,3,1,0:T(8,128)(2,1)}, u32[]{:S(2)}, u32[]{:S(2)}) collective-permute-start(bf16[4,2,336,192]{2,3,1,0:T(8,128)(2,1)} %get-tuple-element.5), channel_id=1, source_target_pairs={{0,4},{4,8},{8,12},{12,16},{16,20},{20,24},{24,28},{28,32},{32,36}... | collective-permute-start | bytes 3096584 | tf_op jit(solution)/shard_map/ppermute | solution.py:21
  58.0 23.6 %collective-permute-start.1 = (bf16[4,2,336,192]{2,3,1,0:T(8,128)(2,1)}, bf16[4,2,336,192]{2,3,1,0:T(8,128)(2,1)}, u32[]{:S(2)}, u32[]{:S(2)}) collective-permute-start(bf16[4,2,336,192]{2,3,1,0:T(8,128)(2,1)} %get-tuple-element.4), channel_id=1, source_target_pairs={{4,0},{8,4},{12,8},{16,12},{20,16},{24,20},{28,24},{32,28},{36,32}... | collective-permute-start | bytes 3096584 | tf_op jit(solution)/shard_map/ppermute | solution.py:22
  71.5 4.5 %copy-start.3 = (bf16[4,36864]{1,0:T(4,128)(2,1)S(1)}, bf16[4,36864]{1,0:T(4,128)(2,1)}, u32[]{:S(2)}) copy-start(bf16[4,36864]{1,0:T(4,128)(2,1)} %param.9) | copy-start | bytes 884740
  71.5 4.9 %copy-start.1 = (bf16[4,4,336,192]{2,3,1,0:T(8,128)(2,1)S(1)}, bf16[4,4,336,192]{2,3,1,0:T(8,128)(2,1)}, u32[]{:S(2)}) copy-start(bf16[4,4,336,192]{2,3,1,0:T(8,128)(2,1)} %all-gather.2.cloned.1.call-done) | copy-start | bytes 6193156
Sparse Core Ops, SparseCore 0:
  10.7 42.0 all-gather.1

commit v2 on v0

v2 whole, which is shorter than its diff:
```python
import jax
import jax.numpy as jnp
from jax import lax
from jax.experimental import pallas as pl
from jax.experimental.pallas import tpu as pltpu
from jax.sharding import PartitionSpec as P

H = 2


RELAXATION = 0.7


def shift(x, axis, k):
    devices = lax.axis_size(axis)
    return lax.ppermute(x, axis, [(i, (i + k) % devices) for i in range(devices)])


def extend(group, left, right):
    return jnp.concatenate([left, group, right], axis=-3)


def stiffness_kernel(cols_ref, x0_ref, x1_ref, x2_ref, t_ref, o_ref):
    nm = x0_ref.shape[0]
    modes_here = o_ref.shape[0] // nm
    loads, block_size = o_ref.shape[1:]
    for m in range(nm):
        acc = None
        for s, x_ref in enumerate((x0_ref, x1_ref, x2_ref)):
            d = lax.dot_general(
                x_ref[m], t_ref[s], (((1,), (1,)), ((), ())), preferred_element_type=jnp.float32
            )
            acc = d if acc is None else acc + d
        o_ref[m * modes_here:(m + 1) * modes_here] = (
            acc.astype(o_ref.dtype).reshape(modes_here, loads, block_size)
        )


def stiffness(cols, ext, tiles5, loads):
    terms, blocks, slots, bs, _ = tiles5.shape
    nm, _, rows, _ = ext.shape
    modes_all = nm * rows // loads

    def x_spec(s):
        return pl.BlockSpec((nm, None, rows, bs), lambda r, k, c: (0, c[r * slots + s], 0, 0))

    return pl.pallas_call(
        stiffness_kernel,
        out_shape=jax.ShapeDtypeStruct((terms, modes_all, blocks, loads, bs), jnp.bfloat16),
        grid_spec=pltpu.PrefetchScalarGridSpec(
            num_scalar_prefetch=1,
            grid=(blocks, terms),
            in_specs=[x_spec(s) for s in range(slots)]
            + [pl.BlockSpec((None, None, slots, bs, bs), lambda r, k, c: (k, r, 0, 0, 0))],
            out_specs=pl.BlockSpec(
                (None, modes_all, None, loads, bs), lambda r, k, c: (k, 0, r, 0, 0)
            ),
        ),
        compiler_params=pltpu.CompilerParams(vmem_limit_bytes=48 * 1024 * 1024),
        cost_estimate=pl.CostEstimate(
            flops=2 * terms * blocks * slots * nm * rows * bs * bs,
            transcendentals=0,
            bytes_accessed=2 * (tiles5.size + blocks * slots * nm * rows * bs + terms * blocks * nm * rows * bs),
        ),
    )(cols, ext, ext, ext, tiles5)


def body(iterate, forcing, tiles, inverse_blocks, columns, coupling):
    modes_here, loads, dofs_here = iterate.shape
    terms, block_count, slots = tiles.shape[:3]
    block_size = dofs_here // block_count
    nm = lax.axis_size("mode")
    me = lax.axis_index("mode")
    tiles5 = tiles.reshape(terms, block_count, slots, block_size, block_size)
    cols = columns.reshape(-1).astype(jnp.int32)
    rounded = iterate.astype(jnp.bfloat16).reshape(modes_here, loads, block_count, block_size)
    own = jnp.transpose(rounded, (2, 0, 1, 3)).reshape(block_count, modes_here * loads, block_size)
    low, high = own[:H], own[block_count - H:]
    from_left = shift(own, "mode", 1)
    from_right = shift(own, "mode", -1)
    near = jnp.stack([from_left, from_right])
    far_low = shift(from_left[:H], "mode", 1)
    far_high = shift(from_right[block_count - H:], "mode", -1)
    far = jnp.concatenate([far_low, far_high], axis=0)
    own_ext = extend(own, shift(high, "space", 1), shift(low, "space", -1))[None]
    near_ext = extend(
        near, shift(near[:, block_count - H:], "space", 1), shift(near[:, :H], "space", -1)
    )
    far_ext = extend(far, shift(far_high, "space", 1), shift(far_low, "space", -1))[None]
    rows_of = lax.dynamic_slice_in_dim(coupling, me * modes_here, modes_here, axis=1)

    def columns_of(index):
        return lax.dynamic_slice_in_dim(rows_of, (index % nm) * modes_here, modes_here, axis=2)

    parts = (
        (own_ext, columns_of(me)),
        (near_ext, jnp.concatenate([columns_of(me + nm - 1), columns_of(me + 1)], axis=2)),
        (far_ext, columns_of(me + 2)),
    )
    mixture = None
    for ext, mix in parts:
        products = stiffness(cols, ext, tiles5, loads)
        term = jnp.einsum(
            "kab,kbrli->alri", mix, products.astype(jnp.float32), precision=lax.Precision.HIGHEST
        )
        mixture = term if mixture is None else mixture + term
    applied = mixture.reshape(modes_here, loads, dofs_here)
    residual = forcing - applied
    rounded_res = residual.astype(jnp.bfloat16).reshape(modes_here, loads, block_count, block_size)
    inverse = inverse_blocks.reshape(block_count, block_size, block_size)
    update = jnp.einsum("jim,pljm->plji", inverse, rounded_res, preferred_element_type=jnp.float32)
    updated = iterate + RELAXATION * update.reshape(modes_here, loads, dofs_here)
    return (updated, residual)


def solution(mesh):
    return jax.shard_map(
        body,
        mesh=mesh,
        in_specs=(
            P("mode", None, "space"),
            P("mode", None, "space"),
            P(None, "space", None, None),
            P("space", None),
            P("space", None),
            P(),
        ),
        out_specs=(P("mode", None, "space"), P("mode", None, "space")),
        check_vma=False,
    )
```

time: 89.8 us -> 117 us (1.30)
  the two profiles are of different devices: /device:TPU:56 before, /device:TPU:2 now
where the time goes in v2:
time: 117 us; the launch traced here: 115 us
  starting transfers between devices  43.4 us (37%)
  Pallas kernels  29.5 us (25%)
  local copies, waits for them, and re-layouts  24.6 us (21%)
  matrix products  9.42 us (8%)
  other arithmetic  7.26 us (6%)
    ppermute x10, starting transfers between devices, shift(): lax.ppermute(x, axis, [(i, (i + k) % devices) for i in range(devices)])  43.4 us
    pallas_call x3, Pallas kernels, stiffness(): pl.pallas_call(stiffness_kernel, out_shape=jax.ShapeDtypeStruct((terms, m...  29.5 us
    dot_general x3, matrix products, body(): jnp.einsum('kab,kbrli->alri', mix, products.astype(jnp.float32), precisio...  9.05 us
    reshape x2, local copies, waits for them, and re-layouts, body(): tiles5 = tiles.reshape(terms, block_count, slots, block_size, block_size)  7.22 us
    ppermute x4, local copies, waits for them, and re-layouts, shift(): lax.ppermute(x, axis, [(i, (i + k) % devices) for i in range(devices)])  4.29 us
  transfers between devices with their start and end apart: 10, of which 1 were waited for; matrix products, arithmetic and copies ran while one was open for 20% of the time, Pallas kernels for 18%

profile of v2, /device:TPU:2, one launch (start us, length us, event | category | flops | bytes accessed | tf_op | source)
XLA Modules:
  0.0 115.4 jit_solution(8462103580633030506)
XLA Ops:
  3.7 3.4 %collective-permute-start.2 = (bf16[4,336,192]{1,2,0:T(8,128)(2,1)}, bf16[4,336,192]{1,2,0:T(8,128)(2,1)}, u32[]{:S(2)}, u32[]{:S(2)}) collective-permute-start(bf16[4,336,192]{1,2,0:T(8,128)(2,1)} %copy.27), channel_id=1, source_target_pairs={{0,1},{1,2},{2,3},{3,0},{4,5},{5,6},{6,7},{7,4},{8,9},{9,10},{10,1... | collective-permute-start | bytes 1548296 | tf_op jit(solution)/shard_map/ppermute | solution.py:16
  7.1 6.3 %collective-permute-start.3 = (bf16[4,336,192]{1,2,0:T(8,128)(2,1)}, bf16[4,336,192]{1,2,0:T(8,128)(2,1)}, u32[]{:S(2)}, u32[]{:S(2)}) collective-permute-start(bf16[4,336,192]{1,2,0:T(8,128)(2,1)} %copy.27), channel_id=1, source_target_pairs={{0,3},{1,0},{2,1},{3,2},{4,7},{5,4},{6,5},{7,6},{8,11},{9,8},{10,9... | collective-permute-start | bytes 1548296 | tf_op jit(solution)/shard_map/ppermute | solution.py:16
  14.4 8.8 %collective-permute-start.1 = (bf16[2,336,192]{2,1,0:T(8,128)(2,1)}, bf16[2,336,192]{2,1,0:T(8,128)(2,1)}, u32[]{:S(2)}, u32[]{:S(2)}) collective-permute-start(bf16[2,336,192]{2,1,0:T(8,128)(2,1)} %bitcast.3), channel_id=1, source_target_pairs={{0,508},{4,0},{8,4},{12,8},{16,12},{20,16},{24,20},{28,24},{32,28}... | collective-permute-start | bytes 774152 | tf_op jit(solution)/shard_map/ppermute | solution.py:16
  23.3 1.9 %collective-permute-start = (bf16[2,336,192]{2,1,0:T(8,128)(2,1)}, bf16[2,336,192]{2,1,0:T(8,128)(2,1)}, u32[]{:S(2)}, u32[]{:S(2)}) collective-permute-start(bf16[2,336,192]{2,1,0:T(8,128)(2,1)} %bitcast.1), channel_id=1, source_target_pairs={{0,4},{4,8},{8,12},{12,16},{16,20},{20,24},{24,28},{28,32},{32,36}... | collective-permute-start | bytes 774152 | tf_op jit(solution)/shard_map/ppermute | solution.py:16
  25.4 5.2 %reshape.33 = bf16[3,4,3,192,192]{4,3,1,2,0:T(8,128)(2,1)S(1)} reshape(bf16[3,4,3,36864]{3,1,2,0:T(4,128)(2,1)} %param.8) | data formatting | bytes 5308416 | tf_op jit(solution)/shard_map/reshape | solution.py:74
  30.6 2.0 %copy.25.t_ref = bf16[3,4,3,192,192]{4,3,2,1,0:T(8,128)(2,1)} copy(bf16[3,4,3,192,192]{4,3,1,2,0:T(8,128)(2,1)S(1)} %reshape.33) | data formatting | bytes 5308416 | tf_op jit(solution)/shard_map/reshape | solution.py:74
  32.6 2.1 %reshape.43 = bf16[4,192,192,1]{2,1,0,3:T(8,128)(2,1)} reshape(bf16[4,36864]{1,0:T(4,128)(2,1)} %param.9) | data formatting | bytes 589824 | tf_op jit(solution)/shard_map/reshape | solution.py:110
  35.7 1.3 %copy.28 = bf16[4,336,192]{2,1,0:T(8,128)(2,1)S(1)} copy(bf16[4,336,192]{1,2,0:T(8,128)(2,1)} %collective-permute-done.2) | data formatting | bytes 1032192 | tf_op jit(solution)/shard_map/ppermute | solution.py:16
  37.0 1.3 %copy.30 = bf16[4,336,192]{2,1,0:T(8,128)(2,1)S(1)} copy(bf16[4,336,192]{1,2,0:T(8,128)(2,1)} %collective-permute-done.3) | data formatting | bytes 1032192 | tf_op jit(solution)/shard_map/ppermute | solution.py:16
  39.7 6.9 %collective-permute-start.5 = (bf16[2,2,336,192]{2,3,1,0:T(8,128)(2,1)}, bf16[2,2,336,192]{2,3,1,0:T(8,128)(2,1)S(1)}, u32[]{:S(2)}, u32[]{:S(2)}) collective-permute-start(bf16[2,2,336,192]{2,3,1,0:T(8,128)(2,1)} %copy.32), channel_id=1, source_target_pairs={{0,508},{4,0},{8,4},{12,8},{16,12},{20,16},{24,20},{28,24},{32,28}... | collective-permute-start | bytes 1548296 | tf_op jit(solution)/shard_map/ppermute | solution.py:16
  47.8 1.9 %collective-permute-start.4 = (bf16[2,2,336,192]{2,3,1,0:T(8,128)(2,1)}, bf16[2,2,336,192]{2,3,1,0:T(8,128)(2,1)}, u32[]{:S(2)}, u32[]{:S(2)}) collective-permute-start(bf16[2,2,336,192]{2,3,1,0:T(8,128)(2,1)} %copy.31), channel_id=1, source_target_pairs={{0,4},{4,8},{8,12},{12,16},{16,20},{20,24},{24,28},{28,32},{32,36}... | collective-permute-start | bytes 1548296 | tf_op jit(solution)/shard_map/ppermute | solution.py:16
  49.7 1.3 %maximum_bitcast_fusion.x0_ref.x1_ref.x2_ref = bf16[1,8,336,192]{3,2,1,0:T(8,128)(2,1)S(1)} fusion(bf16[2,336,192]{2,1,0:T(8,128)(2,1)} %collective-permute-done.1, bf16[4,336,192]{2,1,0:T(8,128)(2,1)S(1)} %bitcast.52, bf16[2,336,192]{2,1,0:T(8,128)(2,1)} %collective-permute-done), kind=kLoop, calls=%fused_computation.12 | loop fusion | flops 1032192 | bytes 2064384 | tf_op jit(solution)/shard_map/broadcast_in_dim | solution.py:85
  51.1 8.8 %shard_map.77 = bf16[3,21,4,16,192]{4,3,2,1,0:T(8,128)(2,1)S(1)} custom-call(s32[12]{0:T(128)S(1)} %reshape.30.cols_ref, bf16[1,8,336,192]{3,2,1,0:T(8,128)(2,1)S(1)} %maximum_bitcast_fusion.x0_ref.x1_ref.x2_ref, bf16[1,8,336,192]{3,2,1,0:T(8,128)(2,1)S(1)} %maximum_bitcast_fusion.x0_ref.x1_ref.x2_ref, ...), custom_call_target="tpu_custom_call" | custom-call | flops 891813888 | bytes 5750784 | tf_op jit(solution)/shard_map/pallas_call | solution.py:47
  60.0 3.4 %collective-permute-start.8 = (bf16[2,336,192]{2,1,0:T(8,128)(2,1)S(1)}, bf16[2,336,192]{2,1,0:T(8,128)(2,1)}, u32[]{:S(2)}, u32[]{:S(2)}) collective-permute-start(bf16[2,336,192]{2,1,0:T(8,128)(2,1)S(1)} %slice.37), channel_id=1, source_target_pairs={{0,1},{1,2},{2,3},{3,0},{4,5},{5,6},{6,7},{7,4},{8,9},{9,10},{10,1... | collective-permute-start | bytes 774152 | tf_op jit(solution)/shard_map/ppermute | solution.py:16
  63.4 2.4 %collective-permute-start.6 = (bf16[2,336,192]{2,1,0:T(8,128)(2,1)S(1)}, bf16[2,336,192]{2,1,0:T(8,128)(2,1)}, u32[]{:S(2)}, u32[]{:S(2)}) collective-permute-start(bf16[2,336,192]{2,1,0:T(8,128)(2,1)S(1)} %slice.36), channel_id=1, source_target_pairs={{0,3},{1,0},{2,1},{3,2},{4,7},{5,4},{6,5},{7,6},{8,11},{9,8},{10,9... | collective-permute-start | bytes 774152 | tf_op jit(solution)/shard_map/ppermute | solution.py:16
  65.9 3.2 %fusion.4 = f32[4,16,192,21,1]{2,3,4,1,0:T(8,128)} fusion(bf16[3,21,4,16,192]{4,3,2,1,0:T(8,128)(2,1)S(1)} %shard_map.77, f32[3,84,84]{2,1,0:T(8,128)S(1)} %copy-done.7, s32[]{:T(128)S(6)} %select_n.45, s32[]{:T(128)S(6)} %select_n.48), kind=kOutput, calls=%fused_computation.5 | convolution fusion | flops 195084288 | bytes 3133448 | tf_op jit(solution)/shard_map/kab,kbrli->alri/dot_general | solution.py:103
  69.2 6.3 %collective-permute-start.9 = (bf16[2,336,192]{2,1,0:T(8,128)(2,1)}, bf16[2,336,192]{2,1,0:T(8,128)(2,1)}, u32[]{:S(2)}, u32[]{:S(2)}) collective-permute-start(bf16[2,336,192]{2,1,0:T(8,128)(2,1)} %collective-permute-done.8), channel_id=1, source_target_pairs={{0,508},{4,0},{8,4},{12,8},{16,12},{20,16},{24,20},{28,24},{32,28}... | collective-permute-start | bytes 774152 | tf_op jit(solution)/shard_map/ppermute | solution.py:16
  75.5 1.9 %collective-permute-start.7 = (bf16[2,336,192]{2,1,0:T(8,128)(2,1)}, bf16[2,336,192]{2,1,0:T(8,128)(2,1)}, u32[]{:S(2)}, u32[]{:S(2)}) collective-permute-start(bf16[2,336,192]{2,1,0:T(8,128)(2,1)} %collective-permute-done.6), channel_id=1, source_target_pairs={{0,4},{4,8},{8,12},{12,16},{16,20},{20,24},{24,28},{28,32},{32,36}... | collective-permute-start | bytes 774152 | tf_op jit(solution)/shard_map/ppermute | solution.py:16
  77.8 1.3 %copy.33 = bf16[2,2,336,192]{3,2,1,0:T(8,128)(2,1)S(1)} copy(bf16[2,2,336,192]{2,3,1,0:T(8,128)(2,1)} %collective-permute-done.4) | data formatting | bytes 1032192 | tf_op jit(solution)/shard_map/ppermute | solution.py:16
  79.8 11.4 %shard_map.78 = bf16[3,42,4,16,192]{4,3,2,1,0:T(8,128)(2,1)} custom-call(s32[12]{0:T(128)S(1)} %reshape.30.cols_ref, bf16[2,8,336,192]{3,2,1,0:T(8,128)(2,1)S(1)} %pad_maximum_fusion.x0_ref.x1_ref.x2_ref, bf16[2,8,336,192]{3,2,1,0:T(8,128)(2,1)S(1)} %pad_maximum_fusion.x0_ref.x1_ref.x2_ref, ...), custom_call_target="tpu_custom_call" | custom-call | flops 1783627776 | bytes 8847360 | tf_op jit(solution)/shard_map/pallas_call | solution.py:47
  91.2 1.6 %maximum_bitcast_fusion.1.x0_ref.x1_ref.x2_ref = bf16[1,8,336,192]{3,2,1,0:T(8,128)(2,1)S(1)} fusion(bf16[2,336,192]{2,1,0:T(8,128)(2,1)} %collective-permute-done.9, bf16[2,336,192]{2,1,0:T(8,128)(2,1)} %collective-permute-done.6, bf16[2,336,192]{2,1,0:T(8,128)(2,1)} %collective-permute-done.8, bf16[2,336,192]{2,1,0:T(8,128)(2,1)} %collective-permute-done.7), kind=kLoop, calls=%fused_computation.15 | loop fusion | flops 1548288 | bytes 2064384 | tf_op jit(solution)/shard_map/broadcast_in_dim | solution.py:89
  92.8 9.3 %shard_map.79 = bf16[3,21,4,16,192]{4,3,2,1,0:T(8,128)(2,1)S(1)} custom-call(s32[12]{0:T(128)S(1)} %reshape.30.cols_ref, bf16[1,8,336,192]{3,2,1,0:T(8,128)(2,1)S(1)} %maximum_bitcast_fusion.1.x0_ref.x1_ref.x2_ref, bf16[1,8,336,192]{3,2,1,0:T(8,128)(2,1)S(1)} %maximum_bitcast_fusion.1.x0_ref.x1_ref.x2_ref, ...), custom_call_target="tpu_custom_call" | custom-call | flops 891813888 | bytes 5750784 | tf_op jit(solution)/shard_map/pallas_call | solution.py:47
  102.1 3.7 %fusion = f32[4,16,192,21,1]{2,3,4,1,0:T(8,128)S(1)} fusion(bf16[3,42,4,16,192]{4,3,2,1,0:T(8,128)(2,1)S(1)} %copy-done, f32[3,21,21]{2,1,0:T(8,128)S(1)} %get-tuple-element.11, f32[3,21,21]{2,1,0:T(8,128)S(1)} %get-tuple-element.10), kind=kOutput, calls=%fused_computation | convolution fusion | flops 390171232 | bytes 4139352 | tf_op jit(solution)/shard_map/kab,kbrli->alri/dot_general | solution.py:103
  105.8 2.1 %fusion.6 = f32[21,16,4,192]{3,0,1,2:T(8,128)S(1)} fusion(f32[4,16,192,21,1]{2,3,4,1,0:T(8,128)S(1)} %fusion, f32[4,16,192,21,1]{2,3,4,1,0:T(8,128)S(1)} %copy-done.3, bf16[3,21,4,16,192]{4,3,2,1,0:T(8,128)(2,1)S(1)} %shard_map.79, f32[3,84,84]{2,1,0:T(8,128)S(1)} %copy-done.7, s32[]{:T(128)S(6)} %select_n.45, s32[]{:T(128)S(6)} %select_n.57), kind=kOutput, calls=%fused_computation.8 | convolution fusion | flops 195600384 | bytes 6279176 | tf_op jit(solution)/shard_map/kab,kbrli->alri/dot_general | solution.py:103
  (50 shorter events, 16.1 us)
Async XLA Ops:
  2.6 22.6 %copy-start.1 = (bf16[21,16,4,192]{3,1,0,2:T(8,128)(2,1)}, bf16[21,16,4,192]{3,1,0,2:T(8,128)(2,1)S(1)}, u32[]{:S(2)}) copy-start(bf16[21,16,4,192]{3,1,0,2:T(8,128)(2,1)S(1)} %copy.63) | copy-start | bytes 1548292
  2.6 22.6 %copy-start.8 = (s32[4,3]{1,0:T(4,128)S(1)}, s32[4,3]{1,0:T(4,128)}, u32[]{:S(2)}) copy-start(s32[4,3]{1,0:T(4,128)} %param.10) | copy-start | bytes 148
  3.7 32.0 %collective-permute-start.2 = (bf16[4,336,192]{1,2,0:T(8,128)(2,1)}, bf16[4,336,192]{1,2,0:T(8,128)(2,1)}, u32[]{:S(2)}, u32[]{:S(2)}) collective-permute-start(bf16[4,336,192]{1,2,0:T(8,128)(2,1)} %copy.27), channel_id=1, source_target_pairs={{0,1},{1,2},{2,3},{3,0},{4,5},{5,6},{6,7},{7,4},{8,9},{9,10},{10,1... | collective-permute-start | bytes 1548296 | tf_op jit(solution)/shard_map/ppermute | solution.py:16
  7.1 29.9 %collective-permute-start.3 = (bf16[4,336,192]{1,2,0:T(8,128)(2,1)}, bf16[4,336,192]{1,2,0:T(8,128)(2,1)}, u32[]{:S(2)}, u32[]{:S(2)}) collective-permute-start(bf16[4,336,192]{1,2,0:T(8,128)(2,1)} %copy.27), channel_id=1, source_target_pairs={{0,3},{1,0},{2,1},{3,2},{4,7},{5,4},{6,5},{7,6},{8,11},{9,8},{10,9... | collective-permute-start | bytes 1548296 | tf_op jit(solution)/shard_map/ppermute | solution.py:16
  14.4 35.3 %collective-permute-start.1 = (bf16[2,336,192]{2,1,0:T(8,128)(2,1)}, bf16[2,336,192]{2,1,0:T(8,128)(2,1)}, u32[]{:S(2)}, u32[]{:S(2)}) collective-permute-start(bf16[2,336,192]{2,1,0:T(8,128)(2,1)} %bitcast.3), channel_id=1, source_target_pairs={{0,508},{4,0},{8,4},{12,8},{16,12},{20,16},{24,20},{28,24},{32,28}... | collective-permute-start | bytes 774152 | tf_op jit(solution)/shard_map/ppermute | solution.py:16
  23.3 26.4 %collective-permute-start = (bf16[2,336,192]{2,1,0:T(8,128)(2,1)}, bf16[2,336,192]{2,1,0:T(8,128)(2,1)}, u32[]{:S(2)}, u32[]{:S(2)}) collective-permute-start(bf16[2,336,192]{2,1,0:T(8,128)(2,1)} %bitcast.1), channel_id=1, source_target_pairs={{0,4},{4,8},{8,12},{12,16},{16,20},{20,24},{24,28},{28,32},{32,36}... | collective-permute-start | bytes 774152 | tf_op jit(solution)/shard_map/ppermute | solution.py:16
  38.6 11.1 %copy-start.2 = (bf16[21,16,4,192]{3,1,0,2:T(8,128)(2,1)S(1)}, bf16[21,16,4,192]{3,1,0,2:T(8,128)(2,1)}, u32[]{:S(2)}) copy-start(bf16[21,16,4,192]{3,1,0,2:T(8,128)(2,1)} %copy-done.1) | copy-start | bytes 1548292
  39.7 37.7 %collective-permute-start.5 = (bf16[2,2,336,192]{2,3,1,0:T(8,128)(2,1)}, bf16[2,2,336,192]{2,3,1,0:T(8,128)(2,1)S(1)}, u32[]{:S(2)}, u32[]{:S(2)}) collective-permute-start(bf16[2,2,336,192]{2,3,1,0:T(8,128)(2,1)} %copy.32), channel_id=1, source_target_pairs={{0,508},{4,0},{8,4},{12,8},{16,12},{20,16},{24,20},{28,24},{32,28}... | collective-permute-start | bytes 1548296 | tf_op jit(solution)/shard_map/ppermute | solution.py:16
  47.8 30.0 %collective-permute-start.4 = (bf16[2,2,336,192]{2,3,1,0:T(8,128)(2,1)}, bf16[2,2,336,192]{2,3,1,0:T(8,128)(2,1)}, u32[]{:S(2)}, u32[]{:S(2)}) collective-permute-start(bf16[2,2,336,192]{2,3,1,0:T(8,128)(2,1)} %copy.31), channel_id=1, source_target_pairs={{0,4},{4,8},{8,12},{12,16},{16,20},{20,24},{24,28},{28,32},{32,36}... | collective-permute-start | bytes 1548296 | tf_op jit(solution)/shard_map/ppermute | solution.py:16
  51.1 14.8 %copy-start.7 = (f32[3,84,84]{2,1,0:T(8,128)S(1)}, f32[3,84,84]{2,1,0:T(8,128)}, u32[]{:S(2)}) copy-start(f32[3,84,84]{2,1,0:T(8,128)} %param.11) | copy-start | bytes 254020
  60.0 9.2 %collective-permute-start.8 = (bf16[2,336,192]{2,1,0:T(8,128)(2,1)S(1)}, bf16[2,336,192]{2,1,0:T(8,128)(2,1)}, u32[]{:S(2)}, u32[]{:S(2)}) collective-permute-start(bf16[2,336,192]{2,1,0:T(8,128)(2,1)S(1)} %slice.37), channel_id=1, source_target_pairs={{0,1},{1,2},{2,3},{3,0},{4,5},{5,6},{6,7},{7,4},{8,9},{9,10},{10,1... | collective-permute-start | bytes 774152 | tf_op jit(solution)/shard_map/ppermute | solution.py:16
  63.4 12.1 %collective-permute-start.6 = (bf16[2,336,192]{2,1,0:T(8,128)(2,1)S(1)}, bf16[2,336,192]{2,1,0:T(8,128)(2,1)}, u32[]{:S(2)}, u32[]{:S(2)}) collective-permute-start(bf16[2,336,192]{2,1,0:T(8,128)(2,1)S(1)} %slice.36), channel_id=1, source_target_pairs={{0,3},{1,0},{2,1},{3,2},{4,7},{5,4},{6,5},{7,6},{8,11},{9,8},{10,9... | collective-permute-start | bytes 774152 | tf_op jit(solution)/shard_map/ppermute | solution.py:16
  69.2 21.9 %collective-permute-start.9 = (bf16[2,336,192]{2,1,0:T(8,128)(2,1)}, bf16[2,336,192]{2,1,0:T(8,128)(2,1)}, u32[]{:S(2)}, u32[]{:S(2)}) collective-permute-start(bf16[2,336,192]{2,1,0:T(8,128)(2,1)} %collective-permute-done.8), channel_id=1, source_target_pairs={{0,508},{4,0},{8,4},{12,8},{16,12},{20,16},{24,20},{28,24},{32,28}... | collective-permute-start | bytes 774152 | tf_op jit(solution)/shard_map/ppermute | solution.py:16
  75.5 15.7 %collective-permute-start.7 = (bf16[2,336,192]{2,1,0:T(8,128)(2,1)}, bf16[2,336,192]{2,1,0:T(8,128)(2,1)}, u32[]{:S(2)}, u32[]{:S(2)}) collective-permute-start(bf16[2,336,192]{2,1,0:T(8,128)(2,1)} %collective-permute-done.6), channel_id=1, source_target_pairs={{0,4},{4,8},{8,12},{12,16},{16,20},{20,24},{24,28},{28,32},{32,36}... | collective-permute-start | bytes 774152 | tf_op jit(solution)/shard_map/ppermute | solution.py:16
  92.7 9.3 %copy-start = (bf16[3,42,4,16,192]{4,3,2,1,0:T(8,128)(2,1)S(1)}, bf16[3,42,4,16,192]{4,3,2,1,0:T(8,128)(2,1)}, u32[]{:S(2)}) copy-start(bf16[3,42,4,16,192]{4,3,2,1,0:T(8,128)(2,1)} %shard_map.78) | copy-start | bytes 9289732
  102.1 3.7 %copy-start.3 = (f32[4,16,192,21,1]{2,3,4,1,0:T(8,128)S(1)}, f32[4,16,192,21,1]{2,3,4,1,0:T(8,128)}, u32[]{:S(2)}) copy-start(f32[4,16,192,21,1]{2,3,4,1,0:T(8,128)} %fusion.4) | copy-start | bytes 3096580
  108.8 1.2 %copy-start.6 = (f32[21,16,768]{2,1,0:T(8,128)S(1)}, f32[21,16,768]{2,1,0:T(8,128)}, u32[]{:S(2)}) copy-start(f32[21,16,768]{2,1,0:T(8,128)} %param.7) | copy-start | bytes 3096580
  110.0 1.7 %copy-start.5 = (bf16[4,192,192,1]{2,1,0,3:T(8,128)(2,1)S(1)}, bf16[4,192,192,1]{2,1,0,3:T(8,128)(2,1)}, u32[]{:S(2)}) copy-start(bf16[4,192,192,1]{2,1,0,3:T(8,128)(2,1)} %reshape.43) | copy-start | bytes 884740
  113.1 1.2 %copy-start.4 = (f32[21,16,768]{2,1,0:T(8,128)S(1)}, f32[21,16,768]{2,1,0:T(8,128)}, u32[]{:S(2)}) copy-start(f32[21,16,768]{2,1,0:T(8,128)} %param.6) | copy-start | bytes 3096580

commit v3 on v0

v3 whole, which is shorter than its diff:
```python
import jax
import jax.numpy as jnp
from jax import lax
from jax.experimental import pallas as pl
from jax.experimental.pallas import tpu as pltpu
from jax.sharding import PartitionSpec as P

H = 2


RELAXATION = 0.7


def shift(x, axis, k):
    devices = lax.axis_size(axis)
    return lax.ppermute(x, axis, [(i, (i + k) % devices) for i in range(devices)])


def stiffness_kernel(cols_ref, x0_ref, x1_ref, x2_ref, t_ref, o_ref):
    acc = None
    for s, x_ref in enumerate((x0_ref, x1_ref, x2_ref)):
        d = jnp.dot(x_ref[...], t_ref[s], preferred_element_type=jnp.float32)
        acc = d if acc is None else acc + d
    o_ref[...] = acc.astype(o_ref.dtype)


def stiffness(cols, ext, tiles_t, term):
    _, blocks, slots, bs, _ = tiles_t.shape
    _, rows, _ = ext.shape

    def x_spec(s):
        return pl.BlockSpec((None, rows, bs), lambda r, c: (c[r * slots + s], 0, 0))

    return pl.pallas_call(
        stiffness_kernel,
        out_shape=jax.ShapeDtypeStruct((blocks, rows, bs), jnp.bfloat16),
        grid_spec=pltpu.PrefetchScalarGridSpec(
            num_scalar_prefetch=1,
            grid=(blocks,),
            in_specs=[x_spec(s) for s in range(slots)]
            + [pl.BlockSpec((None, None, slots, bs, bs), lambda r, c: (term, r, 0, 0, 0))],
            out_specs=pl.BlockSpec((None, rows, bs), lambda r, c: (r, 0, 0)),
        ),
        cost_estimate=pl.CostEstimate(
            flops=2 * blocks * slots * rows * bs * bs,
            transcendentals=0,
            bytes_accessed=2 * (blocks * slots * bs * bs + blocks * slots * rows * bs + blocks * rows * bs),
        ),
    )(cols, ext, ext, ext, tiles_t)


def body(iterate, forcing, tiles, inverse_blocks, columns, coupling):
    modes_here, loads, dofs_here = iterate.shape
    terms, block_count, slots = tiles.shape[:3]
    block_size = dofs_here // block_count
    nm = lax.axis_size("mode")
    me = lax.axis_index("mode")
    cols = columns.reshape(-1).astype(jnp.int32)
    rounded = iterate.astype(jnp.bfloat16).reshape(modes_here, loads, block_count, block_size)
    own = jnp.transpose(rounded, (2, 0, 1, 3)).reshape(block_count, modes_here * loads, block_size)
    ext = jnp.concatenate(
        [shift(own[block_count - H:], "space", 1), own, shift(own[:H], "space", -1)], axis=0
    )
    coupling4 = coupling.reshape(terms, nm * modes_here, nm, modes_here)
    mixture = None
    for k in range(terms):
        tiles_k = jnp.swapaxes(
            tiles[k].reshape(1, block_count, slots, block_size, block_size), 3, 4
        )
        products = stiffness(cols, ext, tiles_k, 0)
        quarter = lax.all_to_all(products, "mode", 0, 0, tiled=True)
        quarter = quarter.reshape(nm, modes_here, loads, block_size)
        term = jnp.einsum(
            "aSp,Spli->ali",
            coupling4[k],
            quarter.astype(jnp.float32),
            precision=lax.Precision.HIGHEST,
        )
        mixture = term if mixture is None else mixture + term
    back = lax.all_to_all(mixture, "mode", 0, 0, tiled=True)
    back = back.reshape(nm, modes_here, loads, block_size)
    applied = jnp.transpose(back, (1, 2, 0, 3)).reshape(modes_here, loads, dofs_here)
    residual = forcing - applied
    rounded_res = residual.astype(jnp.bfloat16).reshape(modes_here, loads, block_count, block_size)
    inverse = inverse_blocks.reshape(block_count, block_size, block_size)
    update = jnp.einsum("jim,pljm->plji", inverse, rounded_res, preferred_element_type=jnp.float32)
    updated = iterate + RELAXATION * update.reshape(modes_here, loads, dofs_here)
    return (updated, residual)


def solution(mesh):
    return jax.shard_map(
        body,
        mesh=mesh,
        in_specs=(
            P("mode", None, "space"),
            P("mode", None, "space"),
            P(None, "space", None, None),
            P("space", None),
            P("space", None),
            P(),
        ),
        out_specs=(P("mode", None, "space"), P("mode", None, "space")),
        check_vma=False,
    )
```

time: 89.8 us -> 111 us (1.24)
  the two profiles are of different devices: /device:TPU:56 before, /device:TPU:2 now
where the time goes in v3:
time: 111 us; the launch traced here: 110 us
  starting transfers between devices  34.9 us (31%)
  local copies, waits for them, and re-layouts  31.4 us (28%)
  waiting for transfers between devices  17 us (15%)
  Pallas kernels  15 us (14%)
  other arithmetic  7.09 us (6%)
  matrix products  3.98 us (4%)
    ppermute x2, starting transfers between devices, shift(): lax.ppermute(x, axis, [(i, (i + k) % devices) for i in range(devices)])  15.3 us
    pallas_call x3, Pallas kernels, stiffness(): pl.pallas_call(stiffness_kernel, out_shape=jax.ShapeDtypeStruct((blocks,...  15 us
    all_to_all x3, starting transfers between devices, body(): quarter = lax.all_to_all(products, 'mode', 0, 0, tiled=True)  14.4 us
    all_to_all x1, waiting for transfers between devices, body(): back = lax.all_to_all(mixture, 'mode', 0, 0, tiled=True)  10.8 us
    another operation x6, local copies, waits for them, and re-layouts, body(): tiles[k].reshape(1, block_count, slots, block_size, block_size)  9.61 us
    pallas_call x3, local copies, waits for them, and re-layouts, stiffness(): pl.pallas_call(stiffness_kernel, out_shape=jax.ShapeDtypeStruct((blocks,...  6.71 us
    all_to_all x1, starting transfers between devices, body(): back = lax.all_to_all(mixture, 'mode', 0, 0, tiled=True)  5.1 us
    dot_general x3, matrix products, body(): jnp.einsum('aSp,Spli->ali', coupling4[k], quarter.astype(jnp.float32), pr...  3.6 us
  transfers between devices with their start and end apart: 6, of which 3 were waited for; matrix products, arithmetic and copies ran while one was open for 19% of the time, Pallas kernels for 9%

profile of v3, /device:TPU:2, one launch (start us, length us, event | category | flops | bytes accessed | tf_op | source)
XLA Modules:
  0.0 110.2 jit_solution(3685457166197886332)
XLA Ops:
  2.7 13.4 %collective-permute-start.1 = (bf16[2,336,192]{2,1,0:T(8,128)(2,1)S(1)}, bf16[2,336,192]{2,1,0:T(8,128)(2,1)}, u32[]{:S(2)}, u32[]{:S(2)}) collective-permute-start(bf16[2,336,192]{2,1,0:T(8,128)(2,1)S(1)} %bitcast.58), channel_id=1, source_target_pairs={{0,508},{4,0},{8,4},{12,8},{16,12},{20,16},{24,20},{28,24},{32,28}... | collective-permute-start | bytes 774152 | tf_op jit(solution)/shard_map/ppermute | solution.py:16
  16.1 1.9 %collective-permute-start = (bf16[2,336,192]{2,1,0:T(8,128)(2,1)S(1)}, bf16[2,336,192]{2,1,0:T(8,128)(2,1)}, u32[]{:S(2)}, u32[]{:S(2)}) collective-permute-start(bf16[2,336,192]{2,1,0:T(8,128)(2,1)S(1)} %bitcast.57), channel_id=1, source_target_pairs={{0,4},{4,8},{8,12},{12,16},{16,20},{20,24},{24,28},{28,32},{32,36}... | collective-permute-start | bytes 774152 | tf_op jit(solution)/shard_map/ppermute | solution.py:16
  18.1 2.2 %fusion.7 = (bf16[1,4,3,36864]{3,1,2,0:T(4,128)(2,1)S(1)}, bf16[1,4,3,36864]{3,1,2,0:T(4,128)(2,1)}, bf16[1,4,3,36864]{3,1,2,0:T(4,128)(2,1)}) fusion(bf16[3,4,3,36864]{3,1,2,0:T(4,128)(2,1)S(1)} %copy-done.3), kind=kLoop, calls=%fused_computation.14 | loop fusion | bytes 5308416 | tf_op jit(solution)/shard_map/slice | solution.py:68
  20.9 2.3 %reshape_squeeze.11 = bf16[1,4,3,192,192]{4,3,1,2,0:T(8,128)(2,1)S(1)} reshape(bf16[1,4,3,36864]{3,1,2,0:T(4,128)(2,1)} %get-tuple-element.5) | data formatting | bytes 1769472 | tf_op jit(solution)/shard_map/reshape;squeeze | solution.py:68
  23.2 1.5 %copy.69 = bf16[1,4,3,192,192]{3,4,2,1,0:T(8,128)(2,1)} copy(bf16[1,4,3,192,192]{4,3,1,2,0:T(8,128)(2,1)S(1)} %reshape_squeeze.11) | data formatting | bytes 1769472 | tf_op jit(solution)/shard_map/reshape;squeeze | solution.py:68
  24.7 3.4 %collective-permute-done = bf16[2,336,192]{2,1,0:T(8,128)(2,1)} collective-permute-done((bf16[2,336,192]{2,1,0:T(8,128)(2,1)S(1)}, bf16[2,336,192]{2,1,0:T(8,128)(2,1)}, u32[]{:S(2)}, u32[]{:S(2)}) %collective-permute-start) | collective-permute-done | bytes 258080 | tf_op jit(solution)/shard_map/ppermute | solution.py:16
  28.1 2.4 %pad_maximum_fusion.x0_ref.x1_ref.x2_ref = bf16[8,336,192]{2,1,0:T(8,128)(2,1)} fusion(bf16[2,336,192]{2,1,0:T(8,128)(2,1)} %collective-permute-done.1, bf16[4,336,192]{2,1,0:T(8,128)(2,1)S(1)} %bitcast.49, bf16[2,336,192]{2,1,0:T(8,128)(2,1)} %collective-permute-done), kind=kLoop, calls=%fused_computation.6 | loop fusion | flops 1032192 | bytes 2064384 | tf_op jit(solution)/shard_map/concatenate | solution.py:61
  30.5 5.0 %shard_map.79 = bf16[4,336,192]{2,1,0:T(8,128)(2,1)} custom-call(s32[12]{0:T(128)} %reshape.46.cols_ref, bf16[8,336,192]{2,1,0:T(8,128)(2,1)} %pad_maximum_fusion.x0_ref.x1_ref.x2_ref, bf16[8,336,192]{2,1,0:T(8,128)(2,1)} %pad_maximum_fusion.x0_ref.x1_ref.x2_ref, bf16[8,336,192]{2,1,0:T(8,128)(2,1)} %pad_maximum_fusion.x0_ref.x1_ref.x2_ref, ...), custom_call_target="tpu_custom_call" | custom-call | flops 297271296 | bytes 2949120 | tf_op jit(solution)/shard_map/pallas_call | solution.py:34
  35.6 2.3 %copy.70 = bf16[4,336,192]{1,2,0:T(8,128)(2,1)} copy(bf16[4,336,192]{2,1,0:T(8,128)(2,1)} %shard_map.79) | data formatting | bytes 1032192 | tf_op jit(solution)/shard_map/pallas_call | solution.py:34
  37.8 4.8 %all-to-all-start.2 = ((bf16[4,336,192]{1,2,0:T(8,128)(2,1)}), bf16[4,336,192]{1,2,0:T(8,128)(2,1)S(1)}, u32[]{:S(2)}, u32[]{:S(2)}) async-start(bf16[4,336,192]{1,2,0:T(8,128)(2,1)} %copy.70), calls=%async_computation.2 | async-start | bytes 1179648 | tf_op jit(solution)/shard_map/all_to_all | solution.py:71
  44.0 1.5 %copy.64 = bf16[1,4,3,192,192]{3,4,2,1,0:T(8,128)(2,1)} copy(bf16[1,4,3,192,192]{4,3,1,2,0:T(8,128)(2,1)S(1)} %reshape_squeeze.10) | data formatting | bytes 1769472 | tf_op jit(solution)/shard_map/reshape;squeeze | solution.py:68
  45.5 5.0 %shard_map.78 = bf16[4,336,192]{2,1,0:T(8,128)(2,1)} custom-call(s32[12]{0:T(128)} %reshape.46.cols_ref, bf16[8,336,192]{2,1,0:T(8,128)(2,1)} %pad_maximum_fusion.x0_ref.x1_ref.x2_ref, bf16[8,336,192]{2,1,0:T(8,128)(2,1)} %pad_maximum_fusion.x0_ref.x1_ref.x2_ref, bf16[8,336,192]{2,1,0:T(8,128)(2,1)} %pad_maximum_fusion.x0_ref.x1_ref.x2_ref, ...), custom_call_target="tpu_custom_call" | custom-call | flops 297271296 | bytes 2949120 | tf_op jit(solution)/shard_map/pallas_call | solution.py:34
  50.6 2.2 %copy.65 = bf16[4,336,192]{1,2,0:T(8,128)(2,1)} copy(bf16[4,336,192]{2,1,0:T(8,128)(2,1)} %shard_map.78) | data formatting | bytes 1032192 | tf_op jit(solution)/shard_map/pallas_call | solution.py:34
  52.7 4.8 %all-to-all-start.1 = ((bf16[4,336,192]{1,2,0:T(8,128)(2,1)}), bf16[4,336,192]{1,2,0:T(8,128)(2,1)S(1)}, u32[]{:S(2)}, u32[]{:S(2)}) async-start(bf16[4,336,192]{1,2,0:T(8,128)(2,1)} %copy.65), calls=%async_computation.1 | async-start | bytes 1179648 | tf_op jit(solution)/shard_map/all_to_all | solution.py:71
  60.4 5.0 %shard_map.77 = bf16[4,336,192]{2,1,0:T(8,128)(2,1)} custom-call(s32[12]{0:T(128)} %reshape.46.cols_ref, bf16[8,336,192]{2,1,0:T(8,128)(2,1)} %pad_maximum_fusion.x0_ref.x1_ref.x2_ref, bf16[8,336,192]{2,1,0:T(8,128)(2,1)} %pad_maximum_fusion.x0_ref.x1_ref.x2_ref, bf16[8,336,192]{2,1,0:T(8,128)(2,1)} %pad_maximum_fusion.x0_ref.x1_ref.x2_ref, ...), custom_call_target="tpu_custom_call" | custom-call | flops 297271296 | bytes 2949120 | tf_op jit(solution)/shard_map/pallas_call | solution.py:34
  65.4 2.2 %copy.60 = bf16[4,336,192]{1,2,0:T(8,128)(2,1)} copy(bf16[4,336,192]{2,1,0:T(8,128)(2,1)} %shard_map.77) | data formatting | bytes 1032192 | tf_op jit(solution)/shard_map/pallas_call | solution.py:34
  67.7 4.8 %all-to-all-start = ((bf16[4,336,192]{1,2,0:T(8,128)(2,1)}), bf16[4,336,192]{1,2,0:T(8,128)(2,1)}, u32[]{:S(2)}, u32[]{:S(2)}) async-start(bf16[4,336,192]{1,2,0:T(8,128)(2,1)} %copy.60), calls=%async_computation | async-start | bytes 1179648 | tf_op jit(solution)/shard_map/all_to_all | solution.py:71
  76.8 2.8 %all-to-all-done = bf16[4,336,192]{1,2,0:T(8,128)(2,1)} async-done(((bf16[4,336,192]{1,2,0:T(8,128)(2,1)}), bf16[4,336,192]{1,2,0:T(8,128)(2,1)}, u32[]{:S(2)}, u32[]{:S(2)}) %all-to-all-start) | async-done | bytes 516128 | tf_op jit(solution)/shard_map/all_to_all | solution.py:71
  79.6 2.2 %copy.61 = bf16[4,336,192]{2,1,0:T(8,128)(2,1)} copy(bf16[4,336,192]{1,2,0:T(8,128)(2,1)} %all-to-all-done) | data formatting | bytes 1032192 | tf_op jit(solution)/shard_map/all_to_all | solution.py:71
  81.8 2.0 %add_bitcast_fusion = f32[84,16,192]{2,0,1:T(8,128)S(1)} fusion(f32[16,192,84]{1,2,0:T(8,128)S(1)} %convolution_bitcast_fusion, f32[16,192,84]{1,2,0:T(8,128)S(1)} %convolution_bitcast_fusion.1, f32[84,4,21,1]{0,2,1,3:T(8,128)S(1)} %reshape.56, bf16[4,21,16,192]{3,2,1,0:T(8,128)(2,1)} %bitcast.54), kind=kOutput, calls=%fused_computation.5 | convolution fusion | flops 260628480 | bytes 3640896 | tf_op jit(solution)/shard_map/aSp,Spli->ali/dot_general | solution.py:73
  83.8 1.5 %copy.74 = f32[84,16,192]{2,1,0:T(8,128)} copy(f32[84,16,192]{2,0,1:T(8,128)S(1)} %add_bitcast_fusion) | data formatting | bytes 2064384 | tf_op jit(solution)/shard_map/add | solution.py:79
  85.3 5.1 %all-to-all-start.3 = ((f32[84,16,192]{2,1,0:T(8,128)}), f32[84,16,192]{2,1,0:T(8,128)S(1)}, u32[]{:S(2)}, u32[]{:S(2)}) async-start(f32[84,16,192]{2,1,0:T(8,128)} %copy.74), calls=%async_computation.3 | async-start | bytes 2752512 | tf_op jit(solution)/shard_map/all_to_all | solution.py:80
  90.9 10.8 %all-to-all-done.3 = f32[84,16,192]{2,1,0:T(8,128)S(1)} async-done(((f32[84,16,192]{2,1,0:T(8,128)}), f32[84,16,192]{2,1,0:T(8,128)S(1)}, u32[]{:S(2)}, u32[]{:S(2)}) %all-to-all-start.3) | async-done | bytes 1032224 | tf_op jit(solution)/shard_map/all_to_all | solution.py:80
  103.6 2.3 %fusion.6 = (bf16[21,16,768]{2,1,0:T(8,128)(2,1)S(1)}, f32[21,16,768]{2,1,0:T(8,128)}) fusion(f32[21,16,768]{2,1,0:T(8,128)} %param.7, f32[21,16,768]{2,1,0:T(8,128)S(1)} %reshape.53), kind=kLoop, calls=%fused_computation.13 | loop fusion | flops 516096 | bytes 3612672 | tf_op jit(solution)/shard_map/convert_element_type | solution.py:84
  (46 shorter events, 17.8 us)
Async XLA Ops:
  2.5 15.5 %copy-start.3 = (bf16[3,4,3,36864]{3,1,2,0:T(4,128)(2,1)S(1)}, bf16[3,4,3,36864]{3,1,2,0:T(4,128)(2,1)}, u32[]{:S(2)}) copy-start(bf16[3,4,3,36864]{3,1,2,0:T(4,128)(2,1)} %param.8) | copy-start | bytes 7962628
  2.7 22.0 %collective-permute-start.1 = (bf16[2,336,192]{2,1,0:T(8,128)(2,1)S(1)}, bf16[2,336,192]{2,1,0:T(8,128)(2,1)}, u32[]{:S(2)}, u32[]{:S(2)}) collective-permute-start(bf16[2,336,192]{2,1,0:T(8,128)(2,1)S(1)} %bitcast.58), channel_id=1, source_target_pairs={{0,508},{4,0},{8,4},{12,8},{16,12},{20,16},{24,20},{28,24},{32,28}... | collective-permute-start | bytes 774152 | tf_op jit(solution)/shard_map/ppermute | solution.py:16
  16.1 4.1 %copy-start.7 = (s32[4,3]{1,0:T(4,128)S(1)}, s32[4,3]{1,0:T(4,128)}, u32[]{:S(2)}) copy-start(s32[4,3]{1,0:T(4,128)} %param.10) | copy-start | bytes 148
  16.1 12.0 %collective-permute-start = (bf16[2,336,192]{2,1,0:T(8,128)(2,1)S(1)}, bf16[2,336,192]{2,1,0:T(8,128)(2,1)}, u32[]{:S(2)}, u32[]{:S(2)}) collective-permute-start(bf16[2,336,192]{2,1,0:T(8,128)(2,1)S(1)} %bitcast.57), channel_id=1, source_target_pairs={{0,4},{4,8},{8,12},{12,16},{16,20},{20,24},{24,28},{28,32},{32,36}... | collective-permute-start | bytes 774152 | tf_op jit(solution)/shard_map/ppermute | solution.py:16
  35.6 7.1 %copy-start.1 = (bf16[1,4,3,36864]{3,1,2,0:T(4,128)(2,1)S(1)}, bf16[1,4,3,36864]{3,1,2,0:T(4,128)(2,1)}, u32[]{:S(2)}) copy-start(bf16[1,4,3,36864]{3,1,2,0:T(4,128)(2,1)} %get-tuple-element.6) | copy-start | bytes 2654212
  37.8 14.9 %all-to-all-start.2 = ((bf16[4,336,192]{1,2,0:T(8,128)(2,1)}), bf16[4,336,192]{1,2,0:T(8,128)(2,1)S(1)}, u32[]{:S(2)}, u32[]{:S(2)}) async-start(bf16[4,336,192]{1,2,0:T(8,128)(2,1)} %copy.70), calls=%async_computation.2 | async-start | bytes 1179648 | tf_op jit(solution)/shard_map/all_to_all | solution.py:71
  52.7 15.0 %all-to-all-start.1 = ((bf16[4,336,192]{1,2,0:T(8,128)(2,1)}), bf16[4,336,192]{1,2,0:T(8,128)(2,1)S(1)}, u32[]{:S(2)}, u32[]{:S(2)}) async-start(bf16[4,336,192]{1,2,0:T(8,128)(2,1)} %copy.65), calls=%async_computation.1 | async-start | bytes 1179648 | tf_op jit(solution)/shard_map/all_to_all | solution.py:71
  65.4 7.1 %copy-start.6 = (f32[3,84,84]{2,1,0:T(8,128)S(1)}, f32[3,84,84]{2,1,0:T(8,128)}, u32[]{:S(2)}) copy-start(f32[3,84,84]{2,1,0:T(8,128)} %param.11) | copy-start | bytes 254020
  67.7 11.9 %all-to-all-start = ((bf16[4,336,192]{1,2,0:T(8,128)(2,1)}), bf16[4,336,192]{1,2,0:T(8,128)(2,1)}, u32[]{:S(2)}, u32[]{:S(2)}) async-start(bf16[4,336,192]{1,2,0:T(8,128)(2,1)} %copy.60), calls=%async_computation | async-start | bytes 1179648 | tf_op jit(solution)/shard_map/all_to_all | solution.py:71
  74.9 1.1 copy-start.2
  74.9 1.1 copy-start.5
  85.3 5.1 %copy-start.4 = (bf16[4,36864]{1,0:T(4,128)(2,1)S(1)}, bf16[4,36864]{1,0:T(4,128)(2,1)}, u32[]{:S(2)}) copy-start(bf16[4,36864]{1,0:T(4,128)(2,1)} %param.9) | copy-start | bytes 884740
  85.3 16.3 %all-to-all-start.3 = ((f32[84,16,192]{2,1,0:T(8,128)}), f32[84,16,192]{2,1,0:T(8,128)S(1)}, u32[]{:S(2)}, u32[]{:S(2)}) async-start(f32[84,16,192]{2,1,0:T(8,128)} %copy.74), calls=%async_computation.3 | async-start | bytes 2752512 | tf_op jit(solution)/shard_map/all_to_all | solution.py:80
  107.9 1.2 %copy-start = (f32[21,16,768]{2,1,0:T(8,128)S(1)}, f32[21,16,768]{2,1,0:T(8,128)}, u32[]{:S(2)}) copy-start(f32[21,16,768]{2,1,0:T(8,128)} %param.6) | copy-start | bytes 3096580

commit v4 on v0

v4 whole, which is shorter than its diff:
```python
import jax
import jax.numpy as jnp
from jax import lax
from jax.sharding import PartitionSpec as P

H = 2


RELAXATION = 0.7


def padded(x, sides, width):
    for axis, dim in sides:
        devices, length = (lax.axis_size(axis), x.shape[dim])
        up = [(i, (i + 1) % devices) for i in range(devices)]
        down = [(j, i) for i, j in up]
        last = lax.slice_in_dim(x, length - width, length, axis=dim)
        initial = lax.slice_in_dim(x, 0, width, axis=dim)
        before = lax.ppermute(last, axis, up)
        after = lax.ppermute(initial, axis, down)
        x = jnp.concatenate([before, x, after], axis=dim)
    return x


def body(iterate, forcing, tiles, inverse_blocks, columns, coupling):
    modes_here, loads, dofs_here = iterate.shape
    terms, block_count, slots = tiles.shape[:3]
    block_size = dofs_here // block_count
    nm = lax.axis_size("mode")
    rounded = iterate.astype(jnp.bfloat16).reshape(modes_here, loads, block_count, block_size)
    extended = padded(rounded, (("space", 2),), H)
    picked = jnp.take(extended, columns, axis=2)
    coupling4 = coupling.reshape(terms, nm * modes_here, nm, modes_here)
    mixture = None
    for k in range(terms):
        shaped = tiles[k].reshape(block_count, slots, block_size, block_size)
        products = jnp.einsum(
            "rsim,plrsm->rpli", shaped, picked, preferred_element_type=jnp.float32
        ).astype(jnp.bfloat16)
        quarter = lax.all_to_all(products, "mode", 0, 0, tiled=True)
        term = jnp.einsum(
            "aSp,Spli->ali",
            coupling4[k],
            quarter.astype(jnp.float32),
            precision=lax.Precision.HIGHEST,
        )
        mixture = term if mixture is None else mixture + term
    back = lax.all_to_all(mixture, "mode", 0, 0, tiled=True)
    back = back.reshape(nm, modes_here, loads, block_size)
    applied = jnp.transpose(back, (1, 2, 0, 3)).reshape(modes_here, loads, dofs_here)
    residual = forcing - applied
    rounded_res = residual.astype(jnp.bfloat16).reshape(modes_here * loads, dofs_here)
    inverse = inverse_blocks.reshape(block_count, block_size, block_size)
    diagonal = jnp.eye(block_count, dtype=inverse.dtype)
    spread = jnp.einsum("rim,rs->rmsi", inverse, diagonal).reshape(dofs_here, dofs_here)
    update = jnp.dot(rounded_res, spread, preferred_element_type=jnp.float32)
    updated = iterate + RELAXATION * update.reshape(modes_here, loads, dofs_here)
    return (updated, residual)


def solution(mesh):
    return jax.shard_map(
        body,
        mesh=mesh,
        in_specs=(
            P("mode", None, "space"),
            P("mode", None, "space"),
            P(None, "space", None, None),
            P("space", None),
            P("space", None),
            P(),
        ),
        out_specs=(P("mode", None, "space"), P("mode", None, "space")),
        check_vma=False,
    )
```

time: 89.8 us -> 98.6 us (1.098)
  blocking collectives: 30.7 us -> 0 us
  waiting for transfers between devices: 19.1 us -> 35.4 us
  starting transfers between devices: 9.42 us -> 21.4 us
  local copies, waits for them, and re-layouts: 15.9 us -> 25.2 us
  matrix products: 6.89 us -> 12.2 us
  other arithmetic: 6.38 us -> 2.78 us
    all_to_all x1 -> x0, blocking collectives: 30.7 us -> none  [body(): lax.all_to_all(products, 'mode', split_axis=3, concat_axis=1, tiled=True)]
    all_to_all x1 -> x4, waiting for transfers between devices: 19 us -> 35.4 us  [the longest x3 21.1 us: body(): quarter = lax.all_to_all(products, 'mode', 0, 0, tiled=True)]
    all_to_all x1 -> x4, starting transfers between devices: 3.86 us -> 15.8 us  [the longest x3 12.1 us: body(): quarter = lax.all_to_all(products, 'mode', 0, 0, tiled=True)]
    another operation x0 -> x3, local copies, waits for them, and re-layouts: none -> 6.19 us  [body(): shaped = tiles[k].reshape(block_count, slots, block_size, block_size)]
    dot_general x3 -> x7, matrix products: 6.89 us -> 12.2 us  [the longest x3 5.97 us: body(): jnp.einsum('rsim,plrsm->rpli', shaped, picked, preferred_element_type=jnp...]
    reshape x3 -> x2, local copies, waits for them, and re-layouts: 7.97 us -> 3.13 us  [the longest x1 2.24 us: body(): jnp.einsum('rim,rs->rmsi', inverse, diagonal).reshape(dofs_here, dofs_here)]
    slice x0 -> x5, local copies, waits for them, and re-layouts: none -> 4.21 us  [the longest x1 3.91 us: body(): shaped = tiles[k].reshape(block_count, slots, block_size, block_size)]
    convert_element_type x0 -> x3, local copies, waits for them, and re-layouts: none -> 3.78 us  [body(): products = jnp.einsum('rsim,plrsm->rpli', shaped, picked, preferred_eleme...]
  transfers between devices with their start and end apart: 3 -> 6, of which waited for: 1 -> 4; matrix products, arithmetic and copies ran while one was open for 8% -> 25% of each run, Pallas kernels for 0% -> 0%
where the time goes in v4:
time: 98.6 us; the launch traced here: 98 us
  waiting for transfers between devices  35.4 us (36%)
  local copies, waits for them, and re-layouts  25.2 us (26%)
  starting transfers between devices  21.4 us (22%)
  matrix products  12.2 us (12%)
  other arithmetic  2.78 us (3%)
    all_to_all x3, waiting for transfers between devices, body(): quarter = lax.all_to_all(products, 'mode', 0, 0, tiled=True)  21.1 us
    all_to_all x1, waiting for transfers between devices, body(): back = lax.all_to_all(mixture, 'mode', 0, 0, tiled=True)  14.4 us
    all_to_all x3, starting transfers between devices, body(): quarter = lax.all_to_all(products, 'mode', 0, 0, tiled=True)  12.1 us
    another operation x3, local copies, waits for them, and re-layouts, body(): shaped = tiles[k].reshape(block_count, slots, block_size, block_size)  6.19 us
    dot_general x3, matrix products, body(): jnp.einsum('rsim,plrsm->rpli', shaped, picked, preferred_element_type=jnp...  5.97 us
    dot_general x3, matrix products, body(): jnp.einsum('aSp,Spli->ali', coupling4[k], quarter.astype(jnp.float32), pr...  4.73 us
    slice x1, local copies, waits for them, and re-layouts, body(): shaped = tiles[k].reshape(block_count, slots, block_size, block_size)  3.91 us
    convert_element_type x3, local copies, waits for them, and re-layouts, body(): products = jnp.einsum('rsim,plrsm->rpli', shaped, picked, preferred_eleme...  3.78 us
  transfers between devices with their start and end apart: 6, of which 4 were waited for; matrix products, arithmetic and copies ran while one was open for 25% of the time, Pallas kernels for 0%

profile of v4, /device:TPU:56, one launch (start us, length us, event | category | flops | bytes accessed | tf_op | source)
XLA Modules:
  0.0 98.0 jit_solution(507473400435020184)
XLA Ops:
  0.6 1.3 %convert_element_type.19 = bf16[21,16,768]{2,1,0:T(8,128)(2,1)S(1)} convert(f32[21,16,768]{2,1,0:T(8,128)} %param.6) | non-fusion elementwise | flops 258048 | bytes 1548288 | tf_op jit(solution)/shard_map/convert_element_type | solution.py:30
  2.7 1.9 %collective-permute-start = (bf16[21,16,2,192]{3,1,2,0:T(8,128)(2,1)S(1)}, bf16[21,16,2,192]{3,1,2,0:T(8,128)(2,1)S(1)}, u32[]{:S(2)}, u32[]{:S(2)}) collective-permute-start(bf16[21,16,2,192]{3,1,2,0:T(8,128)(2,1)S(1)} %get-tuple-element.5), channel_id=1, source_target_pairs={{0,4},{4,8},{8,12},{12,16},{16,20},{20,24},{24,28},{28,32},{32,36}... | collective-permute-start | bytes 774152 | tf_op jit(solution)/shard_map/ppermute | solution.py:19
  4.6 3.6 %collective-permute-start.1 = (bf16[21,16,2,192]{3,1,2,0:T(8,128)(2,1)S(1)}, bf16[21,16,2,192]{3,1,2,0:T(8,128)(2,1)S(1)}, u32[]{:S(2)}, u32[]{:S(2)}) collective-permute-start(bf16[21,16,2,192]{3,1,2,0:T(8,128)(2,1)S(1)} %get-tuple-element.6), channel_id=1, source_target_pairs={{4,0},{8,4},{12,8},{16,12},{20,16},{24,20},{28,24},{32,28},{36,32}... | collective-permute-start | bytes 774152 | tf_op jit(solution)/shard_map/ppermute | solution.py:20
  8.4 3.9 %fusion.24 = (bf16[1,4,3,36864]{3,1,2,0:T(4,128)(2,1)}, bf16[1,4,3,36864]{3,1,2,0:T(4,128)(2,1)}, bf16[1,4,3,36864]{3,1,2,0:T(4,128)(2,1)S(1)}) fusion(bf16[3,4,3,36864]{3,1,2,0:T(4,128)(2,1)} %param.8), kind=kLoop, calls=%fused_computation.34 | loop fusion | bytes 5308416 | tf_op jit(solution)/shard_map/slice | solution.py:36
  12.3 2.4 %reshape_squeeze.10 = bf16[4,3,192,192]{3,2,0,1:T(8,128)(2,1)} reshape(bf16[1,4,3,36864]{3,1,2,0:T(4,128)(2,1)S(1)} %get-tuple-element.4) | data formatting | bytes 1769472 | tf_op jit(solution)/shard_map/reshape;squeeze | solution.py:36
  16.0 1.3 %copy-done.6 = bf16[21,16,4,3,192]{4,1,0,3,2:T(8,128)(2,1)} copy-done((bf16[21,16,4,3,192]{4,1,0,3,2:T(8,128)(2,1)}, bf16[21,16,4,3,192]{4,1,0,3,2:T(8,128)(2,1)S(1)}, u32[]{:S(2)}) %copy-start.6) | copy-done | bytes 1548312
  19.4 4.3 %all-to-all-start.1 = ((bf16[4,21,16,192]{3,2,1,0:T(8,128)(2,1)}), bf16[4,21,16,192]{3,2,1,0:T(8,128)(2,1)S(1)}, u32[]{:S(2)}, u32[]{:S(2)}) async-start(bf16[4,21,16,192]{3,2,1,0:T(8,128)(2,1)} %copy.58), calls=%async_computation.1 | async-start | bytes 1376256 | tf_op jit(solution)/shard_map/all_to_all | solution.py:40
  23.7 1.4 %reshape_squeeze.11 = bf16[4,3,192,192]{3,2,0,1:T(8,128)(2,1)S(1)} reshape(bf16[1,4,3,36864]{3,1,2,0:T(4,128)(2,1)S(1)} %copy-done.4) | data formatting | bytes 1769472 | tf_op jit(solution)/shard_map/reshape;squeeze | solution.py:36
  25.1 2.4 %bitcast_convert_fusion = bf16[4,21,16,192]{3,1,0,2:T(8,128)(2,1)S(1)} fusion(bf16[21,16,4,3,192]{4,1,0,3,2:T(8,128)(2,1)} %copy-done.6, bf16[4,3,192,192]{3,2,0,1:T(8,128)(2,1)S(1)} %reshape_squeeze.11), kind=kOutput, calls=%fused_computation.8 | convolution fusion | flops 297529344 | bytes 2949120 | tf_op jit(solution)/shard_map/rsim,plrsm->rpli/dot_general | solution.py:37
  28.8 6.6 %all-to-all-done.1 = bf16[4,21,16,192]{3,2,1,0:T(8,128)(2,1)S(1)} async-done(((bf16[4,21,16,192]{3,2,1,0:T(8,128)(2,1)}), bf16[4,21,16,192]{3,2,1,0:T(8,128)(2,1)S(1)}, u32[]{:S(2)}, u32[]{:S(2)}) %all-to-all-start.1) | async-done | bytes 516128 | tf_op jit(solution)/shard_map/all_to_all | solution.py:40
  35.3 3.5 %all-to-all-start.2 = ((bf16[4,21,16,192]{3,2,1,0:T(8,128)(2,1)}), bf16[4,21,16,192]{3,2,1,0:T(8,128)(2,1)S(1)}, u32[]{:S(2)}, u32[]{:S(2)}) async-start(bf16[4,21,16,192]{3,2,1,0:T(8,128)(2,1)} %copy.63), calls=%async_computation.2 | async-start | bytes 1376256 | tf_op jit(solution)/shard_map/all_to_all | solution.py:40
  38.8 2.4 %reshape_squeeze.9 = bf16[4,3,192,192]{3,2,0,1:T(8,128)(2,1)} reshape(bf16[1,4,3,36864]{3,1,2,0:T(4,128)(2,1)S(1)} %copy-done.3) | data formatting | bytes 1769472 | tf_op jit(solution)/shard_map/reshape;squeeze | solution.py:36
  41.2 2.7 %bitcast_convert_fusion.2 = bf16[4,21,16,192]{3,1,0,2:T(8,128)(2,1)S(1)} fusion(bf16[21,16,4,3,192]{4,1,0,3,2:T(8,128)(2,1)} %copy-done.6, bf16[4,3,192,192]{3,2,0,1:T(8,128)(2,1)} %reshape_squeeze.9), kind=kOutput, calls=%fused_computation.10 | convolution fusion | flops 297529344 | bytes 2949120 | tf_op jit(solution)/shard_map/rsim,plrsm->rpli/dot_general | solution.py:37
  44.0 1.3 %copy.53 = bf16[4,21,16,192]{3,2,1,0:T(8,128)(2,1)} copy(bf16[4,21,16,192]{3,1,0,2:T(8,128)(2,1)S(1)} %bitcast_convert_fusion.2) | data formatting | bytes 1032192 | tf_op jit(solution)/shard_map/convert_element_type | solution.py:39
  45.3 6.0 %all-to-all-done.2 = bf16[4,21,16,192]{3,2,1,0:T(8,128)(2,1)S(1)} async-done(((bf16[4,21,16,192]{3,2,1,0:T(8,128)(2,1)}), bf16[4,21,16,192]{3,2,1,0:T(8,128)(2,1)S(1)}, u32[]{:S(2)}, u32[]{:S(2)}) %all-to-all-start.2) | async-done | bytes 516128 | tf_op jit(solution)/shard_map/all_to_all | solution.py:40
  51.3 4.3 %all-to-all-start = ((bf16[4,21,16,192]{3,2,1,0:T(8,128)(2,1)}), bf16[4,21,16,192]{3,2,1,0:T(8,128)(2,1)}, u32[]{:S(2)}, u32[]{:S(2)}) async-start(bf16[4,21,16,192]{3,2,1,0:T(8,128)(2,1)} %copy.53), calls=%async_computation | async-start | bytes 1376256 | tf_op jit(solution)/shard_map/all_to_all | solution.py:40
  56.8 1.9 %convolution_bitcast_fusion = f32[16,192,84]{1,2,0:T(8,128)S(1)} fusion(f32[84,4,21,1]{0,2,1,3:T(8,128)S(1)} %reshape.60, bf16[4,21,16,192]{3,2,1,0:T(8,128)(2,1)} %copy-done.5), kind=kOutput, calls=%fused_computation.12 | convolution fusion | flops 260112384 | bytes 1576512 | tf_op jit(solution)/shard_map/aSp,Spli->ali/dot_general | solution.py:41
  58.7 8.5 %all-to-all-done = bf16[4,21,16,192]{3,2,1,0:T(8,128)(2,1)} async-done(((bf16[4,21,16,192]{3,2,1,0:T(8,128)(2,1)}), bf16[4,21,16,192]{3,2,1,0:T(8,128)(2,1)}, u32[]{:S(2)}, u32[]{:S(2)}) %all-to-all-start) | async-done | bytes 516128 | tf_op jit(solution)/shard_map/all_to_all | solution.py:40
  67.2 2.0 %add_bitcast_fusion = f32[84,16,192]{2,0,1:T(8,128)S(1)} fusion(f32[16,192,84]{1,2,0:T(8,128)S(1)} %convolution_bitcast_fusion, f32[16,192,84]{1,2,0:T(8,128)S(1)} %convolution_bitcast_fusion.1, f32[84,4,21,1]{0,2,1,3:T(8,128)S(1)} %reshape.52, bf16[4,21,16,192]{3,2,1,0:T(8,128)(2,1)} %all-to-all-done), kind=kOutput, calls=%fused_computation.15 | convolution fusion | flops 260628480 | bytes 3640896 | tf_op jit(solution)/shard_map/aSp,Spli->ali/dot_general | solution.py:41
  69.2 1.5 %copy.66 = f32[84,16,192]{2,1,0:T(8,128)} copy(f32[84,16,192]{2,0,1:T(8,128)S(1)} %add_bitcast_fusion) | data formatting | bytes 2064384 | tf_op jit(solution)/shard_map/add | solution.py:47
  70.8 3.7 %all-to-all-start.3 = ((f32[84,16,192]{2,1,0:T(8,128)}), f32[84,16,192]{2,1,0:T(8,128)S(1)}, u32[]{:S(2)}, u32[]{:S(2)}) async-start(f32[84,16,192]{2,1,0:T(8,128)} %copy.66), calls=%async_computation.3 | async-start | bytes 2752512 | tf_op jit(solution)/shard_map/all_to_all | solution.py:48
  76.0 2.2 %reshape.62 = bf16[768,768,1]{1,0,2:T(8,128)(2,1)} reshape(bf16[4,192,4,192]{3,2,1,0:T(4,128)(2,1)S(1)} %multiply_bitcast_fusion) | data formatting | bytes 2359296 | tf_op jit(solution)/shard_map/reshape | solution.py:55
  78.2 14.4 %all-to-all-done.3 = f32[84,16,192]{2,1,0:T(8,128)S(1)} async-done(((f32[84,16,192]{2,1,0:T(8,128)}), f32[84,16,192]{2,1,0:T(8,128)S(1)}, u32[]{:S(2)}, u32[]{:S(2)}) %all-to-all-start.3) | async-done | bytes 1032224 | tf_op jit(solution)/shard_map/all_to_all | solution.py:48
  96.4 1.5 %fusion.12 = f32[21,16,768]{2,1,0:T(8,128)} fusion(f32[21,16,768]{2,1,0:T(8,128)S(1)} %copy-done.2, bf16[768,768,1]{1,0,2:T(8,128)(2,1)S(1)} %copy-done, f32[21,16,768]{2,1,0:T(8,128)S(1)} %sub.3), kind=kOutput, calls=%fused_computation.18 | convolution fusion | flops 397135872 | bytes 4276224 | tf_op jit(solution)/shard_map/dot_general | solution.py:56
  (53 shorter events, 11.9 us)
Async XLA Ops:
  2.5 5.8 %copy-start.11 = (s32[4,3]{1,0:T(4,128)S(1)}, s32[4,3]{1,0:T(4,128)}, u32[]{:S(2)}) copy-start(s32[4,3]{1,0:T(4,128)} %param.10) | copy-start | bytes 148
  2.7 12.0 %collective-permute-start = (bf16[21,16,2,192]{3,1,2,0:T(8,128)(2,1)S(1)}, bf16[21,16,2,192]{3,1,2,0:T(8,128)(2,1)S(1)}, u32[]{:S(2)}, u32[]{:S(2)}) collective-permute-start(bf16[21,16,2,192]{3,1,2,0:T(8,128)(2,1)S(1)} %get-tuple-element.5), channel_id=1, source_target_pairs={{0,4},{4,8},{8,12},{12,16},{16,20},{20,24},{24,28},{28,32},{32,36}... | collective-permute-start | bytes 774152 | tf_op jit(solution)/shard_map/ppermute | solution.py:19
  4.6 10.1 %collective-permute-start.1 = (bf16[21,16,2,192]{3,1,2,0:T(8,128)(2,1)S(1)}, bf16[21,16,2,192]{3,1,2,0:T(8,128)(2,1)S(1)}, u32[]{:S(2)}, u32[]{:S(2)}) collective-permute-start(bf16[21,16,2,192]{3,1,2,0:T(8,128)(2,1)S(1)} %get-tuple-element.6), channel_id=1, source_target_pairs={{4,0},{8,4},{12,8},{16,12},{20,16},{24,20},{28,24},{32,28},{36,32}... | collective-permute-start | bytes 774152 | tf_op jit(solution)/shard_map/ppermute | solution.py:20
  15.7 1.6 %copy-start.7 = (bf16[4,3,192,192]{3,2,0,1:T(8,128)(2,1)S(1)}, bf16[4,3,192,192]{3,2,0,1:T(8,128)(2,1)}, u32[]{:S(2)}) copy-start(bf16[4,3,192,192]{3,2,0,1:T(8,128)(2,1)} %reshape_squeeze.10) | copy-start | bytes 2654212
  16.0 1.3 %copy-start.6 = (bf16[21,16,4,3,192]{4,1,0,3,2:T(8,128)(2,1)}, bf16[21,16,4,3,192]{4,1,0,3,2:T(8,128)(2,1)S(1)}, u32[]{:S(2)}) copy-start(bf16[21,16,4,3,192]{4,1,0,3,2:T(8,128)(2,1)S(1)} %select_bitcast_fusion) | copy-start | bytes 4644868
  18.1 5.6 %copy-start.4 = (bf16[1,4,3,36864]{3,1,2,0:T(4,128)(2,1)S(1)}, bf16[1,4,3,36864]{3,1,2,0:T(4,128)(2,1)}, u32[]{:S(2)}) copy-start(bf16[1,4,3,36864]{3,1,2,0:T(4,128)(2,1)} %get-tuple-element.3) | copy-start | bytes 2654212
  19.4 15.9 %all-to-all-start.1 = ((bf16[4,21,16,192]{3,2,1,0:T(8,128)(2,1)}), bf16[4,21,16,192]{3,2,1,0:T(8,128)(2,1)S(1)}, u32[]{:S(2)}, u32[]{:S(2)}) async-start(bf16[4,21,16,192]{3,2,1,0:T(8,128)(2,1)} %copy.58), calls=%async_computation.1 | async-start | bytes 1376256 | tf_op jit(solution)/shard_map/all_to_all | solution.py:40
  27.5 11.3 %copy-start.3 = (bf16[1,4,3,36864]{3,1,2,0:T(4,128)(2,1)S(1)}, bf16[1,4,3,36864]{3,1,2,0:T(4,128)(2,1)}, u32[]{:S(2)}) copy-start(bf16[1,4,3,36864]{3,1,2,0:T(4,128)(2,1)} %get-tuple-element.2) | copy-start | bytes 2654212
  35.3 16.0 %all-to-all-start.2 = ((bf16[4,21,16,192]{3,2,1,0:T(8,128)(2,1)}), bf16[4,21,16,192]{3,2,1,0:T(8,128)(2,1)S(1)}, u32[]{:S(2)}, u32[]{:S(2)}) async-start(bf16[4,21,16,192]{3,2,1,0:T(8,128)(2,1)} %copy.63), calls=%async_computation.2 | async-start | bytes 1376256 | tf_op jit(solution)/shard_map/all_to_all | solution.py:40
  44.0 11.7 %copy-start.10 = (f32[3,84,84]{2,1,0:T(8,128)S(1)}, f32[3,84,84]{2,1,0:T(8,128)}, u32[]{:S(2)}) copy-start(f32[3,84,84]{2,1,0:T(8,128)} %param.11) | copy-start | bytes 254020
  51.3 4.7 %copy-start.5 = (bf16[4,21,16,192]{3,2,1,0:T(8,128)(2,1)}, bf16[4,21,16,192]{3,2,1,0:T(8,128)(2,1)S(1)}, u32[]{:S(2)}) copy-start(bf16[4,21,16,192]{3,2,1,0:T(8,128)(2,1)S(1)} %all-to-all-done.2) | copy-start | bytes 1548292
  51.3 15.9 %all-to-all-start = ((bf16[4,21,16,192]{3,2,1,0:T(8,128)(2,1)}), bf16[4,21,16,192]{3,2,1,0:T(8,128)(2,1)}, u32[]{:S(2)}, u32[]{:S(2)}) async-start(bf16[4,21,16,192]{3,2,1,0:T(8,128)(2,1)} %copy.53), calls=%async_computation | async-start | bytes 1376256 | tf_op jit(solution)/shard_map/all_to_all | solution.py:40
  70.8 3.7 %copy-start.9 = (bf16[4,36864]{1,0:T(4,128)(2,1)S(1)}, bf16[4,36864]{1,0:T(4,128)(2,1)}, u32[]{:S(2)}) copy-start(bf16[4,36864]{1,0:T(4,128)(2,1)} %param.9) | copy-start | bytes 884740
  70.8 21.8 %all-to-all-start.3 = ((f32[84,16,192]{2,1,0:T(8,128)}), f32[84,16,192]{2,1,0:T(8,128)S(1)}, u32[]{:S(2)}, u32[]{:S(2)}) async-start(f32[84,16,192]{2,1,0:T(8,128)} %copy.66), calls=%async_computation.3 | async-start | bytes 2752512 | tf_op jit(solution)/shard_map/all_to_all | solution.py:48
  93.6 1.2 %copy-start.8 = (f32[21,16,768]{2,1,0:T(8,128)S(1)}, f32[21,16,768]{2,1,0:T(8,128)}, u32[]{:S(2)}) copy-start(f32[21,16,768]{2,1,0:T(8,128)} %param.7) | copy-start | bytes 3096580
  94.8 1.3 %copy-start = (bf16[768,768,1]{1,0,2:T(8,128)(2,1)S(1)}, bf16[768,768,1]{1,0,2:T(8,128)(2,1)}, u32[]{:S(2)}) copy-start(bf16[768,768,1]{1,0,2:T(8,128)(2,1)} %reshape.62) | copy-start | bytes 3538948
  94.8 1.6 %copy-start.2 = (f32[21,16,768]{2,1,0:T(8,128)S(1)}, f32[21,16,768]{2,1,0:T(8,128)}, u32[]{:S(2)}) copy-start(f32[21,16,768]{2,1,0:T(8,128)} %param.6) | copy-start | bytes 3096580
  96.4 1.5 %copy-start.1 = (f32[21,16,768]{2,1,0:T(8,128)}, f32[21,16,768]{2,1,0:T(8,128)S(1)}, u32[]{:S(2)}) copy-start(f32[21,16,768]{2,1,0:T(8,128)S(1)} %sub.3) | copy-start | bytes 3096580

commit v5 on v0

--- a/solution.py
+++ b/solution.py
@@ -49,9 +49,11 @@
     applied = lax.all_to_all(mixture, "mode", split_axis=0, concat_axis=2, tiled=True)
     applied = applied.reshape(modes_here, loads, dofs_here)
     residual = forcing - applied
-    rounded_res = residual.astype(jnp.bfloat16).reshape(modes_here, loads, block_count, block_size)
+    rounded_res = residual.astype(jnp.bfloat16).reshape(modes_here * loads, dofs_here)
     inverse = inverse_blocks.reshape(block_count, block_size, block_size)
-    update = jnp.einsum("jim,pljm->plji", inverse, rounded_res, preferred_element_type=jnp.float32)
+    diagonal = jnp.eye(block_count, dtype=inverse.dtype)
+    spread = jnp.einsum("rim,rs->rmsi", inverse, diagonal).reshape(dofs_here, dofs_here)
+    update = jnp.dot(rounded_res, spread, preferred_element_type=jnp.float32)
     updated = iterate + RELAXATION * update.reshape(modes_here, loads, dofs_here)
     return (updated, residual)
 

time: 89.8 us -> 85.5 us (0.952)
  waiting for transfers between devices: 19.1 us -> 15.9 us
  other arithmetic: 6.38 us -> 4.01 us
  matrix products: 6.89 us -> 8.05 us
    all_to_all x1, waiting for transfers between devices: 19 us -> 15.9 us  [body(): lax.all_to_all(mixture, 'mode', split_axis=0, concat_axis=2, tiled=True)]
    convert_element_type x1 -> x0, other arithmetic: 2.42 us -> none  [body(): residual.astype(jnp.bfloat16)]
    add x1 -> x0, other arithmetic: 2.37 us -> none  [body(): iterate + RELAXATION * update.reshape(modes_here, loads, dofs_here)]
    mul x2 -> x0, local copies, waits for them, and re-layouts: 1.96 us -> none  [body(): RELAXATION * update.reshape(modes_here, loads, dofs_here)]
    reshape x1, local copies, waits for them, and re-layouts: 0.59 us -> 2.25 us  [body(): jnp.einsum('rim,rs->rmsi', inverse, diagonal).reshape(dofs_here, dofs_here)]
    sub x0 -> x1, other arithmetic: none -> 1.56 us  [body(): residual = forcing - applied]
    dot_general x1, matrix products: 0.37 us -> 1.54 us  [body(): update = jnp.dot(rounded_res, spread, preferred_element_type=jnp.float32)]
  transfers between devices with their start and end apart: 3 -> 3, of which waited for: 1 -> 1; matrix products, arithmetic and copies ran while one was open for 8% -> 12% of each run, Pallas kernels for 0% -> 0%
where the time goes in v5:
time: 85.5 us; the launch traced here: 84.8 us
  blocking collectives  30.7 us (36%)
  local copies, waits for them, and re-layouts  16.1 us (19%)
  waiting for transfers between devices  15.9 us (19%)
  starting transfers between devices  9.24 us (11%)
  matrix products  8.05 us (9%)
  other arithmetic  4.01 us (5%)
    all_to_all x1, blocking collectives, body(): lax.all_to_all(products, 'mode', split_axis=3, concat_axis=1, tiled=True)  30.7 us
    all_to_all x1, waiting for transfers between devices, body(): lax.all_to_all(mixture, 'mode', split_axis=0, concat_axis=2, tiled=True)  15.9 us
    reshape x1, local copies, waits for them, and re-layouts, stiffness(): tile_rows.reshape(tile_rows.shape[0], tile_rows.shape[1], tile_rows.shape...  6.47 us
    dot_general x1, matrix products, stiffness(): jnp.einsum('krsim,plrsm->kplri', shaped, picked, preferred_element_type=j...  4.42 us
    all_to_all x1, starting transfers between devices, body(): lax.all_to_all(mixture, 'mode', split_axis=0, concat_axis=2, tiled=True)  3.68 us
    ppermute x1, starting transfers between devices, padded(): after = lax.ppermute(initial, axis, down)  3.64 us
    reshape x1, local copies, waits for them, and re-layouts, body(): jnp.einsum('rim,rs->rmsi', inverse, diagonal).reshape(dofs_here, dofs_here)  2.25 us
    gather x1, local copies, waits for them, and re-layouts, stiffness(): picked = jnp.take(extended, column_rows, axis=2)  2.11 us
  transfers between devices with their start and end apart: 3, of which 1 were waited for; matrix products, arithmetic and copies ran while one was open for 12% of the time, Pallas kernels for 0%

profile of v5, /device:TPU:56, one launch (start us, length us, event | category | flops | bytes accessed | tf_op | source)
XLA Modules:
  0.0 84.8 jit_solution(719896355104333143)
XLA Ops:
  0.6 1.3 %convert_element_type.14 = bf16[21,16,768]{2,1,0:T(8,128)(2,1)S(1)} convert(f32[21,16,768]{2,1,0:T(8,128)} %param.6) | non-fusion elementwise | flops 258048 | bytes 1548288 | tf_op jit(solution)/shard_map/convert_element_type | solution.py:38
  2.0 0.6 reshape.34
  2.6 0.1 copy.26
  2.7 1.9 %collective-permute-start = (bf16[21,16,2,192]{3,1,2,0:T(8,128)(2,1)S(1)}, bf16[21,16,2,192]{3,1,2,0:T(8,128)(2,1)S(1)}, u32[]{:S(2)}, u32[]{:S(2)}) collective-permute-start(bf16[21,16,2,192]{3,1,2,0:T(8,128)(2,1)S(1)} %get-tuple-element.2), channel_id=1, source_target_pairs={{0,4},{4,8},{8,12},{12,16},{16,20},{20,24},{24,28},{28,32},{32,36}... | collective-permute-start | bytes 774152 | tf_op jit(solution)/shard_map/ppermute | solution.py:19
  4.7 3.6 %collective-permute-start.1 = (bf16[21,16,2,192]{3,1,2,0:T(8,128)(2,1)S(1)}, bf16[21,16,2,192]{3,1,2,0:T(8,128)(2,1)S(1)}, u32[]{:S(2)}, u32[]{:S(2)}) collective-permute-start(bf16[21,16,2,192]{3,1,2,0:T(8,128)(2,1)S(1)} %get-tuple-element.3), channel_id=1, source_target_pairs={{4,0},{8,4},{12,8},{16,12},{20,16},{24,20},{28,24},{32,28},{36,32}... | collective-permute-start | bytes 774152 | tf_op jit(solution)/shard_map/ppermute | solution.py:20
  8.3 0.1 reshape.42
  8.4 6.5 %reshape.35 = bf16[3,4,3,192,192]{4,3,1,2,0:T(8,128)(2,1)} reshape(bf16[3,4,3,36864]{3,1,2,0:T(4,128)(2,1)} %param.8) | data formatting | bytes 5308416 | tf_op jit(solution)/shard_map/reshape | solution.py:28
  14.9 0.3 pad_maximum_fusion
  15.2 2.1 %gather_fusion = bf16[12,21,16,192]{3,2,1,0:T(8,128)(2,1)} fusion(bf16[21,16,8,192]{3,1,2,0:T(8,128)(2,1)S(1)} %pad_maximum_fusion, s32[1024]{0:T(1024)S(1)} %pad_clamp_fusion), kind=kCustom, calls=%fused_computation | custom fusion | bytes 3096624 | tf_op jit(solution)/shard_map/jit(_take)/gather | solution.py:27
  17.3 4.4 %fusion.4 = bf16[3,21,16,4,192]{4,2,0,1,3:T(8,128)(2,1)S(1)} fusion(bf16[3,4,3,192,192]{4,3,1,2,0:T(8,128)(2,1)} %reshape.35, bf16[4,3,21,16,192]{4,3,2,1,0:T(8,128)(2,1)} %bitcast.45, pred[4,3]{1,0:T(4,128)(4,1)S(1)} %compare_and_fusion), kind=kOutput, calls=%fused_computation.6 | convolution fusion | flops 893362176 | bytes 5750796 | tf_op jit(solution)/shard_map/krsim,plrsm->kplri/dot_general | solution.py:31
  21.7 30.7 %all_to_all.30 = bf16[3,21,16,4,192]{4,2,0,1,3:T(8,128)(2,1)S(1)} all-to-all(bf16[3,21,16,4,192]{4,2,0,1,3:T(8,128)(2,1)S(1)} %fusion.4), channel_id=1, replica_groups=mesh['space'=128,'mode'=4] {'mode'}, dimensions={3} | all-to-all | bytes 3096576 | tf_op jit(solution)/shard_map/all_to_all | solution.py:44
  52.4 2.1 %fusion.10 = f32[84,16,1,192]{3,0,1,2:T(8,128)S(1)} fusion(bf16[3,84,16,192]{3,2,0,1:T(8,128)(2,1)S(1)} %bitcast.43, f32[3,84,84]{2,1,0:T(8,128)S(1)} %copy-done), kind=kOutput, calls=%fused_computation.10 | convolution fusion | flops 780337152 | bytes 2665152 | tf_op jit(solution)/shard_map/kab,kblqn->alqn/dot_general | solution.py:41
  54.5 1.5 %copy.32 = f32[84,16,1,192]{3,1,2,0:T(8,128)} copy(f32[84,16,1,192]{3,0,1,2:T(8,128)S(1)} %fusion.10) | data formatting | bytes 2064384 | tf_op jit(solution)/shard_map/kab,kblqn->alqn/dot_general | solution.py:41
  56.0 3.7 %all-to-all-start.1 = ((f32[84,16,1,192]{3,1,2,0:T(8,128)}), f32[84,16,1,192]{3,1,2,0:T(8,128)S(1)}, u32[]{:S(2)}, u32[]{:S(2)}) async-start(f32[84,16,1,192]{3,1,2,0:T(8,128)} %copy.32), calls=%async_computation.1 | async-start | bytes 2752512 | tf_op jit(solution)/shard_map/all_to_all | solution.py:49
  59.7 0.4 reshape.38
  60.2 0.2 copy.34
  60.4 0.8 %multiply_bitcast_fusion = bf16[4,192,4,192]{3,2,1,0:T(4,128)(2,1)S(1)} fusion(bf16[4,192,192]{1,2,0:T(8,128)(2,1)S(1)} %copy.34, bf16[4,4]{1,0:T(4,128)(2,1)S(1)} %fusion.16), kind=kLoop, calls=%fused_computation.9 | loop fusion | flops 589824 | bytes 1474592 | tf_op jit(solution)/shard_map/rim,rs->rmsi/transpose | solution.py:55
  61.2 2.2 %reshape.55 = bf16[768,768,1]{1,0,2:T(8,128)(2,1)} reshape(bf16[4,192,4,192]{3,2,1,0:T(4,128)(2,1)S(1)} %multiply_bitcast_fusion) | data formatting | bytes 2359296 | tf_op jit(solution)/shard_map/reshape | solution.py:55
  63.5 15.9 %all-to-all-done.1 = f32[84,16,1,192]{3,1,2,0:T(8,128)S(1)} async-done(((f32[84,16,1,192]{3,1,2,0:T(8,128)}), f32[84,16,1,192]{3,1,2,0:T(8,128)S(1)}, u32[]{:S(2)}, u32[]{:S(2)}) %all-to-all-start.1) | async-done | bytes 1032224 | tf_op jit(solution)/shard_map/all_to_all | solution.py:49
  79.4 1.0 %copy.33 = f32[21,16,4,1,192]{4,2,1,0,3:T(4,128)S(1)} copy(f32[21,16,4,1,192]{4,1,0,2,3:T(8,128)S(1)} %bitcast.44) | data formatting | bytes 2064384 | tf_op jit(solution)/shard_map/all_to_all | solution.py:49
  80.4 0.9 %reshape.37 = f32[21,16,768]{2,1,0:T(8,128)S(1)} reshape(f32[21,16,4,1,192]{4,2,1,0,3:T(4,128)S(1)} %copy.33) | data formatting | bytes 2064384 | tf_op jit(solution)/shard_map/reshape | solution.py:50
  81.4 1.6 %sub.3 = f32[21,16,768]{2,1,0:T(8,128)S(1)} subtract(f32[21,16,768]{2,1,0:T(8,128)} %param.7, f32[21,16,768]{2,1,0:T(8,128)S(1)} %reshape.37) | non-fusion elementwise | flops 258048 | bytes 3096576 | tf_op jit(solution)/shard_map/sub | solution.py:51
  82.9 0.3 copy-done.3
  83.2 1.5 %fusion.13 = f32[21,16,768]{2,1,0:T(8,128)} fusion(f32[21,16,768]{2,1,0:T(8,128)S(1)} %copy-done.3, bf16[768,768,1]{1,0,2:T(8,128)(2,1)S(1)} %copy-done.1, f32[21,16,768]{2,1,0:T(8,128)S(1)} %sub.3), kind=kOutput, calls=%fused_computation.13 | convolution fusion | flops 397135872 | bytes 4276224 | tf_op jit(solution)/shard_map/dot_general | solution.py:56
  (18 shorter events, 0.1 us)
Async XLA Ops:
  0.6 51.8 %copy-start = (f32[3,84,84]{2,1,0:T(8,128)S(1)}, f32[3,84,84]{2,1,0:T(8,128)}, u32[]{:S(2)}) copy-start(f32[3,84,84]{2,1,0:T(8,128)} %param.11) | copy-start | bytes 254020
  2.0 6.4 %copy-start.5 = (s32[4,3]{1,0:T(4,128)S(1)}, s32[4,3]{1,0:T(4,128)}, u32[]{:S(2)}) copy-start(s32[4,3]{1,0:T(4,128)} %param.10) | copy-start | bytes 148
  2.7 12.2 %collective-permute-start = (bf16[21,16,2,192]{3,1,2,0:T(8,128)(2,1)S(1)}, bf16[21,16,2,192]{3,1,2,0:T(8,128)(2,1)S(1)}, u32[]{:S(2)}, u32[]{:S(2)}) collective-permute-start(bf16[21,16,2,192]{3,1,2,0:T(8,128)(2,1)S(1)} %get-tuple-element.2), channel_id=1, source_target_pairs={{0,4},{4,8},{8,12},{12,16},{16,20},{20,24},{24,28},{28,32},{32,36}... | collective-permute-start | bytes 774152 | tf_op jit(solution)/shard_map/ppermute | solution.py:19
  4.7 10.2 %collective-permute-start.1 = (bf16[21,16,2,192]{3,1,2,0:T(8,128)(2,1)S(1)}, bf16[21,16,2,192]{3,1,2,0:T(8,128)(2,1)S(1)}, u32[]{:S(2)}, u32[]{:S(2)}) collective-permute-start(bf16[21,16,2,192]{3,1,2,0:T(8,128)(2,1)S(1)} %get-tuple-element.3), channel_id=1, source_target_pairs={{4,0},{8,4},{12,8},{16,12},{20,16},{24,20},{28,24},{32,28},{36,32}... | collective-permute-start | bytes 774152 | tf_op jit(solution)/shard_map/ppermute | solution.py:20
  56.0 3.7 %copy-start.4 = (bf16[4,36864]{1,0:T(4,128)(2,1)S(1)}, bf16[4,36864]{1,0:T(4,128)(2,1)}, u32[]{:S(2)}) copy-start(bf16[4,36864]{1,0:T(4,128)(2,1)} %param.9) | copy-start | bytes 884740
  56.0 23.3 %all-to-all-start.1 = ((f32[84,16,1,192]{3,1,2,0:T(8,128)}), f32[84,16,1,192]{3,1,2,0:T(8,128)S(1)}, u32[]{:S(2)}, u32[]{:S(2)}) async-start(f32[84,16,1,192]{3,1,2,0:T(8,128)} %copy.32), calls=%async_computation.1 | async-start | bytes 2752512 | tf_op jit(solution)/shard_map/all_to_all | solution.py:49
  81.3 1.6 %copy-start.1 = (bf16[768,768,1]{1,0,2:T(8,128)(2,1)S(1)}, bf16[768,768,1]{1,0,2:T(8,128)(2,1)}, u32[]{:S(2)}) copy-start(bf16[768,768,1]{1,0,2:T(8,128)(2,1)} %reshape.55) | copy-start | bytes 3538948
  81.3 1.9 %copy-start.3 = (f32[21,16,768]{2,1,0:T(8,128)S(1)}, f32[21,16,768]{2,1,0:T(8,128)}, u32[]{:S(2)}) copy-start(f32[21,16,768]{2,1,0:T(8,128)} %param.6) | copy-start | bytes 3096580
  83.2 1.5 %copy-start.2 = (f32[21,16,768]{2,1,0:T(8,128)}, f32[21,16,768]{2,1,0:T(8,128)S(1)}, u32[]{:S(2)}) copy-start(f32[21,16,768]{2,1,0:T(8,128)S(1)} %sub.3) | copy-start | bytes 3096580

commit v6 on v5

--- a/solution.py
+++ b/solution.py
@@ -9,17 +9,21 @@
 RELAXATION = 0.7
 
 
-def padded(x, sides, width):
-    for axis, dim in sides:
-        devices, length = (lax.axis_size(axis), x.shape[dim])
-        up = [(i, (i + 1) % devices) for i in range(devices)]
-        down = [(j, i) for i, j in up]
-        last = lax.slice_in_dim(x, length - width, length, axis=dim)
-        initial = lax.slice_in_dim(x, 0, width, axis=dim)
-        before = lax.ppermute(last, axis, up)
-        after = lax.ppermute(initial, axis, down)
-        x = jnp.concatenate([before, x, after], axis=dim)
-    return x
+def halos(x, dim, width):
+    lo = lax.axis_index("s_lo")
+    length = x.shape[dim]
+    last = lax.slice_in_dim(x, length - width, length, axis=dim)
+    initial = lax.slice_in_dim(x, 0, width, axis=dim)
+    inside = lax.ppermute(jnp.where(lo == 0, last, initial), "s_lo", [(0, 1), (1, 0)])
+    chips = lax.axis_size("s_hi")
+    pairs = []
+    for c in range(chips):
+        a, b = 2 * c + 1, 2 * ((c + 1) % chips)
+        pairs += [(a, b), (b, a)]
+    across = lax.ppermute(jnp.where(lo == 1, last, initial), ("s_hi", "s_lo"), pairs)
+    before = jnp.where(lo == 0, across, inside)
+    after = jnp.where(lo == 0, inside, across)
+    return jnp.concatenate([before, x, after], axis=dim)
 
 
 def stiffness(extended, tile_rows, column_rows):
@@ -36,7 +40,7 @@
     terms, block_count = (tiles.shape[0], tiles.shape[1])
     block_size = dofs_here // block_count
     rounded = iterate.astype(jnp.bfloat16).reshape(modes_here, loads, block_count, block_size)
-    extended = padded(rounded, (("space", 2),), H)
+    extended = halos(rounded, 2, H)
     products = stiffness(extended, tiles, columns).astype(jnp.bfloat16)
     mixture = jnp.einsum(
         "kab,kblqn->alqn",
@@ -59,17 +63,21 @@
 
 
 def solution(mesh):
+    space = mesh.shape["space"]
+    pairs = jax.sharding.Mesh(
+        mesh.devices.reshape(space // 2, 2, mesh.shape["mode"]), ("s_hi", "s_lo", "mode")
+    )
     return jax.shard_map(
         body,
-        mesh=mesh,
+        mesh=pairs,
         in_specs=(
-            P("mode", None, "space"),
-            P("mode", None, "space"),
-            P(None, "space", None, None),
-            P("space", None),
-            P("space", None),
+            P("mode", None, ("s_hi", "s_lo")),
+            P("mode", None, ("s_hi", "s_lo")),
+            P(None, ("s_hi", "s_lo"), None, None),
+            P(("s_hi", "s_lo"), None),
+            P(("s_hi", "s_lo"), None),
             P(),
         ),
-        out_specs=(P("mode", None, "space"), P("mode", None, "space")),
+        out_specs=(P("mode", None, ("s_hi", "s_lo")), P("mode", None, ("s_hi", "s_lo"))),
         check_vma=False,
     )

time: 85.5 us -> 93.2 us (1.090)
  the two profiles are of different devices: /device:TPU:56 before, /device:TPU:1 now
where the time goes in v6:
time: 93.2 us; the launch traced here: 92.7 us
  blocking collectives  29.6 us (32%)
  starting transfers between devices  20.6 us (22%)
  local copies, waits for them, and re-layouts  16 us (17%)
  waiting for transfers between devices  13.5 us (14%)
  matrix products  8.05 us (9%)
  other arithmetic  4.11 us (4%)
    all_to_all x1, blocking collectives, body(): lax.all_to_all(products, 'mode', split_axis=3, concat_axis=1, tiled=True)  29.6 us
    all_to_all x1, waiting for transfers between devices, body(): lax.all_to_all(mixture, 'mode', split_axis=0, concat_axis=2, tiled=True)  13.5 us
    ppermute x1, starting transfers between devices, halos(): lax.ppermute(jnp.where(lo == 0, last, initial), 's_lo', [(0, 1), (1, 0)])  12.1 us
    reshape x1, local copies, waits for them, and re-layouts, stiffness(): tile_rows.reshape(tile_rows.shape[0], tile_rows.shape[1], tile_rows.shape...  6.47 us
    ppermute x1, starting transfers between devices, halos(): lax.ppermute(jnp.where(lo == 1, last, initial), ('s_hi', 's_lo'), pairs)  4.59 us
    dot_general x1, matrix products, stiffness(): jnp.einsum('krsim,plrsm->kplri', shaped, picked, preferred_element_type=j...  4.43 us
    all_to_all x1, starting transfers between devices, body(): lax.all_to_all(mixture, 'mode', split_axis=0, concat_axis=2, tiled=True)  3.86 us
    reshape x1, local copies, waits for them, and re-layouts, body(): jnp.einsum('rim,rs->rmsi', inverse, diagonal).reshape(dofs_here, dofs_here)  2.24 us
  transfers between devices with their start and end apart: 3, of which 1 were waited for; matrix products, arithmetic and copies ran while one was open for 11% of the time, Pallas kernels for 0%

profile of v6, /device:TPU:1, one launch (start us, length us, event | category | flops | bytes accessed | tf_op | source)
XLA Modules:
  0.0 92.7 jit_solution(14749228892628590403)
XLA Ops:
  0.6 1.3 %convert_element_type.14 = bf16[21,16,768]{2,1,0:T(8,128)(2,1)S(1)} convert(f32[21,16,768]{2,1,0:T(8,128)} %param.6) | non-fusion elementwise | flops 258048 | bytes 1548288 | tf_op jit(solution)/shard_map/convert_element_type | solution.py:42
  2.0 0.6 reshape.34
  2.6 0.1 copy.26
  2.8 4.6 %collective-permute-start = (bf16[21,16,2,192]{3,1,2,0:T(8,128)(2,1)S(1)}, bf16[21,16,2,192]{3,1,2,0:T(8,128)(2,1)S(1)}, u32[]{:S(2)}, u32[]{:S(2)}) collective-permute-start(bf16[21,16,2,192]{3,1,2,0:T(8,128)(2,1)S(1)} %get-tuple-element.4), channel_id=1, source_target_pairs={{4,8},{8,4},{12,16},{16,12},{20,24},{24,20},{28,32},{32,28},{36,40... | collective-permute-start | bytes 774152 | tf_op jit(solution)/shard_map/ppermute | solution.py:23
  7.4 12.1 %collective-permute-start.1 = (bf16[21,16,2,192]{3,1,2,0:T(8,128)(2,1)S(1)}, bf16[21,16,2,192]{3,1,2,0:T(8,128)(2,1)S(1)}, u32[]{:S(2)}, u32[]{:S(2)}) collective-permute-start(bf16[21,16,2,192]{3,1,2,0:T(8,128)(2,1)S(1)} %get-tuple-element.5), channel_id=1, source_target_pairs={{0,4},{4,0},{1,5},{5,1},{2,6},{6,2},{3,7},{7,3},{8,12},{12,8},{9,1... | collective-permute-start | bytes 774152 | tf_op jit(solution)/shard_map/ppermute | solution.py:17
  19.5 0.1 reshape.42
  19.6 6.5 %reshape.35 = bf16[3,4,3,192,192]{4,3,1,2,0:T(8,128)(2,1)} reshape(bf16[3,4,3,36864]{3,1,2,0:T(4,128)(2,1)} %param.8) | data formatting | bytes 5308416 | tf_op jit(solution)/shard_map/reshape | solution.py:32
  26.1 0.3 pad_maximum_fusion
  26.4 2.1 %gather_fusion = bf16[12,21,16,192]{3,2,1,0:T(8,128)(2,1)} fusion(bf16[21,16,8,192]{3,1,2,0:T(8,128)(2,1)S(1)} %pad_maximum_fusion, s32[1024]{0:T(1024)S(1)} %pad_clamp_fusion), kind=kCustom, calls=%fused_computation | custom fusion | bytes 3096624 | tf_op jit(solution)/shard_map/jit(_take)/gather | solution.py:31
  28.5 4.4 %fusion.4 = bf16[3,21,16,4,192]{4,2,0,1,3:T(8,128)(2,1)S(1)} fusion(bf16[3,4,3,192,192]{4,3,1,2,0:T(8,128)(2,1)} %reshape.35, bf16[4,3,21,16,192]{4,3,2,1,0:T(8,128)(2,1)} %bitcast.45, pred[4,3]{1,0:T(4,128)(4,1)S(1)} %compare_and_fusion), kind=kOutput, calls=%fused_computation.6 | convolution fusion | flops 893362176 | bytes 5750796 | tf_op jit(solution)/shard_map/krsim,plrsm->kplri/dot_general | solution.py:35
  32.9 29.6 %all_to_all.30 = bf16[3,21,16,4,192]{4,2,0,1,3:T(8,128)(2,1)S(1)} all-to-all(bf16[3,21,16,4,192]{4,2,0,1,3:T(8,128)(2,1)S(1)} %fusion.4), channel_id=1, replica_groups=mesh['s_hi'=64,'s_lo'=2,'mode'=4] {'mode'}, dimensions={3} | all-to-all | bytes 3096576 | tf_op jit(solution)/shard_map/all_to_all | solution.py:48
  62.6 2.1 %fusion.10 = f32[84,16,1,192]{3,0,1,2:T(8,128)S(1)} fusion(bf16[3,84,16,192]{3,2,0,1:T(8,128)(2,1)S(1)} %bitcast.43, f32[3,84,84]{2,1,0:T(8,128)S(1)} %copy-done), kind=kOutput, calls=%fused_computation.10 | convolution fusion | flops 780337152 | bytes 2665152 | tf_op jit(solution)/shard_map/kab,kblqn->alqn/dot_general | solution.py:45
  64.7 1.5 %copy.32 = f32[84,16,1,192]{3,1,2,0:T(8,128)} copy(f32[84,16,1,192]{3,0,1,2:T(8,128)S(1)} %fusion.10) | data formatting | bytes 2064384 | tf_op jit(solution)/shard_map/kab,kblqn->alqn/dot_general | solution.py:45
  66.2 3.9 %all-to-all-start.1 = ((f32[84,16,1,192]{3,1,2,0:T(8,128)}), f32[84,16,1,192]{3,1,2,0:T(8,128)S(1)}, u32[]{:S(2)}, u32[]{:S(2)}) async-start(f32[84,16,1,192]{3,1,2,0:T(8,128)} %copy.32), calls=%async_computation.1 | async-start | bytes 2752512 | tf_op jit(solution)/shard_map/all_to_all | solution.py:53
  70.1 0.4 reshape.38
  70.5 0.2 copy.34
  70.7 0.8 multiply_bitcast_fusion
  71.6 2.2 %reshape.55 = bf16[768,768,1]{1,0,2:T(8,128)(2,1)} reshape(bf16[4,192,4,192]{3,2,1,0:T(4,128)(2,1)S(1)} %multiply_bitcast_fusion) | data formatting | bytes 2359296 | tf_op jit(solution)/shard_map/reshape | solution.py:59
  73.8 13.5 %all-to-all-done.1 = f32[84,16,1,192]{3,1,2,0:T(8,128)S(1)} async-done(((f32[84,16,1,192]{3,1,2,0:T(8,128)}), f32[84,16,1,192]{3,1,2,0:T(8,128)S(1)}, u32[]{:S(2)}, u32[]{:S(2)}) %all-to-all-start.1) | async-done | bytes 1032224 | tf_op jit(solution)/shard_map/all_to_all | solution.py:53
  87.3 1.0 %copy.33 = f32[21,16,4,1,192]{4,2,1,0,3:T(4,128)S(1)} copy(f32[21,16,4,1,192]{4,1,0,2,3:T(8,128)S(1)} %bitcast.44) | data formatting | bytes 2064384 | tf_op jit(solution)/shard_map/all_to_all | solution.py:53
  88.4 0.9 reshape.37
  89.3 1.6 %sub.3 = f32[21,16,768]{2,1,0:T(8,128)S(1)} subtract(f32[21,16,768]{2,1,0:T(8,128)} %param.7, f32[21,16,768]{2,1,0:T(8,128)S(1)} %reshape.37) | non-fusion elementwise | flops 258048 | bytes 3096576 | tf_op jit(solution)/shard_map/sub | solution.py:55
  90.9 0.3 copy-done.3
  91.2 1.5 %fusion.13 = f32[21,16,768]{2,1,0:T(8,128)} fusion(f32[21,16,768]{2,1,0:T(8,128)S(1)} %copy-done.3, bf16[768,768,1]{1,0,2:T(8,128)(2,1)S(1)} %copy-done.1, f32[21,16,768]{2,1,0:T(8,128)S(1)} %sub.3), kind=kOutput, calls=%fused_computation.13 | convolution fusion | flops 397135872 | bytes 4276224 | tf_op jit(solution)/shard_map/dot_general | solution.py:60
  (19 shorter events, 0.2 us)
Async XLA Ops:
  0.6 61.9 %copy-start = (f32[3,84,84]{2,1,0:T(8,128)S(1)}, f32[3,84,84]{2,1,0:T(8,128)}, u32[]{:S(2)}) copy-start(f32[3,84,84]{2,1,0:T(8,128)} %param.11) | copy-start | bytes 254020
  2.0 17.5 %copy-start.5 = (s32[4,3]{1,0:T(4,128)S(1)}, s32[4,3]{1,0:T(4,128)}, u32[]{:S(2)}) copy-start(s32[4,3]{1,0:T(4,128)} %param.10) | copy-start | bytes 148
  2.8 23.3 %collective-permute-start = (bf16[21,16,2,192]{3,1,2,0:T(8,128)(2,1)S(1)}, bf16[21,16,2,192]{3,1,2,0:T(8,128)(2,1)S(1)}, u32[]{:S(2)}, u32[]{:S(2)}) collective-permute-start(bf16[21,16,2,192]{3,1,2,0:T(8,128)(2,1)S(1)} %get-tuple-element.4), channel_id=1, source_target_pairs={{4,8},{8,4},{12,16},{16,12},{20,24},{24,20},{28,32},{32,28},{36,40... | collective-permute-start | bytes 774152 | tf_op jit(solution)/shard_map/ppermute | solution.py:23
  7.4 18.7 %collective-permute-start.1 = (bf16[21,16,2,192]{3,1,2,0:T(8,128)(2,1)S(1)}, bf16[21,16,2,192]{3,1,2,0:T(8,128)(2,1)S(1)}, u32[]{:S(2)}, u32[]{:S(2)}) collective-permute-start(bf16[21,16,2,192]{3,1,2,0:T(8,128)(2,1)S(1)} %get-tuple-element.5), channel_id=1, source_target_pairs={{0,4},{4,0},{1,5},{5,1},{2,6},{6,2},{3,7},{7,3},{8,12},{12,8},{9,1... | collective-permute-start | bytes 774152 | tf_op jit(solution)/shard_map/ppermute | solution.py:17
  66.2 3.9 %copy-start.4 = (bf16[4,36864]{1,0:T(4,128)(2,1)S(1)}, bf16[4,36864]{1,0:T(4,128)(2,1)}, u32[]{:S(2)}) copy-start(bf16[4,36864]{1,0:T(4,128)(2,1)} %param.9) | copy-start | bytes 884740
  66.2 21.2 %all-to-all-start.1 = ((f32[84,16,1,192]{3,1,2,0:T(8,128)}), f32[84,16,1,192]{3,1,2,0:T(8,128)S(1)}, u32[]{:S(2)}, u32[]{:S(2)}) async-start(f32[84,16,1,192]{3,1,2,0:T(8,128)} %copy.32), calls=%async_computation.1 | async-start | bytes 2752512 | tf_op jit(solution)/shard_map/all_to_all | solution.py:53
  89.3 1.6 %copy-start.1 = (bf16[768,768,1]{1,0,2:T(8,128)(2,1)S(1)}, bf16[768,768,1]{1,0,2:T(8,128)(2,1)}, u32[]{:S(2)}) copy-start(bf16[768,768,1]{1,0,2:T(8,128)(2,1)} %reshape.55) | copy-start | bytes 3538948
  89.3 1.9 %copy-start.3 = (f32[21,16,768]{2,1,0:T(8,128)S(1)}, f32[21,16,768]{2,1,0:T(8,128)}, u32[]{:S(2)}) copy-start(f32[21,16,768]{2,1,0:T(8,128)} %param.6) | copy-start | bytes 3096580
  91.2 1.5 %copy-start.2 = (f32[21,16,768]{2,1,0:T(8,128)}, f32[21,16,768]{2,1,0:T(8,128)S(1)}, u32[]{:S(2)}) copy-start(f32[21,16,768]{2,1,0:T(8,128)S(1)} %sub.3) | copy-start | bytes 3096580

commit v7 on v5

--- a/solution.py
+++ b/solution.py
@@ -9,13 +9,16 @@
 RELAXATION = 0.7
 
 
-def padded(x, sides, width):
+def padded(x, sides, width, source):
     for axis, dim in sides:
         devices, length = (lax.axis_size(axis), x.shape[dim])
         up = [(i, (i + 1) % devices) for i in range(devices)]
         down = [(j, i) for i, j in up]
-        last = lax.slice_in_dim(x, length - width, length, axis=dim)
-        initial = lax.slice_in_dim(x, 0, width, axis=dim)
+        dofs = source.shape[-1]
+        edge = width * x.shape[-1]
+        shape = x.shape[:dim] + (width,) + x.shape[dim + 1:]
+        last = source[..., dofs - edge:].astype(x.dtype).reshape(shape)
+        initial = source[..., :edge].astype(x.dtype).reshape(shape)
         before = lax.ppermute(last, axis, up)
         after = lax.ppermute(initial, axis, down)
         x = jnp.concatenate([before, x, after], axis=dim)
@@ -36,15 +39,16 @@
     terms, block_count = (tiles.shape[0], tiles.shape[1])
     block_size = dofs_here // block_count
     rounded = iterate.astype(jnp.bfloat16).reshape(modes_here, loads, block_count, block_size)
-    extended = padded(rounded, (("space", 2),), H)
+    extended = padded(rounded, (("space", 2),), H, iterate)
     products = stiffness(extended, tiles, columns).astype(jnp.bfloat16)
-    mixture = jnp.einsum(
-        "kab,kblqn->alqn",
-        coupling,
-        lax.all_to_all(products, "mode", split_axis=3, concat_axis=1, tiled=True).astype(
-            jnp.float32
-        ),
-        precision=lax.Precision.HIGHEST,
+    exchanged = lax.all_to_all(products, "mode", split_axis=3, concat_axis=1, tiled=True)
+    high = coupling.astype(jnp.bfloat16)
+    rest = coupling - high.astype(jnp.float32)
+    middle = rest.astype(jnp.bfloat16)
+    low = (rest - middle.astype(jnp.float32)).astype(jnp.bfloat16)
+    mixture = sum(
+        jnp.einsum("kab,kblqn->alqn", piece, exchanged, preferred_element_type=jnp.float32)
+        for piece in (high, middle, low)
     )
     applied = lax.all_to_all(mixture, "mode", split_axis=0, concat_axis=2, tiled=True)
     applied = applied.reshape(modes_here, loads, dofs_here)

time: 85.5 us -> 86.6 us (1.013)
  waiting for transfers between devices: 15.9 us -> 14.5 us
  other arithmetic: 4.01 us -> 4.98 us
    dot_general x1 -> x0, local copies, waits for them, and re-layouts: 1.52 us -> none  [body(): jnp.einsum('kab,kblqn->alqn', coupling, lax.all_to_all(products, 'mode',...]
    add x0 -> x1, local copies, waits for them, and re-layouts: none -> 1.51 us  [body(): sum((jnp.einsum('kab,kblqn->alqn', piece, exchanged, preferred_element_ty...]
    gather x1, local copies, waits for them, and re-layouts: 2.11 us -> 0.69 us  [stiffness(): picked = jnp.take(extended, column_rows, axis=2)]
    all_to_all x1, waiting for transfers between devices: 15.9 us -> 14.5 us  [body(): lax.all_to_all(mixture, 'mode', split_axis=0, concat_axis=2, tiled=True)]
    convert_element_type x1 -> x0, other arithmetic: 1.31 us -> none  [body(): iterate.astype(jnp.bfloat16)]
    another operation x1 -> x2, other arithmetic: 0.01 us -> 1.28 us
    concatenate x1, other arithmetic: 0.26 us -> 1.35 us  [padded(): x = jnp.concatenate([before, x, after], axis=dim)]
    dot_general x1 -> x3, matrix products: 2.1 us -> 2.92 us  [body(): jnp.einsum('kab,kblqn->alqn', piece, exchanged, preferred_element_type=jn...]
  transfers between devices with their start and end apart: 3 -> 3, of which waited for: 1 -> 1; matrix products, arithmetic and copies ran while one was open for 12% -> 13% of each run, Pallas kernels for 0% -> 0%
where the time goes in v7:
time: 86.6 us; the launch traced here: 85.1 us
  blocking collectives  31.1 us (36%)
  local copies, waits for them, and re-layouts  15.9 us (18%)
  waiting for transfers between devices  14.5 us (17%)
  starting transfers between devices  9.42 us (11%)
  matrix products  8.25 us (10%)
  other arithmetic  4.98 us (6%)
    all_to_all x1, blocking collectives, body(): lax.all_to_all(products, 'mode', split_axis=3, concat_axis=1, tiled=True)  31.1 us
    all_to_all x1, waiting for transfers between devices, body(): lax.all_to_all(mixture, 'mode', split_axis=0, concat_axis=2, tiled=True)  14.5 us
    reshape x1, local copies, waits for them, and re-layouts, stiffness(): tile_rows.reshape(tile_rows.shape[0], tile_rows.shape[1], tile_rows.shape...  6.47 us
    all_to_all x1, starting transfers between devices, body(): lax.all_to_all(mixture, 'mode', split_axis=0, concat_axis=2, tiled=True)  3.86 us
    dot_general x1, matrix products, stiffness(): jnp.einsum('krsim,plrsm->kplri', shaped, picked, preferred_element_type=j...  3.8 us
    ppermute x1, starting transfers between devices, padded(): after = lax.ppermute(initial, axis, down)  3.64 us
    dot_general x3, matrix products, body(): jnp.einsum('kab,kblqn->alqn', piece, exchanged, preferred_element_type=jn...  2.92 us
    reshape x1, local copies, waits for them, and re-layouts, body(): jnp.einsum('rim,rs->rmsi', inverse, diagonal).reshape(dofs_here, dofs_here)  2.24 us
  transfers between devices with their start and end apart: 3, of which 1 were waited for; matrix products, arithmetic and copies ran while one was open for 13% of the time, Pallas kernels for 0%

profile of v7, /device:TPU:56, one launch (start us, length us, event | category | flops | bytes accessed | tf_op | source)
XLA Modules:
  0.0 85.1 jit_solution(261036168853865078)
XLA Ops:
  0.6 1.3 %convert.7 = bf16[21,16,768]{2,1,0:T(8,128)(2,1)S(1)} convert(f32[21,16,768]{2,1,0:T(8,128)} %param.6) | non-fusion elementwise | flops 258048 | bytes 1548288 | tf_op jit(solution)/shard_map/convert.2
  2.2 1.9 %collective-permute-start = (bf16[21,16,2,192]{3,1,2,0:T(8,128)(2,1)S(1)}, bf16[21,16,2,192]{3,1,2,0:T(8,128)(2,1)S(1)}, u32[]{:S(2)}, u32[]{:S(2)}) collective-permute-start(bf16[21,16,2,192]{3,1,2,0:T(8,128)(2,1)S(1)} %copy.32), channel_id=1, source_target_pairs={{0,4},{4,8},{8,12},{12,16},{16,20},{20,24},{24,28},{28,32},{32,36}... | collective-permute-start | bytes 774152 | tf_op jit(solution)/shard_map/ppermute | solution.py:22
  4.4 3.6 %collective-permute-start.1 = (bf16[21,16,2,192]{3,1,2,0:T(8,128)(2,1)S(1)}, bf16[21,16,2,192]{3,1,2,0:T(8,128)(2,1)}, u32[]{:S(2)}, u32[]{:S(2)}) collective-permute-start(bf16[21,16,2,192]{3,1,2,0:T(8,128)(2,1)S(1)} %copy.33), channel_id=1, source_target_pairs={{4,0},{8,4},{12,8},{16,12},{20,16},{24,20},{28,24},{32,28},{36,32}... | collective-permute-start | bytes 774152 | tf_op jit(solution)/shard_map/ppermute | solution.py:23
  8.2 0.6 reshape.49
  8.9 6.5 %reshape.51 = bf16[3,4,3,192,192]{4,3,1,2,0:T(8,128)(2,1)} reshape(bf16[3,4,3,36864]{3,1,2,0:T(4,128)(2,1)} %param.8) | data formatting | bytes 5308416 | tf_op jit(solution)/shard_map/reshape | solution.py:31
  15.4 0.7 copy-done.4
  16.1 1.3 %pad_maximum_fusion = bf16[21,16,8,192]{3,1,2,0:T(8,128)(2,1)S(1)} fusion(bf16[21,16,2,192]{3,1,2,0:T(8,128)(2,1)} %collective-permute-done.1, bf16[21,16,4,192]{3,1,2,0:T(8,128)(2,1)S(1)} %copy.34, bf16[21,16,2,192]{3,1,2,0:T(8,128)(2,1)} %copy-done.4), kind=kLoop, calls=%fused_computation.18 | loop fusion | flops 1032192 | bytes 2064384 | tf_op jit(solution)/shard_map/concatenate | solution.py:24
  17.5 0.7 gather_fusion
  18.2 3.8 %fusion.2 = bf16[3,21,16,4,192]{4,2,0,1,3:T(8,128)(2,1)S(1)} fusion(bf16[3,4,3,192,192]{4,3,1,2,0:T(8,128)(2,1)} %reshape.51, bf16[4,3,21,16,192]{4,3,2,1,0:T(8,128)(2,1)S(1)} %bitcast.61, pred[4,3]{1,0:T(4,128)(4,1)S(1)} %compare_and_fusion), kind=kOutput, calls=%fused_computation.4 | convolution fusion | flops 893362176 | bytes 5750796 | tf_op jit(solution)/shard_map/krsim,plrsm->kplri/dot_general | solution.py:34
  22.0 31.1 %all_to_all.30 = bf16[3,21,16,4,192]{4,2,0,1,3:T(8,128)(2,1)S(1)} all-to-all(bf16[3,21,16,4,192]{4,2,0,1,3:T(8,128)(2,1)S(1)} %fusion.2), channel_id=1, replica_groups=mesh['space'=128,'mode'=4] {'mode'}, dimensions={3} | all-to-all | bytes 3096576 | tf_op jit(solution)/shard_map/all_to_all | solution.py:44
  53.1 1.0 %fusion.14 = f32[84,16,192]{2,0,1:T(8,128)S(1)} fusion(bf16[3,84,16,192]{3,2,0,1:T(8,128)(2,1)S(1)} %bitcast.57, f32[3,84,84]{2,1,0:T(8,128)S(1)} %copy-done.3), kind=kOutput, calls=%fused_computation.14 | convolution fusion | flops 130077360 | bytes 2665152 | tf_op jit(solution)/shard_map/kab,kblqn->alqn/dot_general | solution.py:50
  54.1 0.9 %fusion.17 = f32[84,16,192]{2,0,1:T(8,128)S(1)} fusion(bf16[3,84,16,192]{3,2,0,1:T(8,128)(2,1)S(1)} %bitcast.58, f32[3,84,84]{2,1,0:T(8,128)S(1)} %copy-done.3), kind=kOutput, calls=%fused_computation.15 | convolution fusion | flops 130140864 | bytes 2665152 | tf_op jit(solution)/shard_map/kab,kblqn->alqn/dot_general | solution.py:50
  55.0 1.1 %add_bitcast_fusion = f32[84,16,1,192]{3,0,1,2:T(8,128)S(1)} fusion(f32[84,16,192]{2,0,1:T(8,128)S(1)} %fusion.14, f32[84,16,192]{2,0,1:T(8,128)S(1)} %fusion.17, bf16[3,84,16,192]{3,2,0,1:T(8,128)(2,1)S(1)} %bitcast.59, f32[3,84,84]{2,1,0:T(8,128)S(1)} %copy-done.3), kind=kOutput, calls=%fused_computation.17 | convolution fusion | flops 130720464 | bytes 4729536 | tf_op jit(solution)/shard_map/kab,kblqn->alqn/dot_general | solution.py:50
  56.1 1.5 %copy.40 = f32[84,16,1,192]{3,1,2,0:T(8,128)} copy(f32[84,16,1,192]{3,0,1,2:T(8,128)S(1)} %add_bitcast_fusion) | data formatting | bytes 2064384 | tf_op jit(solution)/shard_map/add | solution.py:49
  57.6 3.9 %all-to-all-start.1 = ((f32[84,16,1,192]{3,1,2,0:T(8,128)}), f32[84,16,1,192]{3,1,2,0:T(8,128)S(1)}, u32[]{:S(2)}, u32[]{:S(2)}) async-start(f32[84,16,1,192]{3,1,2,0:T(8,128)} %copy.40), calls=%async_computation.1 | async-start | bytes 2752512 | tf_op jit(solution)/shard_map/all_to_all | solution.py:53
  61.5 0.4 reshape.54
  62.1 0.8 multiply_bitcast_fusion
  63.0 2.2 %reshape.75 = bf16[768,768,1]{1,0,2:T(8,128)(2,1)} reshape(bf16[4,192,4,192]{3,2,1,0:T(4,128)(2,1)S(1)} %multiply_bitcast_fusion) | data formatting | bytes 2359296 | tf_op jit(solution)/shard_map/reshape | solution.py:59
  65.2 14.5 %all-to-all-done.1 = f32[84,16,1,192]{3,1,2,0:T(8,128)S(1)} async-done(((f32[84,16,1,192]{3,1,2,0:T(8,128)}), f32[84,16,1,192]{3,1,2,0:T(8,128)S(1)}, u32[]{:S(2)}, u32[]{:S(2)}) %all-to-all-start.1) | async-done | bytes 1032224 | tf_op jit(solution)/shard_map/all_to_all | solution.py:53
  79.8 1.0 %copy.41 = f32[21,16,4,1,192]{4,2,1,0,3:T(4,128)S(1)} copy(f32[21,16,4,1,192]{4,1,0,2,3:T(8,128)S(1)} %bitcast.60) | data formatting | bytes 2064384 | tf_op jit(solution)/shard_map/all_to_all | solution.py:53
  80.8 0.9 %reshape.53 = f32[21,16,768]{2,1,0:T(8,128)S(1)} reshape(f32[21,16,4,1,192]{4,2,1,0,3:T(4,128)S(1)} %copy.41) | data formatting | bytes 2064384 | tf_op jit(solution)/shard_map/reshape | solution.py:54
  81.7 1.5 %sub.11 = f32[21,16,768]{2,1,0:T(8,128)S(1)} subtract(f32[21,16,768]{2,1,0:T(8,128)} %param.7, f32[21,16,768]{2,1,0:T(8,128)S(1)} %reshape.53) | non-fusion elementwise | flops 258048 | bytes 3096576 | tf_op jit(solution)/shard_map/sub | solution.py:55
  83.3 0.3 copy-done.2
  83.6 1.5 %fusion.25 = f32[21,16,768]{2,1,0:T(8,128)} fusion(f32[21,16,768]{2,1,0:T(8,128)S(1)} %copy-done.2, bf16[768,768,1]{1,0,2:T(8,128)(2,1)S(1)} %copy-done, f32[21,16,768]{2,1,0:T(8,128)S(1)} %sub.11), kind=kOutput, calls=%fused_computation.20 | convolution fusion | flops 397135872 | bytes 4276224 | tf_op jit(solution)/shard_map/dot_general | solution.py:60
  (26 shorter events, 1.1 us)
Async XLA Ops:
  1.9 6.2 %copy-start.6 = (s32[4,3]{1,0:T(4,128)S(1)}, s32[4,3]{1,0:T(4,128)}, u32[]{:S(2)}) copy-start(s32[4,3]{1,0:T(4,128)} %param.10) | copy-start | bytes 148
  2.2 13.2 %collective-permute-start = (bf16[21,16,2,192]{3,1,2,0:T(8,128)(2,1)S(1)}, bf16[21,16,2,192]{3,1,2,0:T(8,128)(2,1)S(1)}, u32[]{:S(2)}, u32[]{:S(2)}) collective-permute-start(bf16[21,16,2,192]{3,1,2,0:T(8,128)(2,1)S(1)} %copy.32), channel_id=1, source_target_pairs={{0,4},{4,8},{8,12},{12,16},{16,20},{20,24},{24,28},{28,32},{32,36}... | collective-permute-start | bytes 774152 | tf_op jit(solution)/shard_map/ppermute | solution.py:22
  4.4 11.7 %collective-permute-start.1 = (bf16[21,16,2,192]{3,1,2,0:T(8,128)(2,1)S(1)}, bf16[21,16,2,192]{3,1,2,0:T(8,128)(2,1)}, u32[]{:S(2)}, u32[]{:S(2)}) collective-permute-start(bf16[21,16,2,192]{3,1,2,0:T(8,128)(2,1)S(1)} %copy.33), channel_id=1, source_target_pairs={{4,0},{8,4},{12,8},{16,12},{20,16},{24,20},{28,24},{32,28},{36,32}... | collective-permute-start | bytes 774152 | tf_op jit(solution)/shard_map/ppermute | solution.py:23
  15.4 0.7 copy-start.4
  22.0 31.1 %copy-start.3 = (f32[3,84,84]{2,1,0:T(8,128)S(1)}, f32[3,84,84]{2,1,0:T(8,128)}, u32[]{:S(2)}) copy-start(f32[3,84,84]{2,1,0:T(8,128)} %param.11) | copy-start | bytes 254020
  57.6 3.9 %copy-start.5 = (bf16[4,36864]{1,0:T(4,128)(2,1)S(1)}, bf16[4,36864]{1,0:T(4,128)(2,1)}, u32[]{:S(2)}) copy-start(bf16[4,36864]{1,0:T(4,128)(2,1)} %param.9) | copy-start | bytes 884740
  57.6 22.2 %all-to-all-start.1 = ((f32[84,16,1,192]{3,1,2,0:T(8,128)}), f32[84,16,1,192]{3,1,2,0:T(8,128)S(1)}, u32[]{:S(2)}, u32[]{:S(2)}) async-start(f32[84,16,1,192]{3,1,2,0:T(8,128)} %copy.40), calls=%async_computation.1 | async-start | bytes 2752512 | tf_op jit(solution)/shard_map/all_to_all | solution.py:53
  81.7 1.6 %copy-start = (bf16[768,768,1]{1,0,2:T(8,128)(2,1)S(1)}, bf16[768,768,1]{1,0,2:T(8,128)(2,1)}, u32[]{:S(2)}) copy-start(bf16[768,768,1]{1,0,2:T(8,128)(2,1)} %reshape.75) | copy-start | bytes 3538948
  81.7 1.9 %copy-start.2 = (f32[21,16,768]{2,1,0:T(8,128)S(1)}, f32[21,16,768]{2,1,0:T(8,128)}, u32[]{:S(2)}) copy-start(f32[21,16,768]{2,1,0:T(8,128)} %param.6) | copy-start | bytes 3096580
  83.6 1.5 %copy-start.1 = (f32[21,16,768]{2,1,0:T(8,128)}, f32[21,16,768]{2,1,0:T(8,128)S(1)}, u32[]{:S(2)}) copy-start(f32[21,16,768]{2,1,0:T(8,128)S(1)} %sub.11) | copy-start | bytes 3096580

commit v8 on v7

--- a/solution.py
+++ b/solution.py
@@ -42,12 +42,17 @@
     extended = padded(rounded, (("space", 2),), H, iterate)
     products = stiffness(extended, tiles, columns).astype(jnp.bfloat16)
     exchanged = lax.all_to_all(products, "mode", split_axis=3, concat_axis=1, tiled=True)
-    high = coupling.astype(jnp.bfloat16)
-    rest = coupling - high.astype(jnp.float32)
-    middle = rest.astype(jnp.bfloat16)
-    low = (rest - middle.astype(jnp.float32)).astype(jnp.bfloat16)
+    high = lax.reduce_precision(coupling, exponent_bits=8, mantissa_bits=7)
+    rest = coupling - high
+    middle = lax.reduce_precision(rest, exponent_bits=8, mantissa_bits=7)
+    low = rest - middle
     mixture = sum(
-        jnp.einsum("kab,kblqn->alqn", piece, exchanged, preferred_element_type=jnp.float32)
+        jnp.einsum(
+            "kab,kblqn->alqn",
+            piece.astype(jnp.bfloat16),
+            exchanged,
+            preferred_element_type=jnp.float32,
+        )
         for piece in (high, middle, low)
     )
     applied = lax.all_to_all(mixture, "mode", split_axis=0, concat_axis=2, tiled=True)

time: 86.6 us -> 86.6 us (level)
  no operation moved by 1% of the time
where the time goes in v8:
time: 86.6 us; the launch traced here: 85.1 us
  blocking collectives  31.1 us (36%)
  local copies, waits for them, and re-layouts  16 us (18%)
  waiting for transfers between devices  14.6 us (17%)
  starting transfers between devices  9.42 us (11%)
  matrix products  8.23 us (10%)
  other arithmetic  4.98 us (6%)
    all_to_all x1, blocking collectives, body(): lax.all_to_all(products, 'mode', split_axis=3, concat_axis=1, tiled=True)  31.1 us
    all_to_all x1, waiting for transfers between devices, body(): lax.all_to_all(mixture, 'mode', split_axis=0, concat_axis=2, tiled=True)  14.6 us
    reshape x1, local copies, waits for them, and re-layouts, stiffness(): tile_rows.reshape(tile_rows.shape[0], tile_rows.shape[1], tile_rows.shape...  6.47 us
    all_to_all x1, starting transfers between devices, body(): lax.all_to_all(mixture, 'mode', split_axis=0, concat_axis=2, tiled=True)  3.86 us
    dot_general x1, matrix products, stiffness(): jnp.einsum('krsim,plrsm->kplri', shaped, picked, preferred_element_type=j...  3.8 us
    ppermute x1, starting transfers between devices, padded(): after = lax.ppermute(initial, axis, down)  3.64 us
    dot_general x3, matrix products, body(): jnp.einsum('kab,kblqn->alqn', piece.astype(jnp.bfloat16), exchanged, pref...  2.89 us
    reshape x1, local copies, waits for them, and re-layouts, body(): jnp.einsum('rim,rs->rmsi', inverse, diagonal).reshape(dofs_here, dofs_here)  2.24 us
  transfers between devices with their start and end apart: 3, of which 1 were waited for; matrix products, arithmetic and copies ran while one was open for 13% of the time, Pallas kernels for 0%

profile of v8, /device:TPU:56, one launch (start us, length us, event | category | flops | bytes accessed | tf_op | source)
XLA Modules:
  0.0 85.1 jit_solution(4552873512842816534)
XLA Ops:
  0.6 1.3 %convert.7 = bf16[21,16,768]{2,1,0:T(8,128)(2,1)S(1)} convert(f32[21,16,768]{2,1,0:T(8,128)} %param.6) | non-fusion elementwise | flops 258048 | bytes 1548288 | tf_op jit(solution)/shard_map/convert.2
  2.2 1.9 %collective-permute-start = (bf16[21,16,2,192]{3,1,2,0:T(8,128)(2,1)S(1)}, bf16[21,16,2,192]{3,1,2,0:T(8,128)(2,1)S(1)}, u32[]{:S(2)}, u32[]{:S(2)}) collective-permute-start(bf16[21,16,2,192]{3,1,2,0:T(8,128)(2,1)S(1)} %copy.32), channel_id=1, source_target_pairs={{0,4},{4,8},{8,12},{12,16},{16,20},{20,24},{24,28},{28,32},{32,36}... | collective-permute-start | bytes 774152 | tf_op jit(solution)/shard_map/ppermute | solution.py:22
  4.4 3.6 %collective-permute-start.1 = (bf16[21,16,2,192]{3,1,2,0:T(8,128)(2,1)S(1)}, bf16[21,16,2,192]{3,1,2,0:T(8,128)(2,1)}, u32[]{:S(2)}, u32[]{:S(2)}) collective-permute-start(bf16[21,16,2,192]{3,1,2,0:T(8,128)(2,1)S(1)} %copy.33), channel_id=1, source_target_pairs={{4,0},{8,4},{12,8},{16,12},{20,16},{24,20},{28,24},{32,28},{36,32}... | collective-permute-start | bytes 774152 | tf_op jit(solution)/shard_map/ppermute | solution.py:23
  8.2 0.6 reshape.49
  8.9 6.5 %reshape.51 = bf16[3,4,3,192,192]{4,3,1,2,0:T(8,128)(2,1)} reshape(bf16[3,4,3,36864]{3,1,2,0:T(4,128)(2,1)} %param.8) | data formatting | bytes 5308416 | tf_op jit(solution)/shard_map/reshape | solution.py:31
  15.4 0.7 copy-done.4
  16.1 1.3 %pad_maximum_fusion = bf16[21,16,8,192]{3,1,2,0:T(8,128)(2,1)S(1)} fusion(bf16[21,16,2,192]{3,1,2,0:T(8,128)(2,1)} %collective-permute-done.1, bf16[21,16,4,192]{3,1,2,0:T(8,128)(2,1)S(1)} %copy.34, bf16[21,16,2,192]{3,1,2,0:T(8,128)(2,1)} %copy-done.4), kind=kLoop, calls=%fused_computation.18 | loop fusion | flops 1032192 | bytes 2064384 | tf_op jit(solution)/shard_map/concatenate | solution.py:24
  17.5 0.7 gather_fusion
  18.2 3.8 %fusion.2 = bf16[3,21,16,4,192]{4,2,0,1,3:T(8,128)(2,1)S(1)} fusion(bf16[3,4,3,192,192]{4,3,1,2,0:T(8,128)(2,1)} %reshape.51, bf16[4,3,21,16,192]{4,3,2,1,0:T(8,128)(2,1)S(1)} %bitcast.61, pred[4,3]{1,0:T(4,128)(4,1)S(1)} %compare_and_fusion), kind=kOutput, calls=%fused_computation.4 | convolution fusion | flops 893362176 | bytes 5750796 | tf_op jit(solution)/shard_map/krsim,plrsm->kplri/dot_general | solution.py:34
  22.0 31.1 %all_to_all.30 = bf16[3,21,16,4,192]{4,2,0,1,3:T(8,128)(2,1)S(1)} all-to-all(bf16[3,21,16,4,192]{4,2,0,1,3:T(8,128)(2,1)S(1)} %fusion.2), channel_id=1, replica_groups=mesh['space'=128,'mode'=4] {'mode'}, dimensions={3} | all-to-all | bytes 3096576 | tf_op jit(solution)/shard_map/all_to_all | solution.py:44
  53.1 1.0 %fusion.14 = f32[84,16,192]{2,0,1:T(8,128)S(1)} fusion(bf16[3,84,16,192]{3,2,0,1:T(8,128)(2,1)S(1)} %bitcast.57, f32[3,84,84]{2,1,0:T(8,128)S(1)} %copy-done.3), kind=kOutput, calls=%fused_computation.14 | convolution fusion | flops 130098528 | bytes 2665152 | tf_op jit(solution)/shard_map/kab,kblqn->alqn/dot_general | solution.py:50
  54.1 0.9 %fusion.17 = f32[84,16,192]{2,0,1:T(8,128)S(1)} fusion(bf16[3,84,16,192]{3,2,0,1:T(8,128)(2,1)S(1)} %bitcast.58, f32[3,84,84]{2,1,0:T(8,128)S(1)} %copy-done.3), kind=kOutput, calls=%fused_computation.15 | convolution fusion | flops 130140864 | bytes 2665152 | tf_op jit(solution)/shard_map/kab,kblqn->alqn/dot_general | solution.py:50
  55.0 1.0 %add_bitcast_fusion = f32[84,16,1,192]{3,0,1,2:T(8,128)S(1)} fusion(f32[84,16,192]{2,0,1:T(8,128)S(1)} %fusion.14, f32[84,16,192]{2,0,1:T(8,128)S(1)} %fusion.17, bf16[3,84,16,192]{3,2,0,1:T(8,128)(2,1)S(1)} %bitcast.59, f32[3,84,84]{2,1,0:T(8,128)S(1)} %copy-done.3), kind=kOutput, calls=%fused_computation.17 | convolution fusion | flops 130678128 | bytes 4729536 | tf_op jit(solution)/shard_map/kab,kblqn->alqn/dot_general | solution.py:50
  56.1 1.5 %copy.40 = f32[84,16,1,192]{3,1,2,0:T(8,128)} copy(f32[84,16,1,192]{3,0,1,2:T(8,128)S(1)} %add_bitcast_fusion) | data formatting | bytes 2064384 | tf_op jit(solution)/shard_map/add | solution.py:49
  57.6 3.9 %all-to-all-start.1 = ((f32[84,16,1,192]{3,1,2,0:T(8,128)}), f32[84,16,1,192]{3,1,2,0:T(8,128)S(1)}, u32[]{:S(2)}, u32[]{:S(2)}) async-start(f32[84,16,1,192]{3,1,2,0:T(8,128)} %copy.40), calls=%async_computation.1 | async-start | bytes 2752512 | tf_op jit(solution)/shard_map/all_to_all | solution.py:58
  61.4 0.4 reshape.54
  62.1 0.8 multiply_bitcast_fusion
  63.0 2.2 %reshape.75 = bf16[768,768,1]{1,0,2:T(8,128)(2,1)} reshape(bf16[4,192,4,192]{3,2,1,0:T(4,128)(2,1)S(1)} %multiply_bitcast_fusion) | data formatting | bytes 2359296 | tf_op jit(solution)/shard_map/reshape | solution.py:64
  65.2 14.6 %all-to-all-done.1 = f32[84,16,1,192]{3,1,2,0:T(8,128)S(1)} async-done(((f32[84,16,1,192]{3,1,2,0:T(8,128)}), f32[84,16,1,192]{3,1,2,0:T(8,128)S(1)}, u32[]{:S(2)}, u32[]{:S(2)}) %all-to-all-start.1) | async-done | bytes 1032224 | tf_op jit(solution)/shard_map/all_to_all | solution.py:58
  79.7 1.0 %copy.41 = f32[21,16,4,1,192]{4,2,1,0,3:T(4,128)S(1)} copy(f32[21,16,4,1,192]{4,1,0,2,3:T(8,128)S(1)} %bitcast.60) | data formatting | bytes 2064384 | tf_op jit(solution)/shard_map/all_to_all | solution.py:58
  80.8 0.9 %reshape.53 = f32[21,16,768]{2,1,0:T(8,128)S(1)} reshape(f32[21,16,4,1,192]{4,2,1,0,3:T(4,128)S(1)} %copy.41) | data formatting | bytes 2064384 | tf_op jit(solution)/shard_map/reshape | solution.py:59
  81.7 1.5 %sub.11 = f32[21,16,768]{2,1,0:T(8,128)S(1)} subtract(f32[21,16,768]{2,1,0:T(8,128)} %param.7, f32[21,16,768]{2,1,0:T(8,128)S(1)} %reshape.53) | non-fusion elementwise | flops 258048 | bytes 3096576 | tf_op jit(solution)/shard_map/sub | solution.py:60
  83.3 0.3 copy-done.2
  83.6 1.5 %fusion.25 = f32[21,16,768]{2,1,0:T(8,128)} fusion(f32[21,16,768]{2,1,0:T(8,128)S(1)} %copy-done.2, bf16[768,768,1]{1,0,2:T(8,128)(2,1)S(1)} %copy-done, f32[21,16,768]{2,1,0:T(8,128)S(1)} %sub.11), kind=kOutput, calls=%fused_computation.20 | convolution fusion | flops 397135872 | bytes 4276224 | tf_op jit(solution)/shard_map/dot_general | solution.py:65
  (26 shorter events, 1.1 us)
Async XLA Ops:
  1.9 6.2 %copy-start.6 = (s32[4,3]{1,0:T(4,128)S(1)}, s32[4,3]{1,0:T(4,128)}, u32[]{:S(2)}) copy-start(s32[4,3]{1,0:T(4,128)} %param.10) | copy-start | bytes 148
  2.2 13.2 %collective-permute-start = (bf16[21,16,2,192]{3,1,2,0:T(8,128)(2,1)S(1)}, bf16[21,16,2,192]{3,1,2,0:T(8,128)(2,1)S(1)}, u32[]{:S(2)}, u32[]{:S(2)}) collective-permute-start(bf16[21,16,2,192]{3,1,2,0:T(8,128)(2,1)S(1)} %copy.32), channel_id=1, source_target_pairs={{0,4},{4,8},{8,12},{12,16},{16,20},{20,24},{24,28},{28,32},{32,36}... | collective-permute-start | bytes 774152 | tf_op jit(solution)/shard_map/ppermute | solution.py:22
  4.4 11.7 %collective-permute-start.1 = (bf16[21,16,2,192]{3,1,2,0:T(8,128)(2,1)S(1)}, bf16[21,16,2,192]{3,1,2,0:T(8,128)(2,1)}, u32[]{:S(2)}, u32[]{:S(2)}) collective-permute-start(bf16[21,16,2,192]{3,1,2,0:T(8,128)(2,1)S(1)} %copy.33), channel_id=1, source_target_pairs={{4,0},{8,4},{12,8},{16,12},{20,16},{24,20},{28,24},{32,28},{36,32}... | collective-permute-start | bytes 774152 | tf_op jit(solution)/shard_map/ppermute | solution.py:23
  15.4 0.7 copy-start.4
  22.0 31.1 %copy-start.3 = (f32[3,84,84]{2,1,0:T(8,128)S(1)}, f32[3,84,84]{2,1,0:T(8,128)}, u32[]{:S(2)}) copy-start(f32[3,84,84]{2,1,0:T(8,128)} %param.11) | copy-start | bytes 254020
  57.6 3.9 %copy-start.5 = (bf16[4,36864]{1,0:T(4,128)(2,1)S(1)}, bf16[4,36864]{1,0:T(4,128)(2,1)}, u32[]{:S(2)}) copy-start(bf16[4,36864]{1,0:T(4,128)(2,1)} %param.9) | copy-start | bytes 884740
  57.6 22.2 %all-to-all-start.1 = ((f32[84,16,1,192]{3,1,2,0:T(8,128)}), f32[84,16,1,192]{3,1,2,0:T(8,128)S(1)}, u32[]{:S(2)}, u32[]{:S(2)}) async-start(f32[84,16,1,192]{3,1,2,0:T(8,128)} %copy.40), calls=%async_computation.1 | async-start | bytes 2752512 | tf_op jit(solution)/shard_map/all_to_all | solution.py:58
  81.7 1.6 %copy-start = (bf16[768,768,1]{1,0,2:T(8,128)(2,1)S(1)}, bf16[768,768,1]{1,0,2:T(8,128)(2,1)}, u32[]{:S(2)}) copy-start(bf16[768,768,1]{1,0,2:T(8,128)(2,1)} %reshape.75) | copy-start | bytes 3538948
  81.7 1.9 %copy-start.2 = (f32[21,16,768]{2,1,0:T(8,128)S(1)}, f32[21,16,768]{2,1,0:T(8,128)}, u32[]{:S(2)}) copy-start(f32[21,16,768]{2,1,0:T(8,128)} %param.6) | copy-start | bytes 3096580
  83.6 1.5 %copy-start.1 = (f32[21,16,768]{2,1,0:T(8,128)}, f32[21,16,768]{2,1,0:T(8,128)S(1)}, u32[]{:S(2)}) copy-start(f32[21,16,768]{2,1,0:T(8,128)S(1)} %sub.11) | copy-start | bytes 3096580

commit v9 on v5

--- a/solution.py
+++ b/solution.py
@@ -9,7 +9,7 @@
 RELAXATION = 0.7
 
 
-def padded(x, sides, width):
+def padded(x, sides, width, cover):
     for axis, dim in sides:
         devices, length = (lax.axis_size(axis), x.shape[dim])
         up = [(i, (i + 1) % devices) for i in range(devices)]
@@ -17,17 +17,15 @@
         last = lax.slice_in_dim(x, length - width, length, axis=dim)
         initial = lax.slice_in_dim(x, 0, width, axis=dim)
         before = lax.ppermute(last, axis, up)
+        before, initial = lax.optimization_barrier((before, initial))
+        initial, covered = lax.optimization_barrier((initial, cover(before)))
         after = lax.ppermute(initial, axis, down)
         x = jnp.concatenate([before, x, after], axis=dim)
-    return x
+    return x, covered
 
 
-def stiffness(extended, tile_rows, column_rows):
-    block_size = extended.shape[-1]
+def stiffness(extended, shaped, column_rows):
     picked = jnp.take(extended, column_rows, axis=2)
-    shaped = tile_rows.reshape(
-        tile_rows.shape[0], tile_rows.shape[1], tile_rows.shape[2], block_size, block_size
-    )
     return jnp.einsum("krsim,plrsm->kplri", shaped, picked, preferred_element_type=jnp.float32)
 
 
@@ -36,8 +34,15 @@
     terms, block_count = (tiles.shape[0], tiles.shape[1])
     block_size = dofs_here // block_count
     rounded = iterate.astype(jnp.bfloat16).reshape(modes_here, loads, block_count, block_size)
-    extended = padded(rounded, (("space", 2),), H)
-    products = stiffness(extended, tiles, columns).astype(jnp.bfloat16)
+    extended, shaped = padded(
+        rounded,
+        (("space", 2),),
+        H,
+        lambda ready: lax.optimization_barrier((ready, tiles))[1].reshape(
+            terms, block_count, tiles.shape[2], block_size, block_size
+        ),
+    )
+    products = stiffness(extended, shaped, columns).astype(jnp.bfloat16)
     mixture = jnp.einsum(
         "kab,kblqn->alqn",
         coupling,

time: 85.5 us -> 95.1 us (1.11)
  the two profiles are of different devices: /device:TPU:56 before, /device:TPU:2 now
where the time goes in v9:
time: 95.1 us; the launch traced here: 94.7 us
  waiting for transfers between devices  30.5 us (32%)
  blocking collectives  26.3 us (28%)
  local copies, waits for them, and re-layouts  16.1 us (17%)
  starting transfers between devices  8.93 us (9%)
  matrix products  8.06 us (8%)
  other arithmetic  4.01 us (4%)
    all_to_all x1, blocking collectives, body(): lax.all_to_all(products, 'mode', split_axis=3, concat_axis=1, tiled=True)  26.3 us
    ppermute x1, waiting for transfers between devices, padded(): before = lax.ppermute(last, axis, up)  16.2 us
    all_to_all x1, waiting for transfers between devices, body(): lax.all_to_all(mixture, 'mode', split_axis=0, concat_axis=2, tiled=True)  9.62 us
    reshape x1, local copies, waits for them, and re-layouts, body(): lax.optimization_barrier((ready, tiles))[1]  6.47 us
    all_to_all x1, starting transfers between devices, body(): lax.all_to_all(mixture, 'mode', split_axis=0, concat_axis=2, tiled=True)  5.11 us
    ppermute x1, waiting for transfers between devices, padded(): after = lax.ppermute(initial, axis, down)  4.72 us
    dot_general x1, matrix products, stiffness(): jnp.einsum('krsim,plrsm->kplri', shaped, picked, preferred_element_type=j...  4.43 us
    reshape x1, local copies, waits for them, and re-layouts, body(): jnp.einsum('rim,rs->rmsi', inverse, diagonal).reshape(dofs_here, dofs_here)  2.25 us
  transfers between devices with their start and end apart: 3, of which 3 were waited for; matrix products, arithmetic and copies ran while one was open for 4% of the time, Pallas kernels for 0%

profile of v9, /device:TPU:2, one launch (start us, length us, event | category | flops | bytes accessed | tf_op | source)
XLA Modules:
  0.0 94.7 jit_solution(1327085672109073817)
XLA Ops:
  0.6 1.3 %convert_element_type.14 = bf16[21,16,768]{2,1,0:T(8,128)(2,1)S(1)} convert(f32[21,16,768]{2,1,0:T(8,128)} %param.6) | non-fusion elementwise | flops 258048 | bytes 1548288 | tf_op jit(solution)/shard_map/convert_element_type | solution.py:36
  2.0 0.6 reshape.34
  2.7 1.9 %collective-permute-start = (bf16[21,16,2,192]{3,1,2,0:T(8,128)(2,1)S(1)}, bf16[21,16,2,192]{3,1,2,0:T(8,128)(2,1)S(1)}, u32[]{:S(2)}, u32[]{:S(2)}) collective-permute-start(bf16[21,16,2,192]{3,1,2,0:T(8,128)(2,1)S(1)} %get-tuple-element.13), channel_id=1, source_target_pairs={{0,4},{4,8},{8,12},{12,16},{16,20},{20,24},{24,28},{28,32},{32,36}... | collective-permute-start | bytes 774152 | tf_op jit(solution)/shard_map/ppermute | solution.py:19
  4.8 16.2 %collective-permute-done = bf16[21,16,2,192]{3,1,2,0:T(8,128)(2,1)S(1)} collective-permute-done((bf16[21,16,2,192]{3,1,2,0:T(8,128)(2,1)S(1)}, bf16[21,16,2,192]{3,1,2,0:T(8,128)(2,1)S(1)}, u32[]{:S(2)}, u32[]{:S(2)}) %collective-permute-start) | collective-permute-done | bytes 258080 | tf_op jit(solution)/shard_map/ppermute | solution.py:19
  21.0 6.5 %reshape.35 = bf16[3,4,3,192,192]{4,3,1,2,0:T(8,128)(2,1)} reshape(bf16[3,4,3,36864]{3,1,2,0:T(4,128)(2,1)} %param.8) | data formatting | bytes 5308416 | tf_op jit(solution)/shard_map/reshape | solution.py:41
  27.4 1.9 %collective-permute-start.1 = (bf16[21,16,2,192]{3,1,2,0:T(8,128)(2,1)S(1)}, bf16[21,16,2,192]{3,1,2,0:T(8,128)(2,1)S(1)}, u32[]{:S(2)}, u32[]{:S(2)}) collective-permute-start(bf16[21,16,2,192]{3,1,2,0:T(8,128)(2,1)S(1)} %get-tuple-element.10), channel_id=1, source_target_pairs={{4,0},{8,4},{12,8},{16,12},{20,16},{24,20},{28,24},{32,28},{36,32}... | collective-permute-start | bytes 774152 | tf_op jit(solution)/shard_map/ppermute | solution.py:22
  29.4 4.7 %collective-permute-done.1 = bf16[21,16,2,192]{3,1,2,0:T(8,128)(2,1)S(1)} collective-permute-done((bf16[21,16,2,192]{3,1,2,0:T(8,128)(2,1)S(1)}, bf16[21,16,2,192]{3,1,2,0:T(8,128)(2,1)S(1)}, u32[]{:S(2)}, u32[]{:S(2)}) %collective-permute-start.1) | collective-permute-done | bytes 258080 | tf_op jit(solution)/shard_map/ppermute | solution.py:22
  34.1 0.3 pad_maximum_fusion
  34.4 2.1 %gather_fusion = bf16[12,21,16,192]{3,2,1,0:T(8,128)(2,1)} fusion(bf16[21,16,8,192]{3,1,2,0:T(8,128)(2,1)S(1)} %pad_maximum_fusion, s32[1024]{0:T(1024)S(1)} %pad_clamp_fusion), kind=kCustom, calls=%fused_computation | custom fusion | bytes 3096624 | tf_op jit(solution)/shard_map/jit(_take)/gather | solution.py:28
  36.5 4.4 %fusion.4 = bf16[3,21,16,4,192]{4,2,0,1,3:T(8,128)(2,1)S(1)} fusion(bf16[3,4,3,192,192]{4,3,1,2,0:T(8,128)(2,1)} %reshape.35, bf16[4,3,21,16,192]{4,3,2,1,0:T(8,128)(2,1)} %bitcast.45, pred[4,3]{1,0:T(4,128)(4,1)S(1)} %compare_and_fusion), kind=kOutput, calls=%fused_computation.6 | convolution fusion | flops 893362176 | bytes 5750796 | tf_op jit(solution)/shard_map/krsim,plrsm->kplri/dot_general | solution.py:29
  40.9 26.3 %all_to_all.30 = bf16[3,21,16,4,192]{4,2,0,1,3:T(8,128)(2,1)S(1)} all-to-all(bf16[3,21,16,4,192]{4,2,0,1,3:T(8,128)(2,1)S(1)} %fusion.4), channel_id=1, replica_groups=mesh['space'=128,'mode'=4] {'mode'}, dimensions={3} | all-to-all | bytes 3096576 | tf_op jit(solution)/shard_map/all_to_all | solution.py:49
  67.2 2.1 %fusion.10 = f32[84,16,1,192]{3,0,1,2:T(8,128)S(1)} fusion(bf16[3,84,16,192]{3,2,0,1:T(8,128)(2,1)S(1)} %bitcast.43, f32[3,84,84]{2,1,0:T(8,128)S(1)} %copy-done), kind=kOutput, calls=%fused_computation.10 | convolution fusion | flops 780337152 | bytes 2665152 | tf_op jit(solution)/shard_map/kab,kblqn->alqn/dot_general | solution.py:46
  69.3 1.5 %copy.32 = f32[84,16,1,192]{3,1,2,0:T(8,128)} copy(f32[84,16,1,192]{3,0,1,2:T(8,128)S(1)} %fusion.10) | data formatting | bytes 2064384 | tf_op jit(solution)/shard_map/kab,kblqn->alqn/dot_general | solution.py:46
  70.8 5.1 %all-to-all-start.1 = ((f32[84,16,1,192]{3,1,2,0:T(8,128)}), f32[84,16,1,192]{3,1,2,0:T(8,128)S(1)}, u32[]{:S(2)}, u32[]{:S(2)}) async-start(f32[84,16,1,192]{3,1,2,0:T(8,128)} %copy.32), calls=%async_computation.1 | async-start | bytes 2752512 | tf_op jit(solution)/shard_map/all_to_all | solution.py:54
  75.9 0.4 reshape.38
  76.4 0.2 copy.34
  76.6 0.8 multiply_bitcast_fusion
  77.5 2.2 %reshape.55 = bf16[768,768,1]{1,0,2:T(8,128)(2,1)} reshape(bf16[4,192,4,192]{3,2,1,0:T(4,128)(2,1)S(1)} %multiply_bitcast_fusion) | data formatting | bytes 2359296 | tf_op jit(solution)/shard_map/reshape | solution.py:60
  79.7 9.6 %all-to-all-done.1 = f32[84,16,1,192]{3,1,2,0:T(8,128)S(1)} async-done(((f32[84,16,1,192]{3,1,2,0:T(8,128)}), f32[84,16,1,192]{3,1,2,0:T(8,128)S(1)}, u32[]{:S(2)}, u32[]{:S(2)}) %all-to-all-start.1) | async-done | bytes 1032224 | tf_op jit(solution)/shard_map/all_to_all | solution.py:54
  89.3 1.0 %copy.33 = f32[21,16,4,1,192]{4,2,1,0,3:T(4,128)S(1)} copy(f32[21,16,4,1,192]{4,1,0,2,3:T(8,128)S(1)} %bitcast.44) | data formatting | bytes 2064384 | tf_op jit(solution)/shard_map/all_to_all | solution.py:54
  90.4 0.9 reshape.37
  91.3 1.6 %sub.3 = f32[21,16,768]{2,1,0:T(8,128)S(1)} subtract(f32[21,16,768]{2,1,0:T(8,128)} %param.7, f32[21,16,768]{2,1,0:T(8,128)S(1)} %reshape.37) | non-fusion elementwise | flops 258048 | bytes 3096576 | tf_op jit(solution)/shard_map/sub | solution.py:56
  92.9 0.3 copy-done.3
  93.2 1.5 %fusion.13 = f32[21,16,768]{2,1,0:T(8,128)} fusion(f32[21,16,768]{2,1,0:T(8,128)S(1)} %copy-done.3, bf16[768,768,1]{1,0,2:T(8,128)(2,1)S(1)} %copy-done.1, f32[21,16,768]{2,1,0:T(8,128)S(1)} %sub.3), kind=kOutput, calls=%fused_computation.13 | convolution fusion | flops 397135872 | bytes 4276224 | tf_op jit(solution)/shard_map/dot_general | solution.py:61
  (18 shorter events, 0.3 us)
Async XLA Ops:
  0.6 66.6 %copy-start = (f32[3,84,84]{2,1,0:T(8,128)S(1)}, f32[3,84,84]{2,1,0:T(8,128)}, u32[]{:S(2)}) copy-start(f32[3,84,84]{2,1,0:T(8,128)} %param.11) | copy-start | bytes 254020
  2.0 2.7 %copy-start.5 = (s32[4,3]{1,0:T(4,128)S(1)}, s32[4,3]{1,0:T(4,128)}, u32[]{:S(2)}) copy-start(s32[4,3]{1,0:T(4,128)} %param.10) | copy-start | bytes 148
  2.7 18.2 %collective-permute-start = (bf16[21,16,2,192]{3,1,2,0:T(8,128)(2,1)S(1)}, bf16[21,16,2,192]{3,1,2,0:T(8,128)(2,1)S(1)}, u32[]{:S(2)}, u32[]{:S(2)}) collective-permute-start(bf16[21,16,2,192]{3,1,2,0:T(8,128)(2,1)S(1)} %get-tuple-element.13), channel_id=1, source_target_pairs={{0,4},{4,8},{8,12},{12,16},{16,20},{20,24},{24,28},{28,32},{32,36}... | collective-permute-start | bytes 774152 | tf_op jit(solution)/shard_map/ppermute | solution.py:19
  27.4 6.7 %collective-permute-start.1 = (bf16[21,16,2,192]{3,1,2,0:T(8,128)(2,1)S(1)}, bf16[21,16,2,192]{3,1,2,0:T(8,128)(2,1)S(1)}, u32[]{:S(2)}, u32[]{:S(2)}) collective-permute-start(bf16[21,16,2,192]{3,1,2,0:T(8,128)(2,1)S(1)} %get-tuple-element.10), channel_id=1, source_target_pairs={{4,0},{8,4},{12,8},{16,12},{20,16},{24,20},{28,24},{32,28},{36,32}... | collective-permute-start | bytes 774152 | tf_op jit(solution)/shard_map/ppermute | solution.py:22
  70.8 5.1 %copy-start.4 = (bf16[4,36864]{1,0:T(4,128)(2,1)S(1)}, bf16[4,36864]{1,0:T(4,128)(2,1)}, u32[]{:S(2)}) copy-start(bf16[4,36864]{1,0:T(4,128)(2,1)} %param.9) | copy-start | bytes 884740
  70.8 18.5 %all-to-all-start.1 = ((f32[84,16,1,192]{3,1,2,0:T(8,128)}), f32[84,16,1,192]{3,1,2,0:T(8,128)S(1)}, u32[]{:S(2)}, u32[]{:S(2)}) async-start(f32[84,16,1,192]{3,1,2,0:T(8,128)} %copy.32), calls=%async_computation.1 | async-start | bytes 2752512 | tf_op jit(solution)/shard_map/all_to_all | solution.py:54
  91.3 1.6 %copy-start.1 = (bf16[768,768,1]{1,0,2:T(8,128)(2,1)S(1)}, bf16[768,768,1]{1,0,2:T(8,128)(2,1)}, u32[]{:S(2)}) copy-start(bf16[768,768,1]{1,0,2:T(8,128)(2,1)} %reshape.55) | copy-start | bytes 3538948
  91.3 1.9 %copy-start.3 = (f32[21,16,768]{2,1,0:T(8,128)S(1)}, f32[21,16,768]{2,1,0:T(8,128)}, u32[]{:S(2)}) copy-start(f32[21,16,768]{2,1,0:T(8,128)} %param.6) | copy-start | bytes 3096580
  93.2 1.5 %copy-start.2 = (f32[21,16,768]{2,1,0:T(8,128)}, f32[21,16,768]{2,1,0:T(8,128)S(1)}, u32[]{:S(2)}) copy-start(f32[21,16,768]{2,1,0:T(8,128)S(1)} %sub.3) | copy-start | bytes 3096580

commit v10 on v5

--- a/solution.py
+++ b/solution.py
@@ -22,9 +22,30 @@
     return x
 
 
+def pick(extended, column_rows, width):
+    blocks = column_rows.shape[0]
+    rows = []
+    for r in range(blocks):
+        near = width + r
+        chosen = [extended[:, :, near]]
+        for s, options in ((1, (near - 2, near - 1)), (2, (near + 2, near + 1))):
+            if (s == 1 and r == 0) or (s == 2 and r == blocks - 1):
+                chosen.append(extended[:, :, options[0]])
+            else:
+                chosen.append(
+                    jnp.where(
+                        column_rows[r, s] == options[0],
+                        extended[:, :, options[0]],
+                        extended[:, :, options[1]],
+                    )
+                )
+        rows.append(jnp.stack(chosen, axis=2))
+    return jnp.stack(rows, axis=2)
+
+
 def stiffness(extended, tile_rows, column_rows):
     block_size = extended.shape[-1]
-    picked = jnp.take(extended, column_rows, axis=2)
+    picked = pick(extended, column_rows, H)
     shaped = tile_rows.reshape(
         tile_rows.shape[0], tile_rows.shape[1], tile_rows.shape[2], block_size, block_size
     )

time: 85.5 us -> 93.4 us (1.092)
  the two profiles are of different devices: /device:TPU:56 before, /device:TPU:408 now
where the time goes in v10:
time: 93.4 us; the launch traced here: 93 us
  blocking collectives  31.4 us (34%)
  local copies, waits for them, and re-layouts  18.5 us (20%)
  waiting for transfers between devices  15.1 us (16%)
  starting transfers between devices  9.53 us (10%)
  other arithmetic  7.49 us (8%)
  matrix products  6.22 us (7%)
  between operations  4.66 us (5%)
    all_to_all x1, blocking collectives, body(): lax.all_to_all(products, 'mode', split_axis=3, concat_axis=1, tiled=True)  31.4 us
    all_to_all x1, waiting for transfers between devices, body(): lax.all_to_all(mixture, 'mode', split_axis=0, concat_axis=2, tiled=True)  15.1 us
    reshape x1, local copies, waits for them, and re-layouts, stiffness(): tile_rows.reshape(tile_rows.shape[0], tile_rows.shape[1], tile_rows.shape...  5.28 us
    all_to_all x1, starting transfers between devices, body(): lax.all_to_all(mixture, 'mode', split_axis=0, concat_axis=2, tiled=True)  3.86 us
    ppermute x1, starting transfers between devices, padded(): after = lax.ppermute(initial, axis, down)  3.63 us
    select_n x4, other arithmetic, pick(): jnp.where(column_rows[r, s] == options[0], extended[:, :, options[0]], ex...  3.38 us
    dot_general x1, matrix products, stiffness(): jnp.einsum('krsim,plrsm->kplri', shaped, picked, preferred_element_type=j...  2.59 us
    slice x1, local copies, waits for them, and re-layouts, pick(): chosen = [extended[:, :, near]]  2.47 us
  transfers between devices with their start and end apart: 3, of which 1 were waited for; matrix products, arithmetic and copies ran while one was open for 16% of the time, Pallas kernels for 0%

profile of v10, /device:TPU:408, one launch (start us, length us, event | category | flops | bytes accessed | tf_op | source)
XLA Modules:
  0.0 93.0 jit_solution(7072149977139701089)
XLA Ops:
  0.6 1.3 %convert_element_type.14 = bf16[21,16,768]{2,1,0:T(8,128)(2,1)S(1)} convert(f32[21,16,768]{2,1,0:T(8,128)} %param.6) | non-fusion elementwise | flops 258048 | bytes 1548288 | tf_op jit(solution)/shard_map/convert_element_type | solution.py:59
  2.6 0.7 fusion.22
  3.3 0.8 copy.51
  4.1 2.0 %collective-permute-start = (bf16[21,16,2,192]{3,1,2,0:T(8,128)(2,1)}, bf16[21,16,2,192]{3,1,2,0:T(8,128)(2,1)}, u32[]{:S(2)}, u32[]{:S(2)}) collective-permute-start(bf16[21,16,2,192]{3,1,2,0:T(8,128)(2,1)} %copy.51), channel_id=1, source_target_pairs={{0,4},{4,8},{8,12},{12,16},{16,20},{20,24},{24,28},{28,32},{32,36}... | collective-permute-start | bytes 774152 | tf_op jit(solution)/shard_map/ppermute | solution.py:19
  6.1 0.8 copy.55
  6.9 3.6 %collective-permute-start.1 = (bf16[21,16,2,192]{3,1,2,0:T(8,128)(2,1)}, bf16[21,16,2,192]{3,1,2,0:T(8,128)(2,1)}, u32[]{:S(2)}, u32[]{:S(2)}) collective-permute-start(bf16[21,16,2,192]{3,1,2,0:T(8,128)(2,1)} %copy.55), channel_id=1, source_target_pairs={{4,0},{8,4},{12,8},{16,12},{20,16},{24,20},{28,24},{32,28},{36,32}... | collective-permute-start | bytes 774152 | tf_op jit(solution)/shard_map/ppermute | solution.py:20
  10.6 2.5 %fusion.21 = (bf16[21,16,1,192]{3,2,1,0:T(2,128)(2,1)}, bf16[21,16,1,192]{3,2,1,0:T(2,128)(2,1)}, bf16[21,16,1,192]{3,2,1,0:T(2,128)(2,1)}, bf16[21,16,1,192]{3,2,1,0:T(2,128)(2,1)}) fusion(bf16[21,16,4,192]{3,2,1,0:T(4,128)(2,1)S(1)} %reshape.41), kind=kLoop, calls=%fused_computation.32 | loop fusion | bytes 1032192 | tf_op jit(solution)/shard_map/slice | solution.py:30
  13.0 0.7 fusion.23
  13.7 5.3 %reshape.42 = bf16[3,4,3,192,192]{4,3,1,2,0:T(8,128)(2,1)} reshape(bf16[3,4,3,36864]{3,1,2,0:T(4,128)(2,1)S(1)} %copy-done.5) | data formatting | bytes 5308416 | tf_op jit(solution)/shard_map/reshape | solution.py:49
  22.8 1.0 %broadcast_select_fusion.3 = (bf16[21,16,1,192]{3,1,2,0:T(8,128)(2,1)S(1)}, bf16[21,16,1,192]{3,1,2,0:T(8,128)(2,1)S(1)}, bf16[21,16,1,192]{3,1,2,0:T(8,128)(2,1)S(1)}) fusion(pred[]{:T(512)} %bitcast, bf16[21,16,1,192]{3,2,1,0:T(2,128)(2,1)} %get-tuple-element.12, bf16[21,16,1,192]{3,2,1,0:T(2,128)(2,1)S(1)} %copy-done.8), kind=kLoop, calls=%fused_computation.27 | loop fusion | flops 64512 | bytes 645121 | tf_op jit(solution)/shard_map/jit(_where)/select_n | solution.py:36
  23.9 1.1 %slice_select_fusion.1 = (bf16[21,16,1,192]{3,1,2,0:T(8,128)(2,1)S(1)}, bf16[21,16,1,192]{3,1,2,0:T(8,128)(2,1)S(1)}, bf16[21,16,1,192]{3,1,2,0:T(8,128)(2,1)S(1)}) fusion(bf16[21,16,2,192]{3,1,2,0:T(8,128)(2,1)} %collective-permute-done, pred[]{:T(512)} %bitcast.2, bf16[21,16,1,192]{3,2,1,0:T(2,128)(2,1)S(1)} %copy-done.7), kind=kLoop, calls=%fused_computation.23 | loop fusion | flops 64512 | bytes 774145 | tf_op jit(solution)/shard_map/jit(_where)/select_n | solution.py:36
  25.3 1.2 %slice_select_fusion = (bf16[21,16,1,192]{3,1,2,0:T(8,128)(2,1)S(1)}, bf16[21,16,1,192]{3,1,2,0:T(8,128)(2,1)S(1)}) fusion(bf16[21,16,1,192]{3,1,2,0:T(8,128)(2,1)S(1)} %get-tuple-element.21, bf16[21,16,2,192]{3,1,2,0:T(8,128)(2,1)} %collective-permute-done.1, pred[]{:T(512)} %bitcast.6), kind=kLoop, calls=%fused_computation.22 | loop fusion | flops 64512 | bytes 645121 | tf_op jit(solution)/shard_map/jit(_where)/select_n | solution.py:36
  27.2 2.6 %fusion.4 = bf16[3,21,16,4,192]{4,2,0,1,3:T(8,128)(2,1)S(1)} fusion(bf16[21,16,1,3,192]{4,1,3,0,2:T(8,128)(2,1)S(1)} %get-tuple-element.31, bf16[21,16,1,3,192]{4,1,3,0,2:T(8,128)(2,1)S(1)} %get-tuple-element.30, bf16[21,16,1,3,192]{4,1,3,0,2:T(8,128)(2,1)S(1)} %get-tuple-element.29, bf16[21,16,1,3,192]{4,1,3,0,2:T(8,128)(2,1)S(1)} %get-tuple-element.28, ...), kind=kOutput, calls=%fused_computation.5 | convolution fusion | flops 898781184 | bytes 5750784 | tf_op jit(solution)/shard_map/krsim,plrsm->kplri/dot_general | solution.py:52
  29.8 31.4 %all_to_all.30 = bf16[3,21,16,4,192]{4,2,0,1,3:T(8,128)(2,1)S(1)} all-to-all(bf16[3,21,16,4,192]{4,2,0,1,3:T(8,128)(2,1)S(1)} %fusion.4), channel_id=1, replica_groups=mesh['space'=128,'mode'=4] {'mode'}, dimensions={3} | all-to-all | bytes 3096576 | tf_op jit(solution)/shard_map/all_to_all | solution.py:65
  61.2 2.1 %fusion.13 = f32[84,16,1,192]{3,0,1,2:T(8,128)S(1)} fusion(bf16[3,84,16,192]{3,2,0,1:T(8,128)(2,1)S(1)} %bitcast.57, f32[3,84,84]{2,1,0:T(8,128)S(1)} %copy-done), kind=kOutput, calls=%fused_computation.14 | convolution fusion | flops 780337152 | bytes 2665152 | tf_op jit(solution)/shard_map/kab,kblqn->alqn/dot_general | solution.py:62
  63.3 1.5 %copy.41 = f32[84,16,1,192]{3,1,2,0:T(8,128)} copy(f32[84,16,1,192]{3,0,1,2:T(8,128)S(1)} %fusion.13) | data formatting | bytes 2064384 | tf_op jit(solution)/shard_map/kab,kblqn->alqn/dot_general | solution.py:62
  64.8 3.9 %all-to-all-start.1 = ((f32[84,16,1,192]{3,1,2,0:T(8,128)}), f32[84,16,1,192]{3,1,2,0:T(8,128)S(1)}, u32[]{:S(2)}, u32[]{:S(2)}) async-start(f32[84,16,1,192]{3,1,2,0:T(8,128)} %copy.41), calls=%async_computation.1 | async-start | bytes 2752512 | tf_op jit(solution)/shard_map/all_to_all | solution.py:70
  69.4 0.8 multiply_bitcast_fusion
  70.2 2.3 %reshape.52 = bf16[768,768,1]{1,0,2:T(8,128)(2,1)} reshape(bf16[4,192,4,192]{3,2,1,0:T(4,128)(2,1)S(1)} %multiply_bitcast_fusion) | data formatting | bytes 2359296 | tf_op jit(solution)/shard_map/reshape | solution.py:76
  72.5 15.1 %all-to-all-done.1 = f32[84,16,1,192]{3,1,2,0:T(8,128)S(1)} async-done(((f32[84,16,1,192]{3,1,2,0:T(8,128)}), f32[84,16,1,192]{3,1,2,0:T(8,128)S(1)}, u32[]{:S(2)}, u32[]{:S(2)}) %all-to-all-start.1) | async-done | bytes 1032224 | tf_op jit(solution)/shard_map/all_to_all | solution.py:70
  87.6 1.0 %copy.42 = f32[21,16,4,1,192]{4,2,1,0,3:T(4,128)S(1)} copy(f32[21,16,4,1,192]{4,1,0,2,3:T(8,128)S(1)} %bitcast.58) | data formatting | bytes 2064384 | tf_op jit(solution)/shard_map/all_to_all | solution.py:70
  88.6 0.9 reshape.44
  89.5 1.6 %sub.3 = f32[21,16,768]{2,1,0:T(8,128)S(1)} subtract(f32[21,16,768]{2,1,0:T(8,128)} %param.7, f32[21,16,768]{2,1,0:T(8,128)S(1)} %reshape.44) | non-fusion elementwise | flops 258048 | bytes 3096576 | tf_op jit(solution)/shard_map/sub | solution.py:72
  91.4 1.5 %fusion.16 = f32[21,16,768]{2,1,0:T(8,128)} fusion(f32[21,16,768]{2,1,0:T(8,128)S(1)} %copy-done.3, bf16[768,768,1]{1,0,2:T(8,128)(2,1)S(1)} %copy-done.1, f32[21,16,768]{2,1,0:T(8,128)S(1)} %sub.3), kind=kOutput, calls=%fused_computation.16 | convolution fusion | flops 397135872 | bytes 4276224 | tf_op jit(solution)/shard_map/dot_general | solution.py:77
  (31 shorter events, 2.6 us)
Async XLA Ops:
  0.6 60.6 %copy-start = (f32[3,84,84]{2,1,0:T(8,128)S(1)}, f32[3,84,84]{2,1,0:T(8,128)}, u32[]{:S(2)}) copy-start(f32[3,84,84]{2,1,0:T(8,128)} %param.11) | copy-start | bytes 254020
  3.3 9.7 %copy-start.10 = (s32[4,3]{1,0:T(4,128)S(1)}, s32[4,3]{1,0:T(4,128)}, u32[]{:S(2)}) copy-start(s32[4,3]{1,0:T(4,128)} %param.10) | copy-start | bytes 148
  3.3 10.4 %copy-start.5 = (bf16[3,4,3,36864]{3,1,2,0:T(4,128)(2,1)S(1)}, bf16[3,4,3,36864]{3,1,2,0:T(4,128)(2,1)}, u32[]{:S(2)}) copy-start(bf16[3,4,3,36864]{3,1,2,0:T(4,128)(2,1)} %param.8) | copy-start | bytes 7962628
  4.1 19.8 %collective-permute-start = (bf16[21,16,2,192]{3,1,2,0:T(8,128)(2,1)}, bf16[21,16,2,192]{3,1,2,0:T(8,128)(2,1)}, u32[]{:S(2)}, u32[]{:S(2)}) collective-permute-start(bf16[21,16,2,192]{3,1,2,0:T(8,128)(2,1)} %copy.51), channel_id=1, source_target_pairs={{0,4},{4,8},{8,12},{12,16},{16,20},{20,24},{24,28},{28,32},{32,36}... | collective-permute-start | bytes 774152 | tf_op jit(solution)/shard_map/ppermute | solution.py:19
  6.9 18.3 %collective-permute-start.1 = (bf16[21,16,2,192]{3,1,2,0:T(8,128)(2,1)}, bf16[21,16,2,192]{3,1,2,0:T(8,128)(2,1)}, u32[]{:S(2)}, u32[]{:S(2)}) collective-permute-start(bf16[21,16,2,192]{3,1,2,0:T(8,128)(2,1)} %copy.55), channel_id=1, source_target_pairs={{4,0},{8,4},{12,8},{16,12},{20,16},{24,20},{28,24},{32,28},{36,32}... | collective-permute-start | bytes 774152 | tf_op jit(solution)/shard_map/ppermute | solution.py:20
  13.7 9.1 %copy-start.8 = (bf16[21,16,1,192]{3,2,1,0:T(2,128)(2,1)S(1)}, bf16[21,16,1,192]{3,2,1,0:T(2,128)(2,1)}, u32[]{:S(2)}) copy-start(bf16[21,16,1,192]{3,2,1,0:T(2,128)(2,1)} %get-tuple-element.11) | copy-start | bytes 387076
  13.7 10.1 %copy-start.7 = (bf16[21,16,1,192]{3,2,1,0:T(2,128)(2,1)S(1)}, bf16[21,16,1,192]{3,2,1,0:T(2,128)(2,1)}, u32[]{:S(2)}) copy-start(bf16[21,16,1,192]{3,2,1,0:T(2,128)(2,1)} %get-tuple-element.9) | copy-start | bytes 387076
  19.0 5.9 %copy-start.6 = (bf16[21,16,1,192]{3,2,1,0:T(2,128)(2,1)S(1)}, bf16[21,16,1,192]{3,2,1,0:T(2,128)(2,1)}, u32[]{:S(2)}) copy-start(bf16[21,16,1,192]{3,2,1,0:T(2,128)(2,1)} %get-tuple-element.10) | copy-start | bytes 387076
  25.0 2.2 %copy-start.4 = (bf16[3,4,3,192,192]{4,3,1,2,0:T(8,128)(2,1)S(1)}, bf16[3,4,3,192,192]{4,3,1,2,0:T(8,128)(2,1)}, u32[]{:S(2)}) copy-start(bf16[3,4,3,192,192]{4,3,1,2,0:T(8,128)(2,1)} %reshape.42) | copy-start | bytes 7962628
  64.8 3.9 %copy-start.9 = (bf16[4,36864]{1,0:T(4,128)(2,1)S(1)}, bf16[4,36864]{1,0:T(4,128)(2,1)}, u32[]{:S(2)}) copy-start(bf16[4,36864]{1,0:T(4,128)(2,1)} %param.9) | copy-start | bytes 884740
  64.8 22.7 %all-to-all-start.1 = ((f32[84,16,1,192]{3,1,2,0:T(8,128)}), f32[84,16,1,192]{3,1,2,0:T(8,128)S(1)}, u32[]{:S(2)}, u32[]{:S(2)}) async-start(f32[84,16,1,192]{3,1,2,0:T(8,128)} %copy.41), calls=%async_computation.1 | async-start | bytes 2752512 | tf_op jit(solution)/shard_map/all_to_all | solution.py:70
  89.5 1.6 %copy-start.1 = (bf16[768,768,1]{1,0,2:T(8,128)(2,1)S(1)}, bf16[768,768,1]{1,0,2:T(8,128)(2,1)}, u32[]{:S(2)}) copy-start(bf16[768,768,1]{1,0,2:T(8,128)(2,1)} %reshape.52) | copy-start | bytes 3538948
  89.5 1.9 %copy-start.3 = (f32[21,16,768]{2,1,0:T(8,128)S(1)}, f32[21,16,768]{2,1,0:T(8,128)}, u32[]{:S(2)}) copy-start(f32[21,16,768]{2,1,0:T(8,128)} %param.6) | copy-start | bytes 3096580
  91.4 1.5 %copy-start.2 = (f32[21,16,768]{2,1,0:T(8,128)}, f32[21,16,768]{2,1,0:T(8,128)S(1)}, u32[]{:S(2)}) copy-start(f32[21,16,768]{2,1,0:T(8,128)S(1)} %sub.3) | copy-start | bytes 3096580

commit v11 on v5

--- a/solution.py
+++ b/solution.py
@@ -38,14 +38,14 @@
     rounded = iterate.astype(jnp.bfloat16).reshape(modes_here, loads, block_count, block_size)
     extended = padded(rounded, (("space", 2),), H)
     products = stiffness(extended, tiles, columns).astype(jnp.bfloat16)
+    exchanged = lax.all_to_all(products, "mode", split_axis=3, concat_axis=1, tiled=True)
+    high = lax.reduce_precision(coupling, exponent_bits=8, mantissa_bits=7)
+    rest = coupling - high
+    middle = lax.reduce_precision(rest, exponent_bits=8, mantissa_bits=7)
+    pieces = jnp.stack([high, middle, rest - middle]).astype(jnp.bfloat16)
     mixture = jnp.einsum(
-        "kab,kblqn->alqn",
-        coupling,
-        lax.all_to_all(products, "mode", split_axis=3, concat_axis=1, tiled=True).astype(
-            jnp.float32
-        ),
-        precision=lax.Precision.HIGHEST,
-    )
+        "jkab,kblqn->jalqn", pieces, exchanged, preferred_element_type=jnp.float32
+    ).sum(axis=0)
     applied = lax.all_to_all(mixture, "mode", split_axis=0, concat_axis=2, tiled=True)
     applied = applied.reshape(modes_here, loads, dofs_here)
     residual = forcing - applied

time: 85.5 us -> 84.4 us (0.987)
  blocking collectives: 30.7 us -> 0 us
  waiting for transfers between devices: 15.9 us -> 42.4 us
  starting transfers between devices: 9.24 us -> 13.7 us
  local copies, waits for them, and re-layouts: 16.1 us -> 14.7 us
    all_to_all x1 -> x0, blocking collectives: 30.7 us -> none  [body(): lax.all_to_all(products, 'mode', split_axis=3, concat_axis=1, tiled=True)]
    all_to_all x0 -> x1, waiting for transfers between devices: none -> 26.5 us  [body(): lax.all_to_all(products, 'mode', split_axis=3, concat_axis=1, tiled=True)]
    all_to_all x0 -> x1, starting transfers between devices: none -> 4.42 us  [body(): lax.all_to_all(products, 'mode', split_axis=3, concat_axis=1, tiled=True)]
    dot_general x1 -> x0, local copies, waits for them, and re-layouts: 1.52 us -> none  [body(): jnp.einsum('kab,kblqn->alqn', coupling, lax.all_to_all(products, 'mode',...]
    reduce_sum x0 -> x1, local copies, waits for them, and re-layouts: none -> 1.51 us  [body(): mixture = jnp.einsum('jkab,kblqn->jalqn', pieces, exchanged, preferred_el...]
    gather x1, local copies, waits for them, and re-layouts: 2.11 us -> 0.7 us  [stiffness(): picked = jnp.take(extended, column_rows, axis=2)]
  transfers between devices with their start and end apart: 3 -> 4, of which waited for: 1 -> 2; matrix products, arithmetic and copies ran while one was open for 12% -> 12% of each run, Pallas kernels for 0% -> 0%
where the time goes in v11:
time: 84.4 us; the launch traced here: 83.7 us
  waiting for transfers between devices  42.4 us (50%)
  local copies, waits for them, and re-layouts  14.7 us (17%)
  starting transfers between devices  13.7 us (16%)
  matrix products  8.11 us (10%)
  other arithmetic  3.94 us (5%)
    all_to_all x1, waiting for transfers between devices, body(): lax.all_to_all(products, 'mode', split_axis=3, concat_axis=1, tiled=True)  26.5 us
    all_to_all x1, waiting for transfers between devices, body(): lax.all_to_all(mixture, 'mode', split_axis=0, concat_axis=2, tiled=True)  15.9 us
    reshape x1, local copies, waits for them, and re-layouts, stiffness(): tile_rows.reshape(tile_rows.shape[0], tile_rows.shape[1], tile_rows.shape...  6.47 us
    dot_general x1, matrix products, stiffness(): jnp.einsum('krsim,plrsm->kplri', shaped, picked, preferred_element_type=j...  5.14 us
    all_to_all x1, starting transfers between devices, body(): lax.all_to_all(products, 'mode', split_axis=3, concat_axis=1, tiled=True)  4.42 us
    all_to_all x1, starting transfers between devices, body(): lax.all_to_all(mixture, 'mode', split_axis=0, concat_axis=2, tiled=True)  3.68 us
    ppermute x1, starting transfers between devices, padded(): after = lax.ppermute(initial, axis, down)  3.64 us
    reshape x1, local copies, waits for them, and re-layouts, body(): jnp.einsum('rim,rs->rmsi', inverse, diagonal).reshape(dofs_here, dofs_here)  2.24 us
  transfers between devices with their start and end apart: 4, of which 2 were waited for; matrix products, arithmetic and copies ran while one was open for 12% of the time, Pallas kernels for 0%

profile of v11, /device:TPU:56, one launch (start us, length us, event | category | flops | bytes accessed | tf_op | source)
XLA Modules:
  0.0 83.7 jit_solution(4578807247800751573)
XLA Ops:
  0.6 1.3 %convert_element_type.14 = bf16[21,16,768]{2,1,0:T(8,128)(2,1)S(1)} convert(f32[21,16,768]{2,1,0:T(8,128)} %param.6) | non-fusion elementwise | flops 258048 | bytes 1548288 | tf_op jit(solution)/shard_map/convert_element_type | solution.py:38
  1.9 0.6 reshape.35
  2.5 0.1 copy.23
  2.7 1.9 %collective-permute-start = (bf16[21,16,2,192]{3,1,2,0:T(8,128)(2,1)S(1)}, bf16[21,16,2,192]{3,1,2,0:T(8,128)(2,1)S(1)}, u32[]{:S(2)}, u32[]{:S(2)}) collective-permute-start(bf16[21,16,2,192]{3,1,2,0:T(8,128)(2,1)S(1)} %get-tuple-element.2), channel_id=1, source_target_pairs={{0,4},{4,8},{8,12},{12,16},{16,20},{20,24},{24,28},{28,32},{32,36}... | collective-permute-start | bytes 774152 | tf_op jit(solution)/shard_map/ppermute | solution.py:19
  4.6 3.6 %collective-permute-start.1 = (bf16[21,16,2,192]{3,1,2,0:T(8,128)(2,1)S(1)}, bf16[21,16,2,192]{3,1,2,0:T(8,128)(2,1)S(1)}, u32[]{:S(2)}, u32[]{:S(2)}) collective-permute-start(bf16[21,16,2,192]{3,1,2,0:T(8,128)(2,1)S(1)} %get-tuple-element.3), channel_id=1, source_target_pairs={{4,0},{8,4},{12,8},{16,12},{20,16},{24,20},{28,24},{32,28},{36,32}... | collective-permute-start | bytes 774152 | tf_op jit(solution)/shard_map/ppermute | solution.py:20
  8.4 6.5 %reshape.36 = bf16[3,4,3,192,192]{4,3,1,2,0:T(8,128)(2,1)} reshape(bf16[3,4,3,36864]{3,1,2,0:T(4,128)(2,1)} %param.8) | data formatting | bytes 5308416 | tf_op jit(solution)/shard_map/reshape | solution.py:28
  14.9 0.3 pad_maximum_fusion
  15.1 0.7 gather_fusion
  15.8 5.1 %fusion.4 = bf16[3,21,16,4,192]{4,2,0,1,3:T(8,128)(2,1)} fusion(bf16[3,4,3,192,192]{4,3,1,2,0:T(8,128)(2,1)} %reshape.36, bf16[4,3,21,16,192]{4,3,2,1,0:T(8,128)(2,1)S(1)} %bitcast.52, pred[4,3]{1,0:T(4,128)(4,1)S(1)} %compare_and_fusion), kind=kOutput, calls=%fused_computation.7 | convolution fusion | flops 893362176 | bytes 5750796 | tf_op jit(solution)/shard_map/krsim,plrsm->kplri/dot_general | solution.py:31
  21.0 4.4 %all-to-all-start = ((bf16[3,21,16,4,192]{4,2,0,1,3:T(8,128)(2,1)}), bf16[3,21,16,4,192]{4,2,0,1,3:T(8,128)(2,1)S(1)}, u32[]{:S(2)}, u32[]{:S(2)}) async-start(bf16[3,21,16,4,192]{4,2,0,1,3:T(8,128)(2,1)} %fusion.4), calls=%async_computation | async-start | bytes 4128768 | tf_op jit(solution)/shard_map/all_to_all | solution.py:41
  25.5 26.5 %all-to-all-done = bf16[3,21,16,4,192]{4,2,0,1,3:T(8,128)(2,1)S(1)} async-done(((bf16[3,21,16,4,192]{4,2,0,1,3:T(8,128)(2,1)}), bf16[3,21,16,4,192]{4,2,0,1,3:T(8,128)(2,1)S(1)}, u32[]{:S(2)}, u32[]{:S(2)}) %all-to-all-start) | async-done | bytes 1548320 | tf_op jit(solution)/shard_map/all_to_all | solution.py:41
  52.0 1.4 %bitcast_reduce_fusion = f32[84,16,192]{2,0,1:T(8,128)S(1)} fusion(bf16[3,84,16,192]{3,2,0,1:T(8,128)(2,1)S(1)} %bitcast.53, bf16[1,3,84,84]{3,2,1,0:T(8,128)(2,1)S(1)} %get-tuple-element.5, bf16[1,3,84,84]{3,2,1,0:T(8,128)(2,1)S(1)} %get-tuple-element.6, bf16[1,3,84,84]{3,2,1,0:T(8,128)(2,1)S(1)} %get-tuple-element.4), kind=kOutput, calls=%fused_computation.1 | convolution fusion | flops 391065696 | bytes 2707488 | tf_op jit(solution)/shard_map/jkab,kblqn->jalqn/dot_general | solution.py:46
  53.4 1.5 %copy.29 = f32[84,16,1,192]{3,1,2,0:T(8,128)} copy(f32[84,16,1,192]{3,0,1,2:T(8,128)S(1)} %bitcast.54) | data formatting | bytes 2064384 | tf_op jit(solution)/shard_map/reduce_sum | solution.py:48
  54.9 3.7 %all-to-all-start.1 = ((f32[84,16,1,192]{3,1,2,0:T(8,128)}), f32[84,16,1,192]{3,1,2,0:T(8,128)S(1)}, u32[]{:S(2)}, u32[]{:S(2)}) async-start(f32[84,16,1,192]{3,1,2,0:T(8,128)} %copy.29), calls=%async_computation.1 | async-start | bytes 2752512 | tf_op jit(solution)/shard_map/all_to_all | solution.py:49
  58.6 0.4 reshape.39
  59.1 0.2 copy.31
  59.3 0.8 %multiply_bitcast_fusion = bf16[4,192,4,192]{3,2,1,0:T(4,128)(2,1)S(1)} fusion(bf16[4,192,192]{1,2,0:T(8,128)(2,1)S(1)} %copy.31, bf16[4,4]{1,0:T(4,128)(2,1)S(1)} %fusion.20), kind=kLoop, calls=%fused_computation.10 | loop fusion | flops 589824 | bytes 1474592 | tf_op jit(solution)/shard_map/rim,rs->rmsi/transpose | solution.py:55
  60.1 2.2 %reshape.57 = bf16[768,768,1]{1,0,2:T(8,128)(2,1)} reshape(bf16[4,192,4,192]{3,2,1,0:T(4,128)(2,1)S(1)} %multiply_bitcast_fusion) | data formatting | bytes 2359296 | tf_op jit(solution)/shard_map/reshape | solution.py:55
  62.4 15.9 %all-to-all-done.1 = f32[84,16,1,192]{3,1,2,0:T(8,128)S(1)} async-done(((f32[84,16,1,192]{3,1,2,0:T(8,128)}), f32[84,16,1,192]{3,1,2,0:T(8,128)S(1)}, u32[]{:S(2)}, u32[]{:S(2)}) %all-to-all-start.1) | async-done | bytes 1032224 | tf_op jit(solution)/shard_map/all_to_all | solution.py:49
  78.3 1.0 %copy.30 = f32[21,16,4,1,192]{4,2,1,0,3:T(4,128)S(1)} copy(f32[21,16,4,1,192]{4,1,0,2,3:T(8,128)S(1)} %bitcast.51) | data formatting | bytes 2064384 | tf_op jit(solution)/shard_map/all_to_all | solution.py:49
  79.3 0.9 %reshape.38 = f32[21,16,768]{2,1,0:T(8,128)S(1)} reshape(f32[21,16,4,1,192]{4,2,1,0,3:T(4,128)S(1)} %copy.30) | data formatting | bytes 2064384 | tf_op jit(solution)/shard_map/reshape | solution.py:50
  80.2 1.5 %sub.11 = f32[21,16,768]{2,1,0:T(8,128)S(1)} subtract(f32[21,16,768]{2,1,0:T(8,128)} %param.7, f32[21,16,768]{2,1,0:T(8,128)S(1)} %reshape.38) | non-fusion elementwise | flops 258048 | bytes 3096576 | tf_op jit(solution)/shard_map/sub | solution.py:51
  81.8 0.3 copy-done.2
  82.1 1.5 %fusion.10 = f32[21,16,768]{2,1,0:T(8,128)} fusion(f32[21,16,768]{2,1,0:T(8,128)S(1)} %copy-done.2, bf16[768,768,1]{1,0,2:T(8,128)(2,1)S(1)} %copy-done, f32[21,16,768]{2,1,0:T(8,128)S(1)} %sub.11), kind=kOutput, calls=%fused_computation.13 | convolution fusion | flops 397135872 | bytes 4276224 | tf_op jit(solution)/shard_map/dot_general | solution.py:56
  (20 shorter events, 0.3 us)
Async XLA Ops:
  1.9 6.4 %copy-start.5 = (s32[4,3]{1,0:T(4,128)S(1)}, s32[4,3]{1,0:T(4,128)}, u32[]{:S(2)}) copy-start(s32[4,3]{1,0:T(4,128)} %param.10) | copy-start | bytes 148
  2.7 12.2 %collective-permute-start = (bf16[21,16,2,192]{3,1,2,0:T(8,128)(2,1)S(1)}, bf16[21,16,2,192]{3,1,2,0:T(8,128)(2,1)S(1)}, u32[]{:S(2)}, u32[]{:S(2)}) collective-permute-start(bf16[21,16,2,192]{3,1,2,0:T(8,128)(2,1)S(1)} %get-tuple-element.2), channel_id=1, source_target_pairs={{0,4},{4,8},{8,12},{12,16},{16,20},{20,24},{24,28},{28,32},{32,36}... | collective-permute-start | bytes 774152 | tf_op jit(solution)/shard_map/ppermute | solution.py:19
  4.6 10.2 %collective-permute-start.1 = (bf16[21,16,2,192]{3,1,2,0:T(8,128)(2,1)S(1)}, bf16[21,16,2,192]{3,1,2,0:T(8,128)(2,1)S(1)}, u32[]{:S(2)}, u32[]{:S(2)}) collective-permute-start(bf16[21,16,2,192]{3,1,2,0:T(8,128)(2,1)S(1)} %get-tuple-element.3), channel_id=1, source_target_pairs={{4,0},{8,4},{12,8},{16,12},{20,16},{24,20},{28,24},{32,28},{36,32}... | collective-permute-start | bytes 774152 | tf_op jit(solution)/shard_map/ppermute | solution.py:20
  21.0 4.4 %copy-start.4 = (f32[3,84,84]{2,1,0:T(8,128)S(1)}, f32[3,84,84]{2,1,0:T(8,128)}, u32[]{:S(2)}) copy-start(f32[3,84,84]{2,1,0:T(8,128)} %param.11) | copy-start | bytes 254020
  21.0 31.0 %all-to-all-start = ((bf16[3,21,16,4,192]{4,2,0,1,3:T(8,128)(2,1)}), bf16[3,21,16,4,192]{4,2,0,1,3:T(8,128)(2,1)S(1)}, u32[]{:S(2)}, u32[]{:S(2)}) async-start(bf16[3,21,16,4,192]{4,2,0,1,3:T(8,128)(2,1)} %fusion.4), calls=%async_computation | async-start | bytes 4128768 | tf_op jit(solution)/shard_map/all_to_all | solution.py:41
  54.9 3.7 %copy-start.3 = (bf16[4,36864]{1,0:T(4,128)(2,1)S(1)}, bf16[4,36864]{1,0:T(4,128)(2,1)}, u32[]{:S(2)}) copy-start(bf16[4,36864]{1,0:T(4,128)(2,1)} %param.9) | copy-start | bytes 884740
  54.9 23.3 %all-to-all-start.1 = ((f32[84,16,1,192]{3,1,2,0:T(8,128)}), f32[84,16,1,192]{3,1,2,0:T(8,128)S(1)}, u32[]{:S(2)}, u32[]{:S(2)}) async-start(f32[84,16,1,192]{3,1,2,0:T(8,128)} %copy.29), calls=%async_computation.1 | async-start | bytes 2752512 | tf_op jit(solution)/shard_map/all_to_all | solution.py:49
  80.2 1.6 %copy-start = (bf16[768,768,1]{1,0,2:T(8,128)(2,1)S(1)}, bf16[768,768,1]{1,0,2:T(8,128)(2,1)}, u32[]{:S(2)}) copy-start(bf16[768,768,1]{1,0,2:T(8,128)(2,1)} %reshape.57) | copy-start | bytes 3538948
  80.2 1.9 %copy-start.2 = (f32[21,16,768]{2,1,0:T(8,128)S(1)}, f32[21,16,768]{2,1,0:T(8,128)}, u32[]{:S(2)}) copy-start(f32[21,16,768]{2,1,0:T(8,128)} %param.6) | copy-start | bytes 3096580
  82.1 1.5 %copy-start.1 = (f32[21,16,768]{2,1,0:T(8,128)}, f32[21,16,768]{2,1,0:T(8,128)S(1)}, u32[]{:S(2)}) copy-start(f32[21,16,768]{2,1,0:T(8,128)S(1)} %sub.11) | copy-start | bytes 3096580

commit v12 on v11

--- a/solution.py
+++ b/solution.py
@@ -24,7 +24,7 @@
 
 def stiffness(extended, tile_rows, column_rows):
     block_size = extended.shape[-1]
-    picked = jnp.take(extended, column_rows, axis=2)
+    picked = jnp.take(extended, column_rows, axis=2, mode="clip")
     shaped = tile_rows.reshape(
         tile_rows.shape[0], tile_rows.shape[1], tile_rows.shape[2], block_size, block_size
     )

time: 84.4 us -> 84.4 us (level)
  no operation moved by 1% of the time
where the time goes in v12:
time: 84.4 us; the launch traced here: 83.6 us
  waiting for transfers between devices  42.4 us (50%)
  local copies, waits for them, and re-layouts  14.7 us (17%)
  starting transfers between devices  13.7 us (16%)
  matrix products  8.1 us (10%)
  other arithmetic  3.92 us (5%)
    all_to_all x1, waiting for transfers between devices, body(): lax.all_to_all(products, 'mode', split_axis=3, concat_axis=1, tiled=True)  26.5 us
    all_to_all x1, waiting for transfers between devices, body(): lax.all_to_all(mixture, 'mode', split_axis=0, concat_axis=2, tiled=True)  15.9 us
    reshape x1, local copies, waits for them, and re-layouts, stiffness(): tile_rows.reshape(tile_rows.shape[0], tile_rows.shape[1], tile_rows.shape...  6.47 us
    dot_general x1, matrix products, stiffness(): jnp.einsum('krsim,plrsm->kplri', shaped, picked, preferred_element_type=j...  5.13 us
    all_to_all x1, starting transfers between devices, body(): lax.all_to_all(products, 'mode', split_axis=3, concat_axis=1, tiled=True)  4.43 us
    all_to_all x1, starting transfers between devices, body(): lax.all_to_all(mixture, 'mode', split_axis=0, concat_axis=2, tiled=True)  3.68 us
    ppermute x1, starting transfers between devices, padded(): after = lax.ppermute(initial, axis, down)  3.64 us
    reshape x1, local copies, waits for them, and re-layouts, body(): jnp.einsum('rim,rs->rmsi', inverse, diagonal).reshape(dofs_here, dofs_here)  2.24 us
  transfers between devices with their start and end apart: 4, of which 2 were waited for; matrix products, arithmetic and copies ran while one was open for 12% of the time, Pallas kernels for 0%

profile of v12, /device:TPU:56, one launch (start us, length us, event | category | flops | bytes accessed | tf_op | source)
XLA Modules:
  0.0 83.6 jit_solution(2623052598735258498)
XLA Ops:
  0.6 1.3 %convert_element_type.14 = bf16[21,16,768]{2,1,0:T(8,128)(2,1)S(1)} convert(f32[21,16,768]{2,1,0:T(8,128)} %param.6) | non-fusion elementwise | flops 258048 | bytes 1548288 | tf_op jit(solution)/shard_map/convert_element_type | solution.py:38
  1.9 0.6 reshape.30
  2.5 0.1 copy.23
  2.7 1.9 %collective-permute-start = (bf16[21,16,2,192]{3,1,2,0:T(8,128)(2,1)S(1)}, bf16[21,16,2,192]{3,1,2,0:T(8,128)(2,1)S(1)}, u32[]{:S(2)}, u32[]{:S(2)}) collective-permute-start(bf16[21,16,2,192]{3,1,2,0:T(8,128)(2,1)S(1)} %get-tuple-element.2), channel_id=1, source_target_pairs={{0,4},{4,8},{8,12},{12,16},{16,20},{20,24},{24,28},{28,32},{32,36}... | collective-permute-start | bytes 774152 | tf_op jit(solution)/shard_map/ppermute | solution.py:19
  4.6 3.6 %collective-permute-start.1 = (bf16[21,16,2,192]{3,1,2,0:T(8,128)(2,1)S(1)}, bf16[21,16,2,192]{3,1,2,0:T(8,128)(2,1)S(1)}, u32[]{:S(2)}, u32[]{:S(2)}) collective-permute-start(bf16[21,16,2,192]{3,1,2,0:T(8,128)(2,1)S(1)} %get-tuple-element.3), channel_id=1, source_target_pairs={{4,0},{8,4},{12,8},{16,12},{20,16},{24,20},{28,24},{32,28},{36,32}... | collective-permute-start | bytes 774152 | tf_op jit(solution)/shard_map/ppermute | solution.py:20
  8.4 6.5 %reshape.31 = bf16[3,4,3,192,192]{4,3,1,2,0:T(8,128)(2,1)} reshape(bf16[3,4,3,36864]{3,1,2,0:T(4,128)(2,1)} %param.8) | data formatting | bytes 5308416 | tf_op jit(solution)/shard_map/reshape | solution.py:28
  14.9 0.3 pad_maximum_fusion
  15.1 0.7 gather_fusion
  15.8 5.1 %fusion.4 = bf16[3,21,16,4,192]{4,2,0,1,3:T(8,128)(2,1)} fusion(bf16[21,16,4,3,192,1]{4,1,0,3,2,5:T(8,128)(2,1)S(1)} %bitcast.50, bf16[3,4,3,192,192]{4,3,1,2,0:T(8,128)(2,1)} %reshape.31), kind=kOutput, calls=%fused_computation.7 | convolution fusion | flops 892588032 | bytes 5750784 | tf_op jit(solution)/shard_map/krsim,plrsm->kplri/dot_general | solution.py:31
  21.0 4.4 %all-to-all-start = ((bf16[3,21,16,4,192]{4,2,0,1,3:T(8,128)(2,1)}), bf16[3,21,16,4,192]{4,2,0,1,3:T(8,128)(2,1)S(1)}, u32[]{:S(2)}, u32[]{:S(2)}) async-start(bf16[3,21,16,4,192]{4,2,0,1,3:T(8,128)(2,1)} %fusion.4), calls=%async_computation | async-start | bytes 4128768 | tf_op jit(solution)/shard_map/all_to_all | solution.py:41
  25.4 26.5 %all-to-all-done = bf16[3,21,16,4,192]{4,2,0,1,3:T(8,128)(2,1)S(1)} async-done(((bf16[3,21,16,4,192]{4,2,0,1,3:T(8,128)(2,1)}), bf16[3,21,16,4,192]{4,2,0,1,3:T(8,128)(2,1)S(1)}, u32[]{:S(2)}, u32[]{:S(2)}) %all-to-all-start) | async-done | bytes 1548320 | tf_op jit(solution)/shard_map/all_to_all | solution.py:41
  51.9 1.4 %bitcast_reduce_fusion = f32[84,16,192]{2,0,1:T(8,128)S(1)} fusion(bf16[3,84,16,192]{3,2,0,1:T(8,128)(2,1)S(1)} %bitcast.51, bf16[1,3,84,84]{3,2,1,0:T(8,128)(2,1)S(1)} %get-tuple-element.5, bf16[1,3,84,84]{3,2,1,0:T(8,128)(2,1)S(1)} %get-tuple-element.6, bf16[1,3,84,84]{3,2,1,0:T(8,128)(2,1)S(1)} %get-tuple-element.4), kind=kOutput, calls=%fused_computation.1 | convolution fusion | flops 391065696 | bytes 2707488 | tf_op jit(solution)/shard_map/jkab,kblqn->jalqn/dot_general | solution.py:46
  53.4 1.5 %copy.29 = f32[84,16,1,192]{3,1,2,0:T(8,128)} copy(f32[84,16,1,192]{3,0,1,2:T(8,128)S(1)} %bitcast.52) | data formatting | bytes 2064384 | tf_op jit(solution)/shard_map/reduce_sum | solution.py:48
  54.9 3.7 %all-to-all-start.1 = ((f32[84,16,1,192]{3,1,2,0:T(8,128)}), f32[84,16,1,192]{3,1,2,0:T(8,128)S(1)}, u32[]{:S(2)}, u32[]{:S(2)}) async-start(f32[84,16,1,192]{3,1,2,0:T(8,128)} %copy.29), calls=%async_computation.1 | async-start | bytes 2752512 | tf_op jit(solution)/shard_map/all_to_all | solution.py:49
  58.6 0.4 reshape.34
  59.0 0.2 copy.31
  59.2 0.8 %multiply_bitcast_fusion = bf16[4,192,4,192]{3,2,1,0:T(4,128)(2,1)S(1)} fusion(bf16[4,192,192]{1,2,0:T(8,128)(2,1)S(1)} %copy.31, bf16[4,4]{1,0:T(4,128)(2,1)S(1)} %fusion.20), kind=kLoop, calls=%fused_computation.9 | loop fusion | flops 589824 | bytes 1474592 | tf_op jit(solution)/shard_map/rim,rs->rmsi/transpose | solution.py:55
  60.1 2.2 %reshape.52 = bf16[768,768,1]{1,0,2:T(8,128)(2,1)} reshape(bf16[4,192,4,192]{3,2,1,0:T(4,128)(2,1)S(1)} %multiply_bitcast_fusion) | data formatting | bytes 2359296 | tf_op jit(solution)/shard_map/reshape | solution.py:55
  62.3 15.9 %all-to-all-done.1 = f32[84,16,1,192]{3,1,2,0:T(8,128)S(1)} async-done(((f32[84,16,1,192]{3,1,2,0:T(8,128)}), f32[84,16,1,192]{3,1,2,0:T(8,128)S(1)}, u32[]{:S(2)}, u32[]{:S(2)}) %all-to-all-start.1) | async-done | bytes 1032224 | tf_op jit(solution)/shard_map/all_to_all | solution.py:49
  78.3 1.0 %copy.30 = f32[21,16,4,1,192]{4,2,1,0,3:T(4,128)S(1)} copy(f32[21,16,4,1,192]{4,1,0,2,3:T(8,128)S(1)} %bitcast.49) | data formatting | bytes 2064384 | tf_op jit(solution)/shard_map/all_to_all | solution.py:49
  79.3 0.9 %reshape.33 = f32[21,16,768]{2,1,0:T(8,128)S(1)} reshape(f32[21,16,4,1,192]{4,2,1,0,3:T(4,128)S(1)} %copy.30) | data formatting | bytes 2064384 | tf_op jit(solution)/shard_map/reshape | solution.py:50
  80.2 1.5 %sub.11 = f32[21,16,768]{2,1,0:T(8,128)S(1)} subtract(f32[21,16,768]{2,1,0:T(8,128)} %param.7, f32[21,16,768]{2,1,0:T(8,128)S(1)} %reshape.33) | non-fusion elementwise | flops 258048 | bytes 3096576 | tf_op jit(solution)/shard_map/sub | solution.py:51
  81.8 0.3 copy-done.2
  82.1 1.5 %fusion.10 = f32[21,16,768]{2,1,0:T(8,128)} fusion(f32[21,16,768]{2,1,0:T(8,128)S(1)} %copy-done.2, bf16[768,768,1]{1,0,2:T(8,128)(2,1)S(1)} %copy-done, f32[21,16,768]{2,1,0:T(8,128)S(1)} %sub.11), kind=kOutput, calls=%fused_computation.12 | convolution fusion | flops 397135872 | bytes 4276224 | tf_op jit(solution)/shard_map/dot_general | solution.py:56
  (18 shorter events, 0.3 us)
Async XLA Ops:
  1.9 6.4 %copy-start.5 = (s32[4,3]{1,0:T(4,128)S(1)}, s32[4,3]{1,0:T(4,128)}, u32[]{:S(2)}) copy-start(s32[4,3]{1,0:T(4,128)} %param.10) | copy-start | bytes 148
  2.7 12.1 %collective-permute-start = (bf16[21,16,2,192]{3,1,2,0:T(8,128)(2,1)S(1)}, bf16[21,16,2,192]{3,1,2,0:T(8,128)(2,1)S(1)}, u32[]{:S(2)}, u32[]{:S(2)}) collective-permute-start(bf16[21,16,2,192]{3,1,2,0:T(8,128)(2,1)S(1)} %get-tuple-element.2), channel_id=1, source_target_pairs={{0,4},{4,8},{8,12},{12,16},{16,20},{20,24},{24,28},{28,32},{32,36}... | collective-permute-start | bytes 774152 | tf_op jit(solution)/shard_map/ppermute | solution.py:19
  4.6 10.2 %collective-permute-start.1 = (bf16[21,16,2,192]{3,1,2,0:T(8,128)(2,1)S(1)}, bf16[21,16,2,192]{3,1,2,0:T(8,128)(2,1)S(1)}, u32[]{:S(2)}, u32[]{:S(2)}) collective-permute-start(bf16[21,16,2,192]{3,1,2,0:T(8,128)(2,1)S(1)} %get-tuple-element.3), channel_id=1, source_target_pairs={{4,0},{8,4},{12,8},{16,12},{20,16},{24,20},{28,24},{32,28},{36,32}... | collective-permute-start | bytes 774152 | tf_op jit(solution)/shard_map/ppermute | solution.py:20
  21.0 4.4 %copy-start.4 = (f32[3,84,84]{2,1,0:T(8,128)S(1)}, f32[3,84,84]{2,1,0:T(8,128)}, u32[]{:S(2)}) copy-start(f32[3,84,84]{2,1,0:T(8,128)} %param.11) | copy-start | bytes 254020
  21.0 31.0 %all-to-all-start = ((bf16[3,21,16,4,192]{4,2,0,1,3:T(8,128)(2,1)}), bf16[3,21,16,4,192]{4,2,0,1,3:T(8,128)(2,1)S(1)}, u32[]{:S(2)}, u32[]{:S(2)}) async-start(bf16[3,21,16,4,192]{4,2,0,1,3:T(8,128)(2,1)} %fusion.4), calls=%async_computation | async-start | bytes 4128768 | tf_op jit(solution)/shard_map/all_to_all | solution.py:41
  54.9 3.7 %copy-start.3 = (bf16[4,36864]{1,0:T(4,128)(2,1)S(1)}, bf16[4,36864]{1,0:T(4,128)(2,1)}, u32[]{:S(2)}) copy-start(bf16[4,36864]{1,0:T(4,128)(2,1)} %param.9) | copy-start | bytes 884740
  54.9 23.4 %all-to-all-start.1 = ((f32[84,16,1,192]{3,1,2,0:T(8,128)}), f32[84,16,1,192]{3,1,2,0:T(8,128)S(1)}, u32[]{:S(2)}, u32[]{:S(2)}) async-start(f32[84,16,1,192]{3,1,2,0:T(8,128)} %copy.29), calls=%async_computation.1 | async-start | bytes 2752512 | tf_op jit(solution)/shard_map/all_to_all | solution.py:49
  80.2 1.6 %copy-start = (bf16[768,768,1]{1,0,2:T(8,128)(2,1)S(1)}, bf16[768,768,1]{1,0,2:T(8,128)(2,1)}, u32[]{:S(2)}) copy-start(bf16[768,768,1]{1,0,2:T(8,128)(2,1)} %reshape.52) | copy-start | bytes 3538948
  80.2 1.9 %copy-start.2 = (f32[21,16,768]{2,1,0:T(8,128)S(1)}, f32[21,16,768]{2,1,0:T(8,128)}, u32[]{:S(2)}) copy-start(f32[21,16,768]{2,1,0:T(8,128)} %param.6) | copy-start | bytes 3096580
  82.1 1.5 %copy-start.1 = (f32[21,16,768]{2,1,0:T(8,128)}, f32[21,16,768]{2,1,0:T(8,128)S(1)}, u32[]{:S(2)}) copy-start(f32[21,16,768]{2,1,0:T(8,128)S(1)} %sub.11) | copy-start | bytes 3096580

commit v13 on v11

--- a/solution.py
+++ b/solution.py
@@ -28,7 +28,18 @@
     shaped = tile_rows.reshape(
         tile_rows.shape[0], tile_rows.shape[1], tile_rows.shape[2], block_size, block_size
     )
-    return jnp.einsum("krsim,plrsm->kplri", shaped, picked, preferred_element_type=jnp.float32)
+    return jnp.stack(
+        [
+            jnp.einsum(
+                "ksim,plsm->kpli",
+                shaped[:, r],
+                picked[:, :, r],
+                preferred_element_type=jnp.float32,
+            )
+            for r in range(shaped.shape[1])
+        ],
+        axis=3,
+    )
 
 
 def body(iterate, forcing, tiles, inverse_blocks, columns, coupling):

time: 84.4 us -> 85.6 us (1.014)
  matrix products: 8.11 us -> 5.39 us
  other arithmetic: 3.94 us -> 6.06 us
  local copies, waits for them, and re-layouts: 14.7 us -> 16.5 us
    dot_general x1 -> x4, matrix products: 5.14 us -> 2.43 us  [stiffness(): jnp.einsum('ksim,plsm->kpli', shaped[:, r], picked[:, :, r], preferred_el...]
    another operation x1 -> x2, other arithmetic: 0.01 us -> 1.87 us  [the longest x1 1.87 us: stiffness(): jnp.stack([jnp.einsum('ksim,plsm->kpli', shaped[:, r], picked[:, :, r], p...]
    unnamed x12 -> x14, local copies, waits for them, and re-layouts: 0.4 us -> 2.12 us
where the time goes in v13:
time: 85.6 us; the launch traced here: 84.8 us
  waiting for transfers between devices  42.2 us (49%)
  local copies, waits for them, and re-layouts  16.5 us (19%)
  starting transfers between devices  13.8 us (16%)
  other arithmetic  6.06 us (7%)
  matrix products  5.39 us (6%)
    all_to_all x1, waiting for transfers between devices, body(): lax.all_to_all(products, 'mode', split_axis=3, concat_axis=1, tiled=True)  26.5 us
    all_to_all x1, waiting for transfers between devices, body(): lax.all_to_all(mixture, 'mode', split_axis=0, concat_axis=2, tiled=True)  15.7 us
    reshape x1, local copies, waits for them, and re-layouts, stiffness(): tile_rows.reshape(tile_rows.shape[0], tile_rows.shape[1], tile_rows.shape...  6.46 us
    all_to_all x1, starting transfers between devices, body(): lax.all_to_all(products, 'mode', split_axis=3, concat_axis=1, tiled=True)  4.41 us
    all_to_all x1, starting transfers between devices, body(): lax.all_to_all(mixture, 'mode', split_axis=0, concat_axis=2, tiled=True)  3.86 us
    ppermute x1, starting transfers between devices, padded(): after = lax.ppermute(initial, axis, down)  3.64 us
    dot_general x4, matrix products, stiffness(): jnp.einsum('ksim,plsm->kpli', shaped[:, r], picked[:, :, r], preferred_el...  2.43 us
    reshape x1, local copies, waits for them, and re-layouts, body(): jnp.einsum('rim,rs->rmsi', inverse, diagonal).reshape(dofs_here, dofs_here)  2.26 us
  transfers between devices with their start and end apart: 4, of which 2 were waited for; matrix products, arithmetic and copies ran while one was open for 12% of the time, Pallas kernels for 0%

profile of v13, /device:TPU:56, one launch (start us, length us, event | category | flops | bytes accessed | tf_op | source)
XLA Modules:
  0.0 84.8 jit_solution(357807779278169575)
XLA Ops:
  0.6 1.3 %convert_element_type.4 = bf16[21,16,768]{2,1,0:T(8,128)(2,1)S(1)} convert(f32[21,16,768]{2,1,0:T(8,128)} %param.6) | non-fusion elementwise | flops 258048 | bytes 1548288 | tf_op jit(solution)/shard_map/convert_element_type | solution.py:49
  1.9 0.6 reshape.35
  2.7 1.9 %collective-permute-start = (bf16[21,16,2,192]{3,1,2,0:T(8,128)(2,1)S(1)}, bf16[21,16,2,192]{3,1,2,0:T(8,128)(2,1)S(1)}, u32[]{:S(2)}, u32[]{:S(2)}) collective-permute-start(bf16[21,16,2,192]{3,1,2,0:T(8,128)(2,1)S(1)} %get-tuple-element.2), channel_id=1, source_target_pairs={{0,4},{4,8},{8,12},{12,16},{16,20},{20,24},{24,28},{28,32},{32,36}... | collective-permute-start | bytes 774152 | tf_op jit(solution)/shard_map/ppermute | solution.py:19
  4.6 3.6 %collective-permute-start.1 = (bf16[21,16,2,192]{3,1,2,0:T(8,128)(2,1)S(1)}, bf16[21,16,2,192]{3,1,2,0:T(8,128)(2,1)S(1)}, u32[]{:S(2)}, u32[]{:S(2)}) collective-permute-start(bf16[21,16,2,192]{3,1,2,0:T(8,128)(2,1)S(1)} %get-tuple-element.3), channel_id=1, source_target_pairs={{4,0},{8,4},{12,8},{16,12},{20,16},{24,20},{28,24},{32,28},{36,32}... | collective-permute-start | bytes 774152 | tf_op jit(solution)/shard_map/ppermute | solution.py:20
  8.4 6.5 %reshape.36 = bf16[3,4,3,192,192]{4,3,1,2,0:T(8,128)(2,1)} reshape(bf16[3,4,3,36864]{3,1,2,0:T(4,128)(2,1)} %param.8) | data formatting | bytes 5308416 | tf_op jit(solution)/shard_map/reshape | solution.py:28
  15.1 0.7 gather_fusion
  16.1 1.7 %copy-done.3 = bf16[3,4,3,192,192]{4,3,1,2,0:T(8,128)(2,1)S(1)} copy-done((bf16[3,4,3,192,192]{4,3,1,2,0:T(8,128)(2,1)S(1)}, bf16[3,4,3,192,192]{4,3,1,2,0:T(8,128)(2,1)}, u32[]{:S(2)}) %copy-start.3) | copy-done | bytes 2654232
  17.8 0.6 fusion.10
  18.5 0.6 fusion.11
  19.1 0.6 fusion.9
  19.7 0.6 fusion.8
  20.3 1.9 %pad_maximum_fusion = bf16[3,21,16,4,192]{4,2,0,1,3:T(8,128)(2,1)} fusion(bf16[3,21,16,1,192]{4,2,0,1,3:T(8,128)(2,1)S(1)} %fusion.8, bf16[3,21,16,1,192]{4,2,0,1,3:T(8,128)(2,1)S(1)} %fusion.9, bf16[3,21,16,1,192]{4,2,0,1,3:T(8,128)(2,1)S(1)} %fusion.10, bf16[3,21,16,1,192]{4,2,0,1,3:T(8,128)(2,1)S(1)} %fusion.11), kind=kLoop, calls=%fused_computation.4 | loop fusion | flops 2322432 | bytes 3096576 | tf_op jit(solution)/shard_map/stack | solution.py:31
  22.2 4.4 %all-to-all-start = ((bf16[3,21,16,4,192]{4,2,0,1,3:T(8,128)(2,1)}), bf16[3,21,16,4,192]{4,2,0,1,3:T(8,128)(2,1)S(1)}, u32[]{:S(2)}, u32[]{:S(2)}) async-start(bf16[3,21,16,4,192]{4,2,0,1,3:T(8,128)(2,1)} %pad_maximum_fusion), calls=%async_computation | async-start | bytes 4128768 | tf_op jit(solution)/shard_map/all_to_all | solution.py:52
  26.6 26.5 %all-to-all-done = bf16[3,21,16,4,192]{4,2,0,1,3:T(8,128)(2,1)S(1)} async-done(((bf16[3,21,16,4,192]{4,2,0,1,3:T(8,128)(2,1)}), bf16[3,21,16,4,192]{4,2,0,1,3:T(8,128)(2,1)S(1)}, u32[]{:S(2)}, u32[]{:S(2)}) %all-to-all-start) | async-done | bytes 1548320 | tf_op jit(solution)/shard_map/all_to_all | solution.py:52
  53.1 1.4 %bitcast_reduce_fusion = f32[84,16,192]{2,0,1:T(8,128)S(1)} fusion(bf16[3,84,16,192]{3,2,0,1:T(8,128)(2,1)S(1)} %bitcast.130, bf16[1,3,84,84]{3,2,1,0:T(8,128)(2,1)S(1)} %get-tuple-element.5, bf16[1,3,84,84]{3,2,1,0:T(8,128)(2,1)S(1)} %get-tuple-element.6, bf16[1,3,84,84]{3,2,1,0:T(8,128)(2,1)S(1)} %get-tuple-element.4), kind=kOutput, calls=%fused_computation.1 | convolution fusion | flops 391065696 | bytes 2707488 | tf_op jit(solution)/shard_map/jkab,kblqn->jalqn/dot_general | solution.py:57
  54.6 1.5 %copy.38 = f32[84,16,1,192]{3,1,2,0:T(8,128)} copy(f32[84,16,1,192]{3,0,1,2:T(8,128)S(1)} %bitcast.131) | data formatting | bytes 2064384 | tf_op jit(solution)/shard_map/reduce_sum | solution.py:59
  56.1 3.9 %all-to-all-start.1 = ((f32[84,16,1,192]{3,1,2,0:T(8,128)}), f32[84,16,1,192]{3,1,2,0:T(8,128)S(1)}, u32[]{:S(2)}, u32[]{:S(2)}) async-start(f32[84,16,1,192]{3,1,2,0:T(8,128)} %copy.38), calls=%async_computation.1 | async-start | bytes 2752512 | tf_op jit(solution)/shard_map/all_to_all | solution.py:60
  60.6 0.8 %multiply_bitcast_fusion = bf16[4,192,4,192]{3,2,1,0:T(4,128)(2,1)S(1)} fusion(bf16[4,192,192]{1,2,0:T(8,128)(2,1)S(1)} %copy.40, bf16[4,4]{1,0:T(4,128)(2,1)S(1)} %fusion.21), kind=kLoop, calls=%fused_computation.7 | loop fusion | flops 589824 | bytes 1474592 | tf_op jit(solution)/shard_map/rim,rs->rmsi/transpose | solution.py:66
  61.5 2.3 %reshape.66 = bf16[768,768,1]{1,0,2:T(8,128)(2,1)} reshape(bf16[4,192,4,192]{3,2,1,0:T(4,128)(2,1)S(1)} %multiply_bitcast_fusion) | data formatting | bytes 2359296 | tf_op jit(solution)/shard_map/reshape | solution.py:66
  63.7 15.7 %all-to-all-done.1 = f32[84,16,1,192]{3,1,2,0:T(8,128)S(1)} async-done(((f32[84,16,1,192]{3,1,2,0:T(8,128)}), f32[84,16,1,192]{3,1,2,0:T(8,128)S(1)}, u32[]{:S(2)}, u32[]{:S(2)}) %all-to-all-start.1) | async-done | bytes 1032224 | tf_op jit(solution)/shard_map/all_to_all | solution.py:60
  79.5 1.0 %copy.39 = f32[21,16,4,1,192]{4,2,1,0,3:T(4,128)S(1)} copy(f32[21,16,4,1,192]{4,1,0,2,3:T(8,128)S(1)} %bitcast.129) | data formatting | bytes 2064384 | tf_op jit(solution)/shard_map/all_to_all | solution.py:60
  80.5 0.9 %reshape.38 = f32[21,16,768]{2,1,0:T(8,128)S(1)} reshape(f32[21,16,4,1,192]{4,2,1,0,3:T(4,128)S(1)} %copy.39) | data formatting | bytes 2064384 | tf_op jit(solution)/shard_map/reshape | solution.py:61
  81.4 1.5 %sub.11 = f32[21,16,768]{2,1,0:T(8,128)S(1)} subtract(f32[21,16,768]{2,1,0:T(8,128)} %param.7, f32[21,16,768]{2,1,0:T(8,128)S(1)} %reshape.38) | non-fusion elementwise | flops 258048 | bytes 3096576 | tf_op jit(solution)/shard_map/sub | solution.py:62
  83.3 1.5 %fusion.3 = f32[21,16,768]{2,1,0:T(8,128)} fusion(f32[21,16,768]{2,1,0:T(8,128)S(1)} %copy-done.2, bf16[768,768,1]{1,0,2:T(8,128)(2,1)S(1)} %copy-done, f32[21,16,768]{2,1,0:T(8,128)S(1)} %sub.11), kind=kOutput, calls=%fused_computation.10 | convolution fusion | flops 397135872 | bytes 4276224 | tf_op jit(solution)/shard_map/dot_general | solution.py:67
  (27 shorter events, 1.9 us)
Async XLA Ops:
  1.9 6.4 %copy-start.6 = (s32[4,3]{1,0:T(4,128)S(1)}, s32[4,3]{1,0:T(4,128)}, u32[]{:S(2)}) copy-start(s32[4,3]{1,0:T(4,128)} %param.10) | copy-start | bytes 148
  2.7 12.2 %collective-permute-start = (bf16[21,16,2,192]{3,1,2,0:T(8,128)(2,1)S(1)}, bf16[21,16,2,192]{3,1,2,0:T(8,128)(2,1)S(1)}, u32[]{:S(2)}, u32[]{:S(2)}) collective-permute-start(bf16[21,16,2,192]{3,1,2,0:T(8,128)(2,1)S(1)} %get-tuple-element.2), channel_id=1, source_target_pairs={{0,4},{4,8},{8,12},{12,16},{16,20},{20,24},{24,28},{28,32},{32,36}... | collective-permute-start | bytes 774152 | tf_op jit(solution)/shard_map/ppermute | solution.py:19
  4.6 10.2 %collective-permute-start.1 = (bf16[21,16,2,192]{3,1,2,0:T(8,128)(2,1)S(1)}, bf16[21,16,2,192]{3,1,2,0:T(8,128)(2,1)S(1)}, u32[]{:S(2)}, u32[]{:S(2)}) collective-permute-start(bf16[21,16,2,192]{3,1,2,0:T(8,128)(2,1)S(1)} %get-tuple-element.3), channel_id=1, source_target_pairs={{4,0},{8,4},{12,8},{16,12},{20,16},{24,20},{28,24},{32,28},{36,32}... | collective-permute-start | bytes 774152 | tf_op jit(solution)/shard_map/ppermute | solution.py:20
  15.8 2.0 %copy-start.3 = (bf16[3,4,3,192,192]{4,3,1,2,0:T(8,128)(2,1)S(1)}, bf16[3,4,3,192,192]{4,3,1,2,0:T(8,128)(2,1)}, u32[]{:S(2)}) copy-start(bf16[3,4,3,192,192]{4,3,1,2,0:T(8,128)(2,1)} %reshape.36) | copy-start | bytes 7962628
  22.2 4.4 %copy-start.5 = (f32[3,84,84]{2,1,0:T(8,128)S(1)}, f32[3,84,84]{2,1,0:T(8,128)}, u32[]{:S(2)}) copy-start(f32[3,84,84]{2,1,0:T(8,128)} %param.11) | copy-start | bytes 254020
  22.2 31.0 %all-to-all-start = ((bf16[3,21,16,4,192]{4,2,0,1,3:T(8,128)(2,1)}), bf16[3,21,16,4,192]{4,2,0,1,3:T(8,128)(2,1)S(1)}, u32[]{:S(2)}, u32[]{:S(2)}) async-start(bf16[3,21,16,4,192]{4,2,0,1,3:T(8,128)(2,1)} %pad_maximum_fusion), calls=%async_computation | async-start | bytes 4128768 | tf_op jit(solution)/shard_map/all_to_all | solution.py:52
  56.1 3.9 %copy-start.4 = (bf16[4,36864]{1,0:T(4,128)(2,1)S(1)}, bf16[4,36864]{1,0:T(4,128)(2,1)}, u32[]{:S(2)}) copy-start(bf16[4,36864]{1,0:T(4,128)(2,1)} %param.9) | copy-start | bytes 884740
  56.1 23.4 %all-to-all-start.1 = ((f32[84,16,1,192]{3,1,2,0:T(8,128)}), f32[84,16,1,192]{3,1,2,0:T(8,128)S(1)}, u32[]{:S(2)}, u32[]{:S(2)}) async-start(f32[84,16,1,192]{3,1,2,0:T(8,128)} %copy.38), calls=%async_computation.1 | async-start | bytes 2752512 | tf_op jit(solution)/shard_map/all_to_all | solution.py:60
  81.4 1.6 %copy-start = (bf16[768,768,1]{1,0,2:T(8,128)(2,1)S(1)}, bf16[768,768,1]{1,0,2:T(8,128)(2,1)}, u32[]{:S(2)}) copy-start(bf16[768,768,1]{1,0,2:T(8,128)(2,1)} %reshape.66) | copy-start | bytes 3538948
  81.4 1.9 %copy-start.2 = (f32[21,16,768]{2,1,0:T(8,128)S(1)}, f32[21,16,768]{2,1,0:T(8,128)}, u32[]{:S(2)}) copy-start(f32[21,16,768]{2,1,0:T(8,128)} %param.6) | copy-start | bytes 3096580
  83.3 1.5 %copy-start.1 = (f32[21,16,768]{2,1,0:T(8,128)}, f32[21,16,768]{2,1,0:T(8,128)S(1)}, u32[]{:S(2)}) copy-start(f32[21,16,768]{2,1,0:T(8,128)S(1)} %sub.11) | copy-start | bytes 3096580

commit v14 on v13

--- a/solution.py
+++ b/solution.py
@@ -37,8 +37,7 @@
                 preferred_element_type=jnp.float32,
             )
             for r in range(shaped.shape[1])
-        ],
-        axis=3,
+        ]
     )
 
 
@@ -49,14 +48,16 @@
     rounded = iterate.astype(jnp.bfloat16).reshape(modes_here, loads, block_count, block_size)
     extended = padded(rounded, (("space", 2),), H)
     products = stiffness(extended, tiles, columns).astype(jnp.bfloat16)
-    exchanged = lax.all_to_all(products, "mode", split_axis=3, concat_axis=1, tiled=True)
+    exchanged = lax.all_to_all(products, "mode", split_axis=0, concat_axis=0, tiled=True)
+    sources = lax.axis_size("mode")
     high = lax.reduce_precision(coupling, exponent_bits=8, mantissa_bits=7)
     rest = coupling - high
     middle = lax.reduce_precision(rest, exponent_bits=8, mantissa_bits=7)
     pieces = jnp.stack([high, middle, rest - middle]).astype(jnp.bfloat16)
+    pieces = pieces.reshape(pieces.shape[:3] + (sources, modes_here))
     mixture = jnp.einsum(
-        "jkab,kblqn->jalqn", pieces, exchanged, preferred_element_type=jnp.float32
-    ).sum(axis=0)
+        "jkaSp,Skpli->jali", pieces, exchanged, preferred_element_type=jnp.float32
+    ).sum(axis=0)[:, :, None, :]
     applied = lax.all_to_all(mixture, "mode", split_axis=0, concat_axis=2, tiled=True)
     applied = applied.reshape(modes_here, loads, dofs_here)
     residual = forcing - applied

time: 85.6 us -> 85.6 us (level)
    reduce_sum x1 -> x0, local copies, waits for them, and re-layouts: 1.52 us -> none  [body(): mixture = jnp.einsum('jkab,kblqn->jalqn', pieces, exchanged, preferred_el...]
    broadcast_in_dim x0 -> x1, local copies, waits for them, and re-layouts: none -> 1.52 us  [body(): jnp.einsum('jkaSp,Skpli->jali', pieces, exchanged, preferred_element_type...]
  transfers between devices with their start and end apart: 4 -> 4, of which waited for: 2 -> 2; matrix products, arithmetic and copies ran while one was open for 12% -> 13% of each run, Pallas kernels for 0% -> 0%
where the time goes in v14:
time: 85.6 us; the launch traced here: 84.8 us
  waiting for transfers between devices  41.7 us (49%)
  local copies, waits for them, and re-layouts  17 us (20%)
  starting transfers between devices  13.8 us (16%)
  other arithmetic  6.06 us (7%)
  matrix products  5.37 us (6%)
  between operations  0.87 us (1%)
    all_to_all x1, waiting for transfers between devices, body(): lax.all_to_all(products, 'mode', split_axis=0, concat_axis=0, tiled=True)  26 us
    all_to_all x1, waiting for transfers between devices, body(): lax.all_to_all(mixture, 'mode', split_axis=0, concat_axis=2, tiled=True)  15.7 us
    reshape x1, local copies, waits for them, and re-layouts, stiffness(): tile_rows.reshape(tile_rows.shape[0], tile_rows.shape[1], tile_rows.shape...  6.46 us
    all_to_all x1, starting transfers between devices, body(): lax.all_to_all(products, 'mode', split_axis=0, concat_axis=0, tiled=True)  4.43 us
    all_to_all x1, starting transfers between devices, body(): lax.all_to_all(mixture, 'mode', split_axis=0, concat_axis=2, tiled=True)  3.86 us
    ppermute x1, starting transfers between devices, padded(): after = lax.ppermute(initial, axis, down)  3.64 us
    dot_general x4, matrix products, stiffness(): jnp.einsum('ksim,plsm->kpli', shaped[:, r], picked[:, :, r], preferred_el...  2.43 us
    reshape x1, local copies, waits for them, and re-layouts, body(): jnp.einsum('rim,rs->rmsi', inverse, diagonal).reshape(dofs_here, dofs_here)  2.26 us
  transfers between devices with their start and end apart: 4, of which 2 were waited for; matrix products, arithmetic and copies ran while one was open for 13% of the time, Pallas kernels for 0%

profile of v14, /device:TPU:56, one launch (start us, length us, event | category | flops | bytes accessed | tf_op | source)
XLA Modules:
  0.0 84.8 jit_solution(8648102792600090930)
XLA Ops:
  0.6 1.3 %convert_element_type.10 = bf16[21,16,768]{2,1,0:T(8,128)(2,1)S(1)} convert(f32[21,16,768]{2,1,0:T(8,128)} %param.6) | non-fusion elementwise | flops 258048 | bytes 1548288 | tf_op jit(solution)/shard_map/convert_element_type | solution.py:48
  1.9 0.6 reshape.39
  2.7 1.9 %collective-permute-start = (bf16[21,16,2,192]{3,1,2,0:T(8,128)(2,1)S(1)}, bf16[21,16,2,192]{3,1,2,0:T(8,128)(2,1)S(1)}, u32[]{:S(2)}, u32[]{:S(2)}) collective-permute-start(bf16[21,16,2,192]{3,1,2,0:T(8,128)(2,1)S(1)} %get-tuple-element.2), channel_id=1, source_target_pairs={{0,4},{4,8},{8,12},{12,16},{16,20},{20,24},{24,28},{28,32},{32,36}... | collective-permute-start | bytes 774152 | tf_op jit(solution)/shard_map/ppermute | solution.py:19
  4.6 3.6 %collective-permute-start.1 = (bf16[21,16,2,192]{3,1,2,0:T(8,128)(2,1)S(1)}, bf16[21,16,2,192]{3,1,2,0:T(8,128)(2,1)S(1)}, u32[]{:S(2)}, u32[]{:S(2)}) collective-permute-start(bf16[21,16,2,192]{3,1,2,0:T(8,128)(2,1)S(1)} %get-tuple-element.3), channel_id=1, source_target_pairs={{4,0},{8,4},{12,8},{16,12},{20,16},{24,20},{28,24},{32,28},{36,32}... | collective-permute-start | bytes 774152 | tf_op jit(solution)/shard_map/ppermute | solution.py:20
  8.4 6.5 %reshape.40 = bf16[3,4,3,192,192]{4,3,1,2,0:T(8,128)(2,1)} reshape(bf16[3,4,3,36864]{3,1,2,0:T(4,128)(2,1)} %param.8) | data formatting | bytes 5308416 | tf_op jit(solution)/shard_map/reshape | solution.py:28
  15.1 0.7 gather_fusion
  16.1 1.7 %copy-done.3 = bf16[3,4,3,192,192]{4,3,1,2,0:T(8,128)(2,1)S(1)} copy-done((bf16[3,4,3,192,192]{4,3,1,2,0:T(8,128)(2,1)S(1)}, bf16[3,4,3,192,192]{4,3,1,2,0:T(8,128)(2,1)}, u32[]{:S(2)}) %copy-start.3) | copy-done | bytes 2654232
  17.8 0.6 fusion.13
  18.5 0.6 fusion.14
  19.1 0.6 fusion.12
  19.7 0.6 fusion.11
  20.3 1.9 %pad_maximum_fusion = bf16[4,3,21,16,192]{4,3,1,2,0:T(8,128)(2,1)} fusion(bf16[1,3,21,16,192]{4,3,1,2,0:T(8,128)(2,1)S(1)} %fusion.11, bf16[1,3,21,16,192]{4,3,1,2,0:T(8,128)(2,1)S(1)} %fusion.12, bf16[1,3,21,16,192]{4,3,1,2,0:T(8,128)(2,1)S(1)} %fusion.13, bf16[1,3,21,16,192]{4,3,1,2,0:T(8,128)(2,1)S(1)} %fusion.14), kind=kLoop, calls=%fused_computation.5 | loop fusion | flops 2322432 | bytes 3096576 | tf_op jit(solution)/shard_map/stack | solution.py:31
  22.2 4.4 %all-to-all-start = ((bf16[4,3,21,16,192]{4,3,1,2,0:T(8,128)(2,1)}), bf16[4,3,21,16,192]{4,3,1,2,0:T(8,128)(2,1)S(1)}, u32[]{:S(2)}, u32[]{:S(2)}) async-start(bf16[4,3,21,16,192]{4,3,1,2,0:T(8,128)(2,1)} %pad_maximum_fusion), calls=%async_computation | async-start | bytes 4128768 | tf_op jit(solution)/shard_map/all_to_all | solution.py:51
  27.2 26.0 %all-to-all-done = bf16[4,3,21,16,192]{4,3,1,2,0:T(8,128)(2,1)S(1)} async-done(((bf16[4,3,21,16,192]{4,3,1,2,0:T(8,128)(2,1)}), bf16[4,3,21,16,192]{4,3,1,2,0:T(8,128)(2,1)S(1)}, u32[]{:S(2)}, u32[]{:S(2)}) %all-to-all-start) | async-done | bytes 1548320 | tf_op jit(solution)/shard_map/all_to_all | solution.py:51
  53.2 1.4 %bitcast_reduce_fusion = f32[84,16,192]{2,0,1:T(8,128)S(1)} fusion(bf16[4,3,21,16,192]{4,3,1,2,0:T(8,128)(2,1)S(1)} %all-to-all-done, bf16[1,3,84,4,21]{2,4,3,1,0:T(8,128)(2,1)S(1)} %stack.34, bf16[1,3,84,4,21]{2,4,3,1,0:T(8,128)(2,1)S(1)} %stack.33, bf16[1,3,84,4,21]{2,4,3,1,0:T(8,128)(2,1)S(1)} %stack.32), kind=kOutput, calls=%fused_computation.1 | convolution fusion | flops 390811680 | bytes 2707488 | tf_op jit(solution)/shard_map/jkaSp,Skpli->jali/dot_general | solution.py:58
  54.6 1.5 %copy.56 = f32[84,16,1,192]{3,1,2,0:T(8,128)} copy(f32[84,16,1,192]{3,0,1,2:T(8,128)S(1)} %bitcast.126) | data formatting | bytes 2064384 | tf_op jit(solution)/shard_map/broadcast_in_dim | solution.py:58
  56.1 3.9 %all-to-all-start.1 = ((f32[84,16,1,192]{3,1,2,0:T(8,128)}), f32[84,16,1,192]{3,1,2,0:T(8,128)S(1)}, u32[]{:S(2)}, u32[]{:S(2)}) async-start(f32[84,16,1,192]{3,1,2,0:T(8,128)} %copy.56), calls=%async_computation.1 | async-start | bytes 2752512 | tf_op jit(solution)/shard_map/all_to_all | solution.py:61
  60.6 0.8 %multiply_bitcast_fusion = bf16[4,192,4,192]{3,2,1,0:T(4,128)(2,1)S(1)} fusion(bf16[4,192,192]{1,2,0:T(8,128)(2,1)S(1)} %copy.58, bf16[4,4]{1,0:T(4,128)(2,1)S(1)} %fusion.18), kind=kLoop, calls=%fused_computation.8 | loop fusion | flops 589824 | bytes 1474592 | tf_op jit(solution)/shard_map/rim,rs->rmsi/transpose | solution.py:67
  61.5 2.3 %reshape.69 = bf16[768,768,1]{1,0,2:T(8,128)(2,1)} reshape(bf16[4,192,4,192]{3,2,1,0:T(4,128)(2,1)S(1)} %multiply_bitcast_fusion) | data formatting | bytes 2359296 | tf_op jit(solution)/shard_map/reshape | solution.py:67
  63.7 15.7 %all-to-all-done.1 = f32[84,16,1,192]{3,1,2,0:T(8,128)S(1)} async-done(((f32[84,16,1,192]{3,1,2,0:T(8,128)}), f32[84,16,1,192]{3,1,2,0:T(8,128)S(1)}, u32[]{:S(2)}, u32[]{:S(2)}) %all-to-all-start.1) | async-done | bytes 1032224 | tf_op jit(solution)/shard_map/all_to_all | solution.py:61
  79.4 1.0 %copy.57 = f32[21,16,4,1,192]{4,2,1,0,3:T(4,128)S(1)} copy(f32[21,16,4,1,192]{4,1,0,2,3:T(8,128)S(1)} %bitcast.127) | data formatting | bytes 2064384 | tf_op jit(solution)/shard_map/all_to_all | solution.py:61
  80.5 0.9 %reshape.41 = f32[21,16,768]{2,1,0:T(8,128)S(1)} reshape(f32[21,16,4,1,192]{4,2,1,0,3:T(4,128)S(1)} %copy.57) | data formatting | bytes 2064384 | tf_op jit(solution)/shard_map/reshape | solution.py:62
  81.4 1.5 %sub.11 = f32[21,16,768]{2,1,0:T(8,128)S(1)} subtract(f32[21,16,768]{2,1,0:T(8,128)} %param.7, f32[21,16,768]{2,1,0:T(8,128)S(1)} %reshape.41) | non-fusion elementwise | flops 258048 | bytes 3096576 | tf_op jit(solution)/shard_map/sub | solution.py:63
  83.3 1.5 %fusion.4 = f32[21,16,768]{2,1,0:T(8,128)} fusion(f32[21,16,768]{2,1,0:T(8,128)S(1)} %copy-done.2, bf16[768,768,1]{1,0,2:T(8,128)(2,1)S(1)} %copy-done, f32[21,16,768]{2,1,0:T(8,128)S(1)} %sub.11), kind=kOutput, calls=%fused_computation.11 | convolution fusion | flops 397135872 | bytes 4276224 | tf_op jit(solution)/shard_map/dot_general | solution.py:68
  (33 shorter events, 2.4 us)
Async XLA Ops:
  1.9 6.4 %copy-start.6 = (s32[4,3]{1,0:T(4,128)S(1)}, s32[4,3]{1,0:T(4,128)}, u32[]{:S(2)}) copy-start(s32[4,3]{1,0:T(4,128)} %param.10) | copy-start | bytes 148
  2.7 12.2 %collective-permute-start = (bf16[21,16,2,192]{3,1,2,0:T(8,128)(2,1)S(1)}, bf16[21,16,2,192]{3,1,2,0:T(8,128)(2,1)S(1)}, u32[]{:S(2)}, u32[]{:S(2)}) collective-permute-start(bf16[21,16,2,192]{3,1,2,0:T(8,128)(2,1)S(1)} %get-tuple-element.2), channel_id=1, source_target_pairs={{0,4},{4,8},{8,12},{12,16},{16,20},{20,24},{24,28},{28,32},{32,36}... | collective-permute-start | bytes 774152 | tf_op jit(solution)/shard_map/ppermute | solution.py:19
  4.6 10.2 %collective-permute-start.1 = (bf16[21,16,2,192]{3,1,2,0:T(8,128)(2,1)S(1)}, bf16[21,16,2,192]{3,1,2,0:T(8,128)(2,1)S(1)}, u32[]{:S(2)}, u32[]{:S(2)}) collective-permute-start(bf16[21,16,2,192]{3,1,2,0:T(8,128)(2,1)S(1)} %get-tuple-element.3), channel_id=1, source_target_pairs={{4,0},{8,4},{12,8},{16,12},{20,16},{24,20},{28,24},{32,28},{36,32}... | collective-permute-start | bytes 774152 | tf_op jit(solution)/shard_map/ppermute | solution.py:20
  15.8 2.0 %copy-start.3 = (bf16[3,4,3,192,192]{4,3,1,2,0:T(8,128)(2,1)S(1)}, bf16[3,4,3,192,192]{4,3,1,2,0:T(8,128)(2,1)}, u32[]{:S(2)}) copy-start(bf16[3,4,3,192,192]{4,3,1,2,0:T(8,128)(2,1)} %reshape.40) | copy-start | bytes 7962628
  22.2 4.4 %copy-start.5 = (f32[3,84,84]{2,1,0:T(8,128)S(1)}, f32[3,84,84]{2,1,0:T(8,128)}, u32[]{:S(2)}) copy-start(f32[3,84,84]{2,1,0:T(8,128)} %param.11) | copy-start | bytes 254020
  22.2 31.0 %all-to-all-start = ((bf16[4,3,21,16,192]{4,3,1,2,0:T(8,128)(2,1)}), bf16[4,3,21,16,192]{4,3,1,2,0:T(8,128)(2,1)S(1)}, u32[]{:S(2)}, u32[]{:S(2)}) async-start(bf16[4,3,21,16,192]{4,3,1,2,0:T(8,128)(2,1)} %pad_maximum_fusion), calls=%async_computation | async-start | bytes 4128768 | tf_op jit(solution)/shard_map/all_to_all | solution.py:51
  56.1 3.9 %copy-start.4 = (bf16[4,36864]{1,0:T(4,128)(2,1)S(1)}, bf16[4,36864]{1,0:T(4,128)(2,1)}, u32[]{:S(2)}) copy-start(bf16[4,36864]{1,0:T(4,128)(2,1)} %param.9) | copy-start | bytes 884740
  56.1 23.4 %all-to-all-start.1 = ((f32[84,16,1,192]{3,1,2,0:T(8,128)}), f32[84,16,1,192]{3,1,2,0:T(8,128)S(1)}, u32[]{:S(2)}, u32[]{:S(2)}) async-start(f32[84,16,1,192]{3,1,2,0:T(8,128)} %copy.56), calls=%async_computation.1 | async-start | bytes 2752512 | tf_op jit(solution)/shard_map/all_to_all | solution.py:61
  81.4 1.6 %copy-start = (bf16[768,768,1]{1,0,2:T(8,128)(2,1)S(1)}, bf16[768,768,1]{1,0,2:T(8,128)(2,1)}, u32[]{:S(2)}) copy-start(bf16[768,768,1]{1,0,2:T(8,128)(2,1)} %reshape.69) | copy-start | bytes 3538948
  81.4 1.9 %copy-start.2 = (f32[21,16,768]{2,1,0:T(8,128)S(1)}, f32[21,16,768]{2,1,0:T(8,128)}, u32[]{:S(2)}) copy-start(f32[21,16,768]{2,1,0:T(8,128)} %param.6) | copy-start | bytes 3096580
  83.3 1.5 %copy-start.1 = (f32[21,16,768]{2,1,0:T(8,128)}, f32[21,16,768]{2,1,0:T(8,128)S(1)}, u32[]{:S(2)}) copy-start(f32[21,16,768]{2,1,0:T(8,128)S(1)} %sub.11) | copy-start | bytes 3096580

commit v15 on v11

--- a/solution.py
+++ b/solution.py
@@ -9,13 +9,16 @@
 RELAXATION = 0.7
 
 
-def padded(x, sides, width):
+def padded(x, sides, width, source):
     for axis, dim in sides:
         devices, length = (lax.axis_size(axis), x.shape[dim])
         up = [(i, (i + 1) % devices) for i in range(devices)]
         down = [(j, i) for i, j in up]
-        last = lax.slice_in_dim(x, length - width, length, axis=dim)
-        initial = lax.slice_in_dim(x, 0, width, axis=dim)
+        dofs = source.shape[-1]
+        edge = width * x.shape[-1]
+        shape = x.shape[:dim] + (width,) + x.shape[dim + 1:]
+        last = source[..., dofs - edge:].astype(x.dtype).reshape(shape)
+        initial = source[..., :edge].astype(x.dtype).reshape(shape)
         before = lax.ppermute(last, axis, up)
         after = lax.ppermute(initial, axis, down)
         x = jnp.concatenate([before, x, after], axis=dim)
@@ -36,7 +39,7 @@
     terms, block_count = (tiles.shape[0], tiles.shape[1])
     block_size = dofs_here // block_count
     rounded = iterate.astype(jnp.bfloat16).reshape(modes_here, loads, block_count, block_size)
-    extended = padded(rounded, (("space", 2),), H)
+    extended = padded(rounded, (("space", 2),), H, iterate)
     products = stiffness(extended, tiles, columns).astype(jnp.bfloat16)
     exchanged = lax.all_to_all(products, "mode", split_axis=3, concat_axis=1, tiled=True)
     high = lax.reduce_precision(coupling, exponent_bits=8, mantissa_bits=7)

time: 84.4 us -> 86.7 us (1.027)
  local copies, waits for them, and re-layouts: 14.7 us -> 16 us
  other arithmetic: 3.94 us -> 5.02 us
    another operation x1 -> x2, other arithmetic: 0.01 us -> 1.28 us
    convert_element_type x1 -> x0, other arithmetic: 1.28 us -> none  [body(): iterate.astype(jnp.bfloat16)]
    concatenate x1, other arithmetic: 0.26 us -> 1.34 us  [padded(): x = jnp.concatenate([before, x, after], axis=dim)]
    all_to_all x1, waiting for transfers between devices: 15.9 us -> 14.9 us  [body(): lax.all_to_all(mixture, 'mode', split_axis=0, concat_axis=2, tiled=True)]
  transfers between devices with their start and end apart: 4 -> 4, of which waited for: 2 -> 2; matrix products, arithmetic and copies ran while one was open for 12% -> 13% of each run, Pallas kernels for 0% -> 0%
where the time goes in v15:
time: 86.7 us; the launch traced here: 85.4 us
  waiting for transfers between devices  41.8 us (48%)
  local copies, waits for them, and re-layouts  16 us (18%)
  starting transfers between devices  13.7 us (16%)
  matrix products  8.12 us (9%)
  other arithmetic  5.02 us (6%)
    all_to_all x1, waiting for transfers between devices, body(): lax.all_to_all(products, 'mode', split_axis=3, concat_axis=1, tiled=True)  26.9 us
    all_to_all x1, waiting for transfers between devices, body(): lax.all_to_all(mixture, 'mode', split_axis=0, concat_axis=2, tiled=True)  14.9 us
    reshape x1, local copies, waits for them, and re-layouts, stiffness(): tile_rows.reshape(tile_rows.shape[0], tile_rows.shape[1], tile_rows.shape...  6.47 us
    dot_general x1, matrix products, stiffness(): jnp.einsum('krsim,plrsm->kplri', shaped, picked, preferred_element_type=j...  5.15 us
    all_to_all x1, starting transfers between devices, body(): lax.all_to_all(products, 'mode', split_axis=3, concat_axis=1, tiled=True)  4.43 us
    all_to_all x1, starting transfers between devices, body(): lax.all_to_all(mixture, 'mode', split_axis=0, concat_axis=2, tiled=True)  3.68 us
    ppermute x1, starting transfers between devices, padded(): after = lax.ppermute(initial, axis, down)  3.64 us
    reshape x1, local copies, waits for them, and re-layouts, body(): jnp.einsum('rim,rs->rmsi', inverse, diagonal).reshape(dofs_here, dofs_here)  2.26 us
  transfers between devices with their start and end apart: 4, of which 2 were waited for; matrix products, arithmetic and copies ran while one was open for 13% of the time, Pallas kernels for 0%

profile of v15, /device:TPU:56, one launch (start us, length us, event | category | flops | bytes accessed | tf_op | source)
XLA Modules:
  0.0 85.4 jit_solution(7573097392738629541)
XLA Ops:
  0.6 1.3 %convert.22 = bf16[21,16,768]{2,1,0:T(8,128)(2,1)S(1)} convert(f32[21,16,768]{2,1,0:T(8,128)} %param.6) | non-fusion elementwise | flops 258048 | bytes 1548288 | tf_op jit(solution)/shard_map/convert.2
  2.2 1.9 %collective-permute-start = (bf16[21,16,2,192]{3,1,2,0:T(8,128)(2,1)S(1)}, bf16[21,16,2,192]{3,1,2,0:T(8,128)(2,1)S(1)}, u32[]{:S(2)}, u32[]{:S(2)}) collective-permute-start(bf16[21,16,2,192]{3,1,2,0:T(8,128)(2,1)S(1)} %copy.23), channel_id=1, source_target_pairs={{0,4},{4,8},{8,12},{12,16},{16,20},{20,24},{24,28},{28,32},{32,36}... | collective-permute-start | bytes 774152 | tf_op jit(solution)/shard_map/ppermute | solution.py:22
  4.4 3.6 %collective-permute-start.1 = (bf16[21,16,2,192]{3,1,2,0:T(8,128)(2,1)S(1)}, bf16[21,16,2,192]{3,1,2,0:T(8,128)(2,1)}, u32[]{:S(2)}, u32[]{:S(2)}) collective-permute-start(bf16[21,16,2,192]{3,1,2,0:T(8,128)(2,1)S(1)} %copy.24), channel_id=1, source_target_pairs={{4,0},{8,4},{12,8},{16,12},{20,16},{24,20},{28,24},{32,28},{36,32}... | collective-permute-start | bytes 774152 | tf_op jit(solution)/shard_map/ppermute | solution.py:23
  8.2 0.6 reshape.42
  8.9 6.5 %reshape.44 = bf16[3,4,3,192,192]{4,3,1,2,0:T(8,128)(2,1)} reshape(bf16[3,4,3,36864]{3,1,2,0:T(4,128)(2,1)} %param.8) | data formatting | bytes 5308416 | tf_op jit(solution)/shard_map/reshape | solution.py:31
  15.4 0.7 copy-done.3
  16.1 1.3 %pad_maximum_fusion = bf16[21,16,8,192]{3,1,2,0:T(8,128)(2,1)S(1)} fusion(bf16[21,16,2,192]{3,1,2,0:T(8,128)(2,1)} %collective-permute-done.1, bf16[21,16,4,192]{3,1,2,0:T(8,128)(2,1)S(1)} %copy.25, bf16[21,16,2,192]{3,1,2,0:T(8,128)(2,1)} %copy-done.3), kind=kLoop, calls=%fused_computation.11 | loop fusion | flops 1032192 | bytes 2064384 | tf_op jit(solution)/shard_map/concatenate | solution.py:24
  17.5 0.7 gather_fusion
  18.2 5.2 %fusion.4 = bf16[3,21,16,4,192]{4,2,0,1,3:T(8,128)(2,1)} fusion(bf16[3,4,3,192,192]{4,3,1,2,0:T(8,128)(2,1)} %reshape.44, bf16[4,3,21,16,192]{4,3,2,1,0:T(8,128)(2,1)S(1)} %bitcast.52, pred[4,3]{1,0:T(4,128)(4,1)S(1)} %compare_and_fusion), kind=kOutput, calls=%fused_computation.7 | convolution fusion | flops 893362176 | bytes 5750796 | tf_op jit(solution)/shard_map/krsim,plrsm->kplri/dot_general | solution.py:34
  23.3 4.4 %all-to-all-start = ((bf16[3,21,16,4,192]{4,2,0,1,3:T(8,128)(2,1)}), bf16[3,21,16,4,192]{4,2,0,1,3:T(8,128)(2,1)S(1)}, u32[]{:S(2)}, u32[]{:S(2)}) async-start(bf16[3,21,16,4,192]{4,2,0,1,3:T(8,128)(2,1)} %fusion.4), calls=%async_computation | async-start | bytes 4128768 | tf_op jit(solution)/shard_map/all_to_all | solution.py:44
  27.8 26.9 %all-to-all-done = bf16[3,21,16,4,192]{4,2,0,1,3:T(8,128)(2,1)S(1)} async-done(((bf16[3,21,16,4,192]{4,2,0,1,3:T(8,128)(2,1)}), bf16[3,21,16,4,192]{4,2,0,1,3:T(8,128)(2,1)S(1)}, u32[]{:S(2)}, u32[]{:S(2)}) %all-to-all-start) | async-done | bytes 1548320 | tf_op jit(solution)/shard_map/all_to_all | solution.py:44
  54.7 1.4 %bitcast_reduce_fusion = f32[84,16,192]{2,0,1:T(8,128)S(1)} fusion(bf16[3,84,16,192]{3,2,0,1:T(8,128)(2,1)S(1)} %bitcast.53, bf16[1,3,84,84]{3,2,1,0:T(8,128)(2,1)S(1)} %get-tuple-element.5, bf16[1,3,84,84]{3,2,1,0:T(8,128)(2,1)S(1)} %get-tuple-element.6, bf16[1,3,84,84]{3,2,1,0:T(8,128)(2,1)S(1)} %get-tuple-element.4), kind=kOutput, calls=%fused_computation.1 | convolution fusion | flops 391065696 | bytes 2707488 | tf_op jit(solution)/shard_map/jkab,kblqn->jalqn/dot_general | solution.py:49
  56.1 1.5 %copy.29 = f32[84,16,1,192]{3,1,2,0:T(8,128)} copy(f32[84,16,1,192]{3,0,1,2:T(8,128)S(1)} %bitcast.54) | data formatting | bytes 2064384 | tf_op jit(solution)/shard_map/reduce_sum | solution.py:51
  57.6 3.7 %all-to-all-start.1 = ((f32[84,16,1,192]{3,1,2,0:T(8,128)}), f32[84,16,1,192]{3,1,2,0:T(8,128)S(1)}, u32[]{:S(2)}, u32[]{:S(2)}) async-start(f32[84,16,1,192]{3,1,2,0:T(8,128)} %copy.29), calls=%async_computation.1 | async-start | bytes 2752512 | tf_op jit(solution)/shard_map/all_to_all | solution.py:52
  61.3 0.4 reshape.47
  61.8 0.2 copy.31
  62.0 0.8 multiply_bitcast_fusion
  62.8 2.3 %reshape.65 = bf16[768,768,1]{1,0,2:T(8,128)(2,1)} reshape(bf16[4,192,4,192]{3,2,1,0:T(4,128)(2,1)S(1)} %multiply_bitcast_fusion) | data formatting | bytes 2359296 | tf_op jit(solution)/shard_map/reshape | solution.py:58
  65.1 14.9 %all-to-all-done.1 = f32[84,16,1,192]{3,1,2,0:T(8,128)S(1)} async-done(((f32[84,16,1,192]{3,1,2,0:T(8,128)}), f32[84,16,1,192]{3,1,2,0:T(8,128)S(1)}, u32[]{:S(2)}, u32[]{:S(2)}) %all-to-all-start.1) | async-done | bytes 1032224 | tf_op jit(solution)/shard_map/all_to_all | solution.py:52
  80.0 1.0 %copy.30 = f32[21,16,4,1,192]{4,2,1,0,3:T(4,128)S(1)} copy(f32[21,16,4,1,192]{4,1,0,2,3:T(8,128)S(1)} %bitcast.51) | data formatting | bytes 2064384 | tf_op jit(solution)/shard_map/all_to_all | solution.py:52
  81.1 0.9 %reshape.46 = f32[21,16,768]{2,1,0:T(8,128)S(1)} reshape(f32[21,16,4,1,192]{4,2,1,0,3:T(4,128)S(1)} %copy.30) | data formatting | bytes 2064384 | tf_op jit(solution)/shard_map/reshape | solution.py:53
  82.0 1.5 %sub.11 = f32[21,16,768]{2,1,0:T(8,128)S(1)} subtract(f32[21,16,768]{2,1,0:T(8,128)} %param.7, f32[21,16,768]{2,1,0:T(8,128)S(1)} %reshape.46) | non-fusion elementwise | flops 258048 | bytes 3096576 | tf_op jit(solution)/shard_map/sub | solution.py:54
  83.5 0.3 copy-done.2
  83.9 1.5 %fusion.10 = f32[21,16,768]{2,1,0:T(8,128)} fusion(f32[21,16,768]{2,1,0:T(8,128)S(1)} %copy-done.2, bf16[768,768,1]{1,0,2:T(8,128)(2,1)S(1)} %copy-done, f32[21,16,768]{2,1,0:T(8,128)S(1)} %sub.11), kind=kOutput, calls=%fused_computation.13 | convolution fusion | flops 397135872 | bytes 4276224 | tf_op jit(solution)/shard_map/dot_general | solution.py:59
  (26 shorter events, 0.9 us)
Async XLA Ops:
  1.9 6.2 %copy-start.6 = (s32[4,3]{1,0:T(4,128)S(1)}, s32[4,3]{1,0:T(4,128)}, u32[]{:S(2)}) copy-start(s32[4,3]{1,0:T(4,128)} %param.10) | copy-start | bytes 148
  2.2 13.2 %collective-permute-start = (bf16[21,16,2,192]{3,1,2,0:T(8,128)(2,1)S(1)}, bf16[21,16,2,192]{3,1,2,0:T(8,128)(2,1)S(1)}, u32[]{:S(2)}, u32[]{:S(2)}) collective-permute-start(bf16[21,16,2,192]{3,1,2,0:T(8,128)(2,1)S(1)} %copy.23), channel_id=1, source_target_pairs={{0,4},{4,8},{8,12},{12,16},{16,20},{20,24},{24,28},{28,32},{32,36}... | collective-permute-start | bytes 774152 | tf_op jit(solution)/shard_map/ppermute | solution.py:22
  4.4 11.7 %collective-permute-start.1 = (bf16[21,16,2,192]{3,1,2,0:T(8,128)(2,1)S(1)}, bf16[21,16,2,192]{3,1,2,0:T(8,128)(2,1)}, u32[]{:S(2)}, u32[]{:S(2)}) collective-permute-start(bf16[21,16,2,192]{3,1,2,0:T(8,128)(2,1)S(1)} %copy.24), channel_id=1, source_target_pairs={{4,0},{8,4},{12,8},{16,12},{20,16},{24,20},{28,24},{32,28},{36,32}... | collective-permute-start | bytes 774152 | tf_op jit(solution)/shard_map/ppermute | solution.py:23
  15.4 0.7 copy-start.3
  23.3 4.4 %copy-start.5 = (f32[3,84,84]{2,1,0:T(8,128)S(1)}, f32[3,84,84]{2,1,0:T(8,128)}, u32[]{:S(2)}) copy-start(f32[3,84,84]{2,1,0:T(8,128)} %param.11) | copy-start | bytes 254020
  23.3 31.3 %all-to-all-start = ((bf16[3,21,16,4,192]{4,2,0,1,3:T(8,128)(2,1)}), bf16[3,21,16,4,192]{4,2,0,1,3:T(8,128)(2,1)S(1)}, u32[]{:S(2)}, u32[]{:S(2)}) async-start(bf16[3,21,16,4,192]{4,2,0,1,3:T(8,128)(2,1)} %fusion.4), calls=%async_computation | async-start | bytes 4128768 | tf_op jit(solution)/shard_map/all_to_all | solution.py:44
  57.6 3.7 %copy-start.4 = (bf16[4,36864]{1,0:T(4,128)(2,1)S(1)}, bf16[4,36864]{1,0:T(4,128)(2,1)}, u32[]{:S(2)}) copy-start(bf16[4,36864]{1,0:T(4,128)(2,1)} %param.9) | copy-start | bytes 884740
  57.6 22.4 %all-to-all-start.1 = ((f32[84,16,1,192]{3,1,2,0:T(8,128)}), f32[84,16,1,192]{3,1,2,0:T(8,128)S(1)}, u32[]{:S(2)}, u32[]{:S(2)}) async-start(f32[84,16,1,192]{3,1,2,0:T(8,128)} %copy.29), calls=%async_computation.1 | async-start | bytes 2752512 | tf_op jit(solution)/shard_map/all_to_all | solution.py:52
  82.0 1.6 %copy-start = (bf16[768,768,1]{1,0,2:T(8,128)(2,1)S(1)}, bf16[768,768,1]{1,0,2:T(8,128)(2,1)}, u32[]{:S(2)}) copy-start(bf16[768,768,1]{1,0,2:T(8,128)(2,1)} %reshape.65) | copy-start | bytes 3538948
  82.0 1.9 %copy-start.2 = (f32[21,16,768]{2,1,0:T(8,128)S(1)}, f32[21,16,768]{2,1,0:T(8,128)}, u32[]{:S(2)}) copy-start(f32[21,16,768]{2,1,0:T(8,128)} %param.6) | copy-start | bytes 3096580
  83.9 1.5 %copy-start.1 = (f32[21,16,768]{2,1,0:T(8,128)}, f32[21,16,768]{2,1,0:T(8,128)S(1)}, u32[]{:S(2)}) copy-start(f32[21,16,768]{2,1,0:T(8,128)S(1)} %sub.11) | copy-start | bytes 3096580
